TPU v7x, 512 devices: a whole 4x4x16 slice. The times are simulated.
512 devices in a mesh: dp: 8 (over z_lo), seq: 4 (over z_hi, core), expert: 16 (over x, y).
Axes of the slice: x: 4, y: 4, z: 16 (z_hi: 2, z_lo: 8; z = z_hi * 8 + z_lo), core: 2. Of those that a mesh axis runs over, the one named last changes fastest.
Arguments:
- keys: bfloat16 [16, 4096, 512], P('expert', ('dp', 'seq')), may hold values from -4 to 4
- values: bfloat16 [16, 4096, 512], P('expert', ('dp', 'seq')), may hold values from -5 to 5
- queries: bfloat16 [16, 32, 4096], P('expert', ('dp', 'seq')), may hold values from -80 to 80
- residual: bfloat16 [16, 32, 2048], P('expert', ('dp', 'seq')), may hold values from -9 to 9
- out_proj: bfloat16 [4096, 2048], P(('dp', 'seq')), may hold values from -0.09375 to 0.09375
- norm_gain: bfloat16 [2048], replicated, may hold values from 0.25 to 1.75
- router: bfloat16 [2048, 128], replicated, may hold values from -8 to 8
- w_gate: bfloat16 [128, 2048, 768], P(('dp', 'expert'), None, 'seq'), may hold values from -0.125 to 0.125
- w_up: bfloat16 [128, 2048, 768], P(('dp', 'expert'), None, 'seq'), may hold values from -0.125 to 0.125
- w_down: bfloat16 [128, 768, 2048], P(('dp', 'expert'), 'seq'), may hold values from -0.21875 to 0.21875
- head_vec: bfloat16 [2048], replicated, may hold values from -0.09 to 0.09
- routes: int32 [16, 32, 8], P('expert', 'dp'), may hold values from 0 to 127, all different within a row; in each aligned block of 4 rows (0 to 3, 4 to 7, ..., all dimensions but the last counted through in order) at most 2 rows name the same one
- step_pos: int32 [16, 32], P('expert'), may hold values from 0 to 4095, as said below
- labels: int32 [16, 32], P('expert', ('dp', 'seq')), may hold values 0 or 1
- trace_len: int32 [16, 8], P('expert'), may hold values from 1 to 1024, 4096 in all within a row
Outputs:
- loss: float32 [], replicated
- grad_down: bfloat16 [128, 768, 2048], P(('dp', 'expert'), 'seq')
- grad_router: bfloat16 [2048, 128], P(('dp', 'seq', 'expert'))
Inputs may be any that keep to these rules, and one draw needn't show every extreme that they name: `step_pos`: increasing along each pack; distinct. `routes`: in each aligned block of 4 step ends (those of one index of dp in one pack) no expert is named by more than 2 of them.
All inputs are finite; a program needn't handle non-finite values. No bound on the sum of `labels` on one device may be relied on, other than what follows from the above.
Results may differ from a plain program's by a relative error of at most 0.018.
Values may be sent and summed in bfloat16 or wider, within the bound.
No kernel may reach another device: no remote copies, remote signals or barrier semaphores. Data moves between devices by JAX's collectives and lax.ppermute only.
A program may use at most 64 MiB of HBM per device.

v0:
```python
import jax
import jax.numpy as jnp
from jax import lax
from jax.sharding import Mesh
from jax.sharding import PartitionSpec as P

QUERY_HEADS = 32
KEY_VALUE_HEADS = 4
HEAD_WIDTH = 128
DP_EXPERT = ("dp", "expert_0", "expert_1")
DP_SEQ = ("dp", "seq_0", "seq_1")
SEQ = ("seq_0", "seq_1")
DP_SEQ_EXPERT = ("dp", "seq_0", "seq_1", "expert_0", "expert_1")
EXPERT = ("expert_0", "expert_1")


MASKED = -1e30
EPSILON = 1e-06


def joined_along(blocks, dim):
    blocks = jnp.moveaxis(blocks, 0, dim)
    lengths = blocks.shape
    return blocks.reshape(*lengths[:dim], lengths[dim] * lengths[dim + 1], *lengths[dim + 2 :])


def from_everyone(array, axis):
    copies = jnp.broadcast_to(array, (lax.axis_size(axis), *array.shape))
    return lax.all_to_all(copies, axis, split_axis=0, concat_axis=0, tiled=True)


def gather_directly(array, axis, dim):
    return joined_along(from_everyone(array, axis), dim)


def in_blocks(array, dim, count):
    lengths = array.shape
    blocks = array.reshape(*lengths[:dim], count, lengths[dim] // count, *lengths[dim + 1 :])
    return jnp.moveaxis(blocks, dim, 0)


def sent_and_summed(array, axis, dim):
    count = lax.axis_size(axis)
    blocks = lax.all_to_all(in_blocks(array, dim, count), axis, 0, 0, tiled=True)
    return jnp.sum(blocks.astype(jnp.float32), axis=0)


def by_axis(array, axes):
    for axis in axes:
        array = lax.psum(array, axis)
    return array


def taken_together(array, axis):
    return from_everyone(array, axis).sum(axis=0)


def reduced_to_own(blocks, axes, order):
    inside = blocks.shape[1:]
    blocks = blocks.reshape(*(lax.axis_size(a) for a in axes), *inside)
    blocks = jnp.moveaxis(blocks, order, range(len(axes))).reshape(-1, *inside)
    for k in order:
        blocks = lax.psum_scatter(blocks, axes[k], scatter_dimension=0, tiled=True)
    return blocks[0]


def scatter_axes(array, axes, order, dim):
    count = lax.axis_size(axes)
    return reduced_to_own(in_blocks(array, dim, count), axes, order)


def rms_scale(stream):
    return lax.rsqrt(jnp.mean(stream * stream, axis=-1, keepdims=True) + EPSILON)


def head_logit(final, head_vec):
    return jnp.sum(final * rms_scale(final) * head_vec.astype(jnp.float32)[None, :], axis=1)


def move_rows(buffer):
    return lax.all_to_all(buffer, DP_EXPERT, split_axis=0, concat_axis=0, tiled=True)


def move_back(buffer):
    return lax.all_to_all(
        buffer.astype(jnp.bfloat16), DP_EXPERT, split_axis=0, concat_axis=0, tiled=True
    ).astype(buffer.dtype)


def merge_heads(parts):
    weighted_r, totals_r, peak_r = parts
    peak_all = jnp.max(peak_r, axis=0)
    factor = jnp.exp(peak_r - peak_all[None])
    weighted_sum = jnp.sum(weighted_r * factor[..., None], axis=0)
    totals_sum = jnp.sum(totals_r * factor, axis=0)
    merged = weighted_sum / totals_sum[..., None]
    return merged.reshape(merged.shape[0], -1).astype(jnp.bfloat16)


def shards(
    keys,
    values,
    queries,
    residual,
    out_proj,
    norm_gain,
    router,
    w_gate,
    w_up,
    w_down,
    head_vec,
    routes,
    step_pos,
    labels,
    trace_len,
):
    count_of_keys = keys.shape[1]
    query_groups = QUERY_HEADS // KEY_VALUE_HEADS
    query_all = gather_directly(queries, DP_SEQ, 1)[0]
    positions = step_pos[0]
    number_of_steps = positions.shape[0]
    lengths = trace_len[0]
    trace_ends = jnp.cumsum(lengths)
    starts = jnp.sum(
        jnp.where(trace_ends[None, :] <= positions[:, None], lengths[None, :], 0), axis=1
    )
    key_pos = lax.axis_index(DP_SEQ) * count_of_keys + jnp.arange(count_of_keys, dtype=jnp.int32)
    allowed = (key_pos[None, :] <= positions[:, None]) & (key_pos[None, :] >= starts[:, None])
    score_list = []
    for head_cluster in range(KEY_VALUE_HEADS):
        query_part = query_all[
            :,
            head_cluster
            * query_groups
            * HEAD_WIDTH : (head_cluster + 1)
            * query_groups
            * HEAD_WIDTH,
        ].reshape(number_of_steps * query_groups, HEAD_WIDTH)
        key_part = keys[0, :, head_cluster * HEAD_WIDTH : (head_cluster + 1) * HEAD_WIDTH]
        score_part = lax.dot_general(
            query_part, key_part, (((1,), (1,)), ((), ())), preferred_element_type=jnp.float32
        ) * HEAD_WIDTH ** (-0.5)
        score_part = score_part.reshape(number_of_steps, query_groups, count_of_keys)
        score_list.append(jnp.where(allowed[:, None, :], score_part, MASKED))
    scores = jnp.stack(score_list, axis=1).reshape(number_of_steps, QUERY_HEADS, count_of_keys)
    local_peak = jnp.max(scores, axis=2)
    heads_of_values = values[0].reshape(count_of_keys, KEY_VALUE_HEADS, HEAD_WIDTH)
    complete_weight_rows = jnp.where(
        allowed[:, None, :], jnp.exp(scores - local_peak[:, :, None]), 0.0
    )
    totals = jnp.sum(complete_weight_rows, axis=2)
    reduced_weight_rows = complete_weight_rows.astype(jnp.bfloat16).reshape(
        number_of_steps, KEY_VALUE_HEADS, query_groups, count_of_keys
    )
    weighted = jnp.einsum(
        "skgt,tkd->skgd", reduced_weight_rows, heads_of_values, preferred_element_type=jnp.float32
    )
    weighted, totals = (weighted.reshape(number_of_steps, QUERY_HEADS * HEAD_WIDTH), totals)
    attn = merge_heads(
        (
            lax.all_to_all(
                weighted.reshape(1, number_of_steps, QUERY_HEADS, HEAD_WIDTH).astype(jnp.bfloat16),
                DP_SEQ,
                split_axis=2,
                concat_axis=0,
                tiled=True,
            ).astype(jnp.float32),
            lax.all_to_all(
                totals.reshape(1, number_of_steps, QUERY_HEADS).astype(jnp.bfloat16),
                DP_SEQ,
                split_axis=2,
                concat_axis=0,
                tiled=True,
            ).astype(jnp.float32),
            lax.all_to_all(
                local_peak.reshape(1, number_of_steps, QUERY_HEADS).astype(jnp.bfloat16),
                DP_SEQ,
                split_axis=2,
                concat_axis=0,
                tiled=True,
            ).astype(jnp.float32),
        )
    )
    mixed = sent_and_summed(
        jnp.dot(attn, out_proj, preferred_element_type=jnp.float32).astype(jnp.bfloat16), DP_SEQ, 0
    )
    stream = residual[0].astype(jnp.float32) + mixed
    normed = (stream * rms_scale(stream) * norm_gain.astype(jnp.float32)[None, :]).astype(
        jnp.bfloat16
    )
    block_normed = gather_directly(normed, SEQ, 0)
    block_rows = routes.shape[1]
    topk = routes.shape[2]
    experts = router.shape[1]
    capacity = min(block_rows, 2 * ((block_rows * topk + experts - 1) // experts))
    route_ids = routes[0]
    logits = jnp.dot(block_normed, router, preferred_element_type=jnp.float32)
    chosen = (route_ids[:, :, None] == jnp.arange(experts, dtype=jnp.int32)[None, None, :]).astype(
        jnp.float32
    )
    picked = jnp.sum(chosen * logits[:, None, :], axis=2)
    gate_weight = jax.nn.softmax(picked, axis=-1)
    flat_routes = route_ids.reshape(-1)
    onehot = (flat_routes[:, None] == jnp.arange(experts, dtype=jnp.int32)[None, :]).astype(
        jnp.int32
    )
    order_rank = jnp.sum((jnp.cumsum(onehot, axis=0) - 1) * onehot, axis=1)
    slot_index = flat_routes * capacity + order_rank
    place_map = (
        slot_index[:, None] == jnp.arange(experts * capacity, dtype=jnp.int32)[None, :]
    ).astype(jnp.float32)
    place_map = place_map.reshape(block_rows, topk, experts * capacity)
    row_map = jnp.sum(place_map, axis=1)
    weight_map = jnp.sum(gate_weight[:, :, None] * place_map, axis=1)
    contract_rows = (((0,), (0,)), ((), ()))
    send_rows = lax.dot_general(
        row_map.astype(jnp.bfloat16),
        block_normed,
        contract_rows,
        preferred_element_type=jnp.float32,
    ).astype(jnp.bfloat16)
    arrived = move_rows(send_rows.reshape(experts, capacity, -1))
    width = arrived.shape[2]
    arrived = arrived.reshape(experts * capacity, width)
    gate_act = jnp.dot(arrived, w_gate[0], preferred_element_type=jnp.float32)
    up_act = jnp.dot(arrived, w_up[0], preferred_element_type=jnp.float32)
    hidden = (jax.nn.silu(gate_act) * up_act).astype(jnp.bfloat16)
    partial_value = jnp.dot(hidden, w_down[0], preferred_element_type=jnp.float32)
    returned = move_back(partial_value.reshape(experts, capacity, width)).reshape(
        experts * capacity, width
    )
    block_mix = lax.dot_general(
        weight_map, returned, (((1,), (0,)), ((), ())), precision=lax.Precision.HIGHEST
    )
    expert_mix = sent_and_summed(block_mix.astype(jnp.bfloat16), SEQ, 0)
    final = stream + expert_mix
    reward, pull = jax.vjp(lambda value: head_logit(value, head_vec), final)
    target = labels[0].astype(jnp.float32)
    local_loss = jnp.sum(jax.nn.softplus(reward) - target * reward)
    loss = by_axis(local_loss, DP_SEQ_EXPERT)
    logit_grad = jax.nn.sigmoid(reward) - target
    (final_grad,) = pull(logit_grad)
    d_mix = final_grad.astype(jnp.bfloat16)
    block_grads = gather_directly(d_mix, SEQ, 0)
    slot_grads = lax.dot_general(
        row_map.astype(jnp.bfloat16), block_grads, contract_rows, preferred_element_type=jnp.float32
    )
    slot_dots = jnp.sum(slot_grads * returned, axis=1)
    dots_part = jnp.sum(place_map * slot_dots[None, None, :], axis=2)
    d_out = lax.dot_general(
        weight_map, block_grads.astype(jnp.float32), contract_rows, precision=lax.Precision.HIGHEST
    ).astype(jnp.bfloat16)
    grads_arrived = move_rows(d_out.reshape(experts, capacity, width)).reshape(
        experts * capacity, width
    )
    grad_down = lax.dot_general(
        hidden, grads_arrived, contract_rows, preferred_element_type=jnp.float32
    )
    grad_down = grad_down.astype(jnp.bfloat16).reshape((1,) + grad_down.shape)
    route_dot = taken_together(dots_part, SEQ)
    pick_grad = gate_weight * (route_dot - jnp.sum(gate_weight * route_dot, axis=1, keepdims=True))
    d_logits = jnp.sum(chosen * pick_grad[:, :, None], axis=1)
    columns = block_normed.reshape(
        block_rows, lax.axis_size("dp"), lax.axis_size(SEQ), lax.axis_size(EXPERT), -1
    )
    my_columns = lax.dynamic_index_in_dim(columns, lax.axis_index(SEQ), 2, keepdims=False).reshape(
        block_rows, -1
    )
    router_part = lax.dot_general(
        my_columns.astype(jnp.float32), d_logits, contract_rows, precision=lax.Precision.HIGHEST
    )
    grad_router = scatter_axes(router_part, DP_EXPERT, (1, 2, 0), 0).astype(jnp.bfloat16)
    return (loss, grad_down, grad_router)


def solution(mesh):
    finer = Mesh(
        mesh.devices.reshape(mesh.shape["dp"], 2, 2, 4, 4),
        ("dp", "seq_0", "seq_1", "expert_0", "expert_1"),
    )
    return jax.shard_map(
        shards,
        mesh=finer,
        in_specs=(
            P(EXPERT, DP_SEQ, None),
            P(EXPERT, DP_SEQ, None),
            P(EXPERT, DP_SEQ, None),
            P(EXPERT, DP_SEQ, None),
            P(DP_SEQ, None),
            P(),
            P(),
            P(DP_EXPERT, None, SEQ),
            P(DP_EXPERT, None, SEQ),
            P(DP_EXPERT, SEQ, None),
            P(),
            P(EXPERT, "dp", None),
            P(EXPERT, None),
            P(EXPERT, DP_SEQ),
            P(EXPERT, None),
        ),
        out_specs=(P(), P(DP_EXPERT, SEQ, None), P(DP_SEQ_EXPERT, None)),
        check_vma=False,
    )
```

profile of v0, /device:TPU:1, one launch (start us, length us, event | category | flops | bytes accessed | tf_op | source)
XLA Modules:
  0.0 514.7 jit_solution(14545275616170389167)
XLA Ops:
  9.0 2.3 reduce.21
  12.2 16.7 %all-to-all-start = ((bf16[32,2,2048]{2,1,0:T(2,128)(2,1)}), bf16[32,2,2048]{2,1,0:T(2,128)(2,1)S(1)}, u32[]{:S(2)}, u32[]{:S(2)}) async-start(bf16[32,2,2048]{2,1,0:T(2,128)(2,1)} %reshape.602), calls=%async_computation | async-start | bytes 524288 | tf_op jit(solution)/shard_map/all_to_all | solution.py:29
  29.4 18.7 %all-to-all-done = bf16[32,2,2048]{2,1,0:T(2,128)(2,1)S(1)} async-done(((bf16[32,2,2048]{2,1,0:T(2,128)(2,1)}), bf16[32,2,2048]{2,1,0:T(2,128)(2,1)S(1)}, u32[]{:S(2)}, u32[]{:S(2)}) %all-to-all-start) | async-done | bytes 262176 | tf_op jit(solution)/shard_map/all_to_all | solution.py:29
  50.4 5.9 %all-to-all-start.2 = ((bf16[1,32,32]{1,0,2:T(2,128)(2,1)}), bf16[1,32,32]{1,0,2:T(2,128)(2,1)S(1)}, u32[]{:S(2)}, u32[]{:S(2)}) async-start(bf16[1,32,32]{1,0,2:T(2,128)(2,1)} %copy.74), calls=%async_computation.2 | async-start | bytes 32768 | tf_op jit(solution)/shard_map/all_to_all | solution.py:175
  57.5 10.6 %all-to-all-done.2 = bf16[1,32,32]{1,0,2:T(2,128)(2,1)S(1)} async-done(((bf16[1,32,32]{1,0,2:T(2,128)(2,1)}), bf16[1,32,32]{1,0,2:T(2,128)(2,1)S(1)}, u32[]{:S(2)}, u32[]{:S(2)}) %all-to-all-start.2) | async-done | bytes 2080 | tf_op jit(solution)/shard_map/all_to_all | solution.py:175
  68.1 4.1 all-to-all-start.3
  73.4 10.5 %all-to-all-done.3 = bf16[1,32,32]{1,0,2:T(2,128)(2,1)S(1)} async-done(((bf16[1,32,32]{1,0,2:T(2,128)(2,1)}), bf16[1,32,32]{1,0,2:T(2,128)(2,1)S(1)}, u32[]{:S(2)}, u32[]{:S(2)}) %all-to-all-start.3) | async-done | bytes 2080 | tf_op jit(solution)/shard_map/all_to_all | solution.py:168
  83.9 4.2 all-to-all-start.1
  88.2 19.1 %all-to-all-done.1 = bf16[1,32,32,128]{3,1,0,2:T(8,128)(2,1)S(1)} async-done(((bf16[1,32,32,128]{3,1,0,2:T(8,128)(2,1)}), bf16[1,32,32,128]{3,1,0,2:T(8,128)(2,1)S(1)}, u32[]{:S(2)}, u32[]{:S(2)}) %all-to-all-start.1) | async-done | bytes 262176 | tf_op jit(solution)/shard_map/all_to_all | solution.py:161
  109.3 5.8 %all-to-all-start.4 = ((bf16[32,2,1024]{2,1,0:T(2,128)(2,1)}), bf16[32,2,1024]{2,1,0:T(2,128)(2,1)S(1)}, u32[]{:S(2)}, u32[]{:S(2)}) async-start(bf16[32,2,1024]{2,1,0:T(2,128)(2,1)} %reshape.604), calls=%async_computation.4 | async-start | bytes 262144 | tf_op jit(solution)/shard_map/all_to_all | solution.py:44
  115.6 14.8 %all-to-all-done.4 = bf16[32,2,1024]{2,1,0:T(2,128)(2,1)S(1)} async-done(((bf16[32,2,1024]{2,1,0:T(2,128)(2,1)}), bf16[32,2,1024]{2,1,0:T(2,128)(2,1)S(1)}, u32[]{:S(2)}, u32[]{:S(2)}) %all-to-all-start.4) | async-done | bytes 131104 | tf_op jit(solution)/shard_map/all_to_all | solution.py:44
  133.5 3.6 all-to-all-start.5
  137.0 11.8 %all-to-all-done.5 = bf16[4,2,1024]{2,1,0:T(2,128)(2,1)S(1)} async-done(((bf16[4,2,1024]{2,1,0:T(2,128)(2,1)}), bf16[4,2,1024]{2,1,0:T(2,128)(2,1)S(1)}, u32[]{:S(2)}, u32[]{:S(2)}) %all-to-all-start.5) | async-done | bytes 16416 | tf_op jit(solution)/shard_map/all_to_all | solution.py:29
  150.9 68.3 %all_to_all.72 = bf16[128,2,2048]{2,1,0:T(2,128)(2,1)S(1)} all-to-all(bf16[128,2,2048]{2,1,0:T(2,128)(2,1)S(1)} %reshape.572), channel_id=1, replica_groups=mesh['dp'=8,'seq_0'=2,'seq_1'=2,'expert_0'=4,'expert_1'=4] {'dp','expert..., dimensions={0} | all-to-all | bytes 2097152 | tf_op jit(solution)/shard_map/all_to_all | solution.py:81
  219.7 1.7 fusion.16
  223.6 60.7 %all_to_all.73 = bf16[128,2,2048]{2,1,0:T(2,128)(2,1)S(1)} all-to-all(bf16[128,2,2048]{2,1,0:T(2,128)(2,1)S(1)} %copy.81), channel_id=1, replica_groups=mesh['dp'=8,'seq_0'=2,'seq_1'=2,'expert_0'=4,'expert_1'=4] {'dp','expert..., dimensions={0} | all-to-all | bytes 2097152 | tf_op jit(solution)/shard_map/all_to_all | solution.py:85
  286.6 5.4 %all-to-all-start.8 = ((bf16[4,2,1024]{2,1,0:T(2,128)(2,1)}), bf16[4,2,1024]{2,1,0:T(2,128)(2,1)S(1)}, u32[]{:S(2)}, u32[]{:S(2)}) async-start(bf16[4,2,1024]{2,1,0:T(2,128)(2,1)} %reshape.608), calls=%async_computation.8 | async-start | bytes 32768 | tf_op jit(solution)/shard_map/all_to_all | solution.py:44
  292.7 11.2 %all-to-all-done.8 = bf16[4,2,1024]{2,1,0:T(2,128)(2,1)S(1)} async-done(((bf16[4,2,1024]{2,1,0:T(2,128)(2,1)}), bf16[4,2,1024]{2,1,0:T(2,128)(2,1)S(1)}, u32[]{:S(2)}, u32[]{:S(2)}) %all-to-all-start.8) | async-done | bytes 16416 | tf_op jit(solution)/shard_map/all_to_all | solution.py:44
  308.6 14.9 %all_to_all.74 = bf16[4,2,1024]{2,1,0:T(2,128)(2,1)S(1)} all-to-all(bf16[4,2,1024]{2,1,0:T(2,128)(2,1)S(1)} %reshape.610), channel_id=1, replica_groups=mesh['dp'=8,'seq_0'=2,'seq_1'=2,'expert_0'=4,'expert_1'=4] {'seq_0','seq..., dimensions={0} | all-to-all | bytes 32768 | tf_op jit(solution)/shard_map/all_to_all | solution.py:29
  324.9 3.9 all-to-all-start.11
  329.9 1.5 reshape.578
  331.4 9.3 %all-to-all-done.11 = f32[4,4,8]{2,1,0:T(4,128)S(1)} async-done(((f32[4,4,8]{2,1,0:T(4,128)}), f32[4,4,8]{2,1,0:T(4,128)S(1)}, u32[]{:S(2)}, u32[]{:S(2)}) %all-to-all-start.11) | async-done | bytes 544 | tf_op jit(solution)/shard_map/all_to_all | solution.py:29
  340.7 6.9 %all-to-all-start.10 = ((bf16[128,2,2048]{2,1,0:T(2,128)(2,1)}), bf16[128,2,2048]{2,1,0:T(2,128)(2,1)S(1)}, u32[]{:S(2)}, u32[]{:S(2)}) async-start(bf16[128,2,2048]{2,1,0:T(2,128)(2,1)} %reshape.578), calls=%async_computation.10 | async-start | bytes 2097152 | tf_op jit(solution)/shard_map/all_to_all | solution.py:81
  351.4 26.3 %reduce-scatter.3.cloned.1.call-done = f32[32,4,128]{2,0,1:T(8,128)} async-done(((f32[128,4,128]{2,0,1:T(8,128)}), f32[32,4,128]{2,0,1:T(8,128)}) %reduce-scatter.3.cloned.1.call-update) | async-done | bytes 65552 | tf_op jit(solution)/shard_map/reduce_scatter | solution.py:63
  381.7 26.4 %reduce-scatter.5.cloned.1.call-done = f32[8,4,128]{2,0,1:T(8,128)} async-done(((f32[32,4,128]{2,0,1:T(8,128)}), f32[8,4,128]{2,0,1:T(8,128)}) %reduce-scatter.5.cloned.1.call-update) | async-done | bytes 16400 | tf_op jit(solution)/shard_map/reduce_scatter | solution.py:63
  408.9 51.5 %all-reduce.1 = (f32[]{:T(128)}, bf16[8,4,128]{2,1,0:T(4,128)(2,1)S(1)}) all-reduce(f32[]{:T(128)} %bitcast.40, f32[8,4,128]{2,1,0:T(4,128)S(1)} %copy.85), channel_id=1, replica_groups=mesh['dp'=8,'seq_0'=2,'seq_1'=2,'expert_0'=4,'expert_1'=4] {'dp'}, use_global_device_ids=true, to_apply=%region_19.20 | all-reduce | flops 4097 | bytes 24584 | tf_op jit(solution)/shard_map/psum | solution.py:50
  460.4 13.1 %psum.36 = f32[]{:T(128)} all-reduce(f32[]{:T(128)} %get-tuple-element.5), channel_id=1, replica_groups=mesh['dp'=8,'seq_0'=2,'seq_1'=2,'expert_0'=4,'expert_1'=4] {'seq_0'}, use_global_device_ids=true, to_apply=%region_20.21 | all-reduce | flops 1 | bytes 8 | tf_op jit(solution)/shard_map/psum | solution.py:50
  473.5 14.1 %psum.37 = f32[]{:T(128)} all-reduce(f32[]{:T(128)} %psum.36), channel_id=1, replica_groups=mesh['dp'=8,'seq_0'=2,'seq_1'=2,'expert_0'=4,'expert_1'=4] {'seq_1'}, use_global_device_ids=true, to_apply=%region_21.22 | all-reduce | flops 1 | bytes 8 | tf_op jit(solution)/shard_map/psum | solution.py:50
  487.6 9.0 %psum.38 = f32[]{:T(128)} all-reduce(f32[]{:T(128)} %psum.37), channel_id=1, replica_groups=mesh['dp'=8,'seq_0'=2,'seq_1'=2,'expert_0'=4,'expert_1'=4] {'expert_0'}, use_global_device_ids=true, to_apply=%region_22.23 | all-reduce | flops 1 | bytes 8 | tf_op jit(solution)/shard_map/psum | solution.py:50
  496.6 1.3 dynamic-slice
  497.9 7.1 %psum.39 = f32[]{:T(128)} all-reduce(f32[]{:T(128)} %psum.38), channel_id=1, replica_groups=mesh['dp'=8,'seq_0'=2,'seq_1'=2,'expert_0'=4,'expert_1'=4] {'expert_1'}, use_global_device_ids=true, to_apply=%region_23.24 | all-reduce | flops 1 | bytes 8 | tf_op jit(solution)/shard_map/psum | solution.py:50
  506.6 1.3 fusion
  (128 shorter events, 30.7 us)
Async XLA Ops:
  7.2 214.9 %copy-start = (bf16[1,192,2048]{2,1,0:T(8,128)(2,1)S(1)}, bf16[1,192,2048]{2,1,0:T(8,128)(2,1)}, u32[]{:S(2)}) copy-start(bf16[1,192,2048]{2,1,0:T(8,128)(2,1)} %param.24) | copy-start | bytes 2359300
  8.5 20.4 %copy-start.4 = (bf16[1,128,512]{2,1,0:T(8,128)(2,1)S(1)}, bf16[1,128,512]{2,1,0:T(8,128)(2,1)}, u32[]{:S(2)}) copy-start(bf16[1,128,512]{2,1,0:T(8,128)(2,1)} %param.16) | copy-start | bytes 393220
  9.0 20.0 %copy-start.10 = (s32[1,8]{1,0:T(1,128)S(1)}, s32[1,8]{1,0:T(1,128)}, u32[]{:S(2)}) copy-start(s32[1,8]{1,0:T(1,128)} %param.29) | copy-start | bytes 100
  9.0 20.2 %copy-start.9 = (s32[1,32]{1,0:T(1,128)S(1)}, s32[1,32]{1,0:T(1,128)}, u32[]{:S(2)}) copy-start(s32[1,32]{1,0:T(1,128)} %param.27) | copy-start | bytes 388
  12.2 35.9 %all-to-all-start = ((bf16[32,2,2048]{2,1,0:T(2,128)(2,1)}), bf16[32,2,2048]{2,1,0:T(2,128)(2,1)S(1)}, u32[]{:S(2)}, u32[]{:S(2)}) async-start(bf16[32,2,2048]{2,1,0:T(2,128)(2,1)} %reshape.602), calls=%async_computation | async-start | bytes 524288 | tf_op jit(solution)/shard_map/all_to_all | solution.py:29
  29.4 19.4 %copy-start.3 = (bf16[1,128,512]{2,1,0:T(8,128)(2,1)S(1)}, bf16[1,128,512]{2,1,0:T(8,128)(2,1)}, u32[]{:S(2)}) copy-start(bf16[1,128,512]{2,1,0:T(8,128)(2,1)} %param.15) | copy-start | bytes 393220
  50.4 17.6 %all-to-all-start.2 = ((bf16[1,32,32]{1,0,2:T(2,128)(2,1)}), bf16[1,32,32]{1,0,2:T(2,128)(2,1)S(1)}, u32[]{:S(2)}, u32[]{:S(2)}) async-start(bf16[1,32,32]{1,0,2:T(2,128)(2,1)} %copy.74), calls=%async_computation.2 | async-start | bytes 32768 | tf_op jit(solution)/shard_map/all_to_all | solution.py:175
  68.1 15.8 %all-to-all-start.3 = ((bf16[1,32,32]{1,0,2:T(2,128)(2,1)}), bf16[1,32,32]{1,0,2:T(2,128)(2,1)S(1)}, u32[]{:S(2)}, u32[]{:S(2)}) async-start(bf16[1,32,32]{1,0,2:T(2,128)(2,1)} %copy.76), calls=%async_computation.3 | async-start | bytes 32768 | tf_op jit(solution)/shard_map/all_to_all | solution.py:168
  72.5 35.0 %copy-start.1 = (bf16[128,2048]{1,0:T(8,128)(2,1)S(1)}, bf16[128,2048]{1,0:T(8,128)(2,1)}, u32[]{:S(2)}) copy-start(bf16[128,2048]{1,0:T(8,128)(2,1)} %param.19) | copy-start | bytes 1572868
  83.9 23.4 %all-to-all-start.1 = ((bf16[1,32,32,128]{3,1,0,2:T(8,128)(2,1)}), bf16[1,32,32,128]{3,1,0,2:T(8,128)(2,1)S(1)}, u32[]{:S(2)}, u32[]{:S(2)}) async-start(bf16[1,32,32,128]{3,1,0,2:T(8,128)(2,1)} %copy.72), calls=%async_computation.1 | async-start | bytes 524288 | tf_op jit(solution)/shard_map/all_to_all | solution.py:161
  88.1 27.0 %copy-start.7 = (bf16[1,1,2048]{2,1,0:T(2,128)(2,1)S(1)}, bf16[1,1,2048]{2,1,0:T(2,128)(2,1)}, u32[]{:S(2)}) copy-start(bf16[1,1,2048]{2,1,0:T(2,128)(2,1)} %param.18) | copy-start | bytes 12292
  88.1 27.0 %copy-start.6 = (s32[1,4,8]{2,1,0:T(4,128)S(1)}, s32[1,4,8]{2,1,0:T(4,128)}, u32[]{:S(2)}) copy-start(s32[1,4,8]{2,1,0:T(4,128)} %param.26) | copy-start | bytes 388
  107.6 24.5 %copy-start.8 = (bf16[2048]{0:T(1024)(128)(2,1)S(1)}, bf16[2048]{0:T(1024)(128)(2,1)}, u32[]{:S(2)}) copy-start(bf16[2048]{0:T(1024)(128)(2,1)} %param.20) | copy-start | bytes 12292
  107.8 41.1 %copy-start.2 = (bf16[2048,128]{1,0:T(8,128)(2,1)S(1)}, bf16[2048,128]{1,0:T(8,128)(2,1)}, u32[]{:S(2)}) copy-start(bf16[2048,128]{1,0:T(8,128)(2,1)} %param.21) | copy-start | bytes 1572868
  109.3 21.1 %all-to-all-start.4 = ((bf16[32,2,1024]{2,1,0:T(2,128)(2,1)}), bf16[32,2,1024]{2,1,0:T(2,128)(2,1)S(1)}, u32[]{:S(2)}, u32[]{:S(2)}) async-start(bf16[32,2,1024]{2,1,0:T(2,128)(2,1)} %reshape.604), calls=%async_computation.4 | async-start | bytes 262144 | tf_op jit(solution)/shard_map/all_to_all | solution.py:44
  133.5 15.4 %all-to-all-start.5 = ((bf16[4,2,1024]{2,1,0:T(2,128)(2,1)}), bf16[4,2,1024]{2,1,0:T(2,128)(2,1)S(1)}, u32[]{:S(2)}, u32[]{:S(2)}) async-start(bf16[4,2,1024]{2,1,0:T(2,128)(2,1)} %reshape.606), calls=%async_computation.5 | async-start | bytes 32768 | tf_op jit(solution)/shard_map/all_to_all | solution.py:29
  219.7 1.7 copy-start.11
  284.8 20.5 %copy-start.5 = (bf16[2048]{0:T(1024)(128)(2,1)S(1)}, bf16[2048]{0:T(1024)(128)(2,1)}, u32[]{:S(2)}) copy-start(bf16[2048]{0:T(1024)(128)(2,1)} %param.25) | copy-start | bytes 12292
  286.6 17.3 %all-to-all-start.8 = ((bf16[4,2,1024]{2,1,0:T(2,128)(2,1)}), bf16[4,2,1024]{2,1,0:T(2,128)(2,1)S(1)}, u32[]{:S(2)}, u32[]{:S(2)}) async-start(bf16[4,2,1024]{2,1,0:T(2,128)(2,1)} %reshape.608), calls=%async_computation.8 | async-start | bytes 32768 | tf_op jit(solution)/shard_map/all_to_all | solution.py:44
  324.9 15.8 %all-to-all-start.11 = ((f32[4,4,8]{2,1,0:T(4,128)}), f32[4,4,8]{2,1,0:T(4,128)S(1)}, u32[]{:S(2)}, u32[]{:S(2)}) async-start(f32[4,4,8]{2,1,0:T(4,128)} %broadcast_in_dim.112), calls=%async_computation.11 | async-start | bytes 16384 | tf_op jit(solution)/shard_map/all_to_all | solution.py:29
  340.7 165.5 %all-to-all-start.10 = ((bf16[128,2,2048]{2,1,0:T(2,128)(2,1)}), bf16[128,2,2048]{2,1,0:T(2,128)(2,1)S(1)}, u32[]{:S(2)}, u32[]{:S(2)}) async-start(bf16[128,2,2048]{2,1,0:T(2,128)(2,1)} %reshape.578), calls=%async_computation.10 | async-start | bytes 2097152 | tf_op jit(solution)/shard_map/all_to_all | solution.py:81
  347.6 30.1 %reduce-scatter.3.cloned.1.call-start = ((), (), s32[]{:S(2)}) async-start(), calls=%async_computation.14 | async-start | bytes 327680 | tf_op jit(solution)/shard_map/reduce_scatter | solution.py:63
  351.3 56.8 %reduce-scatter.5.cloned.1.call-start = ((), (), s32[]{:S(2)}) async-start(), calls=%async_computation.15 | async-start | bytes 81920 | tf_op jit(solution)/shard_map/reduce_scatter | solution.py:63
Sparse Core Ops, SparseCore 0:
  351.8 25.8 reduce-scatter.2
  380.7 27.3 reduce-scatter.4
where the time goes:
time: 519 us; the launch traced here: 515 us
  blocking collectives  239 us (46%)
  waiting for transfers between devices  159 us (31%)
  starting transfers between devices  56.6 us (11%)
  between operations  22 us (4%)
  local copies, waits for them, and re-layouts  18.7 us (4%)
  other arithmetic  11.6 us (2%)
  matrix products  8.29 us (2%)
    psum x5, blocking collectives, by_axis(): array = lax.psum(array, axis)  94.8 us
    all_to_all x1, blocking collectives, move_rows(): lax.all_to_all(buffer, DP_EXPERT, split_axis=0, concat_axis=0, tiled=True)  68.3 us
    all_to_all x1, blocking collectives, move_back(): lax.all_to_all(buffer.astype(jnp.bfloat16), DP_EXPERT, split_axis=0, conc...  60.7 us
    reduce_scatter x2, waiting for transfers between devices, reduced_to_own(): blocks = lax.psum_scatter(blocks, axes[k], scatter_dimension=0, tiled=True)  52.8 us
    all_to_all x3, waiting for transfers between devices, from_everyone(): return lax.all_to_all(copies, axis, split_axis=0, concat_axis=0, tiled=True)  39.8 us
    all_to_all x2, waiting for transfers between devices, sent_and_summed(): lax.all_to_all(in_blocks(array, dim, count), axis, 0, 0, tiled=True)  25.9 us
    all_to_all x3, starting transfers between devices, from_everyone(): return lax.all_to_all(copies, axis, split_axis=0, concat_axis=0, tiled=True)  24.3 us
    all_to_all x1, waiting for transfers between devices, shards(): lax.all_to_all(weighted.reshape(1, number_of_steps, QUERY_HEADS, HEAD_WID...  19.1 us
  transfers between devices with their start and end apart: 11, of which 10 were waited for; matrix products, arithmetic and copies ran while one was open for 2% of the time, Pallas kernels for 0%

commit v1 on v0

v1 whole, which is shorter than its diff:
```python
import jax
import jax.numpy as jnp
from jax import lax
from jax.sharding import Mesh
from jax.sharding import PartitionSpec as P

QUERY_HEADS = 32
KEY_VALUE_HEADS = 4
HEAD_WIDTH = 128
DP_EXPERT = ("dp", "expert_0", "expert_1")
DP_SEQ = ("dp", "seq_0", "seq_1")
SEQ = ("seq_0", "seq_1")
DP_SEQ_EXPERT = ("dp", "seq_0", "seq_1", "expert_0", "expert_1")
EXPERT = ("expert_0", "expert_1")
ROWS = DP_SEQ_EXPERT


MASKED = -1e30
EPSILON = 1e-06


def joined_along(blocks, dim):
    blocks = jnp.moveaxis(blocks, 0, dim)
    lengths = blocks.shape
    return blocks.reshape(*lengths[:dim], lengths[dim] * lengths[dim + 1], *lengths[dim + 2 :])


def from_everyone(array, axis):
    copies = jnp.broadcast_to(array, (lax.axis_size(axis), *array.shape))
    return lax.all_to_all(copies, axis, split_axis=0, concat_axis=0, tiled=True)


def gather_directly(array, axis, dim):
    return joined_along(from_everyone(array, axis), dim)


def in_blocks(array, dim, count):
    lengths = array.shape
    blocks = array.reshape(*lengths[:dim], count, lengths[dim] // count, *lengths[dim + 1 :])
    return jnp.moveaxis(blocks, dim, 0)


def sent_and_summed(array, axis, dim):
    count = lax.axis_size(axis)
    blocks = lax.all_to_all(in_blocks(array, dim, count), axis, 0, 0, tiled=True)
    return jnp.sum(blocks.astype(jnp.float32), axis=0)


def rms_scale(stream):
    return lax.rsqrt(jnp.mean(stream * stream, axis=-1, keepdims=True) + EPSILON)


def head_logit(final, head_vec):
    return jnp.sum(final * rms_scale(final) * head_vec.astype(jnp.float32)[None, :], axis=1)


def split_pair(value):
    high = value.astype(jnp.bfloat16)
    low = (value - high.astype(jnp.float32)).astype(jnp.bfloat16)
    return high, low


def join_pair(high, low):
    return high.astype(jnp.float32) + low.astype(jnp.float32)


def merge_heads(weighted_r, totals_r, peak_r):
    peak_all = jnp.max(peak_r, axis=0)
    factor = jnp.exp(peak_r - peak_all[None])
    weighted_sum = jnp.sum(weighted_r * factor[..., None], axis=0)
    totals_sum = jnp.sum(totals_r * factor, axis=0)
    merged = weighted_sum / totals_sum[..., None]
    return merged.reshape(merged.shape[0], -1).astype(jnp.bfloat16)


def shards(
    keys,
    values,
    queries,
    residual,
    out_proj,
    norm_gain,
    router,
    w_gate,
    w_up,
    w_down,
    head_vec,
    routes,
    step_pos,
    labels,
    trace_len,
):
    block_routes = lax.all_gather(routes[0], DP_EXPERT, axis=0)
    block_routes = block_routes.reshape(
        lax.axis_size("dp"), lax.axis_size(EXPERT), *routes.shape[1:]
    )
    routes_all = jnp.swapaxes(block_routes, 1, 2).reshape(-1, routes.shape[2])
    count_of_keys = keys.shape[1]
    query_groups = QUERY_HEADS // KEY_VALUE_HEADS
    query_all = gather_directly(queries, DP_SEQ, 1)[0]
    positions = step_pos[0]
    number_of_steps = positions.shape[0]
    lengths = trace_len[0]
    trace_ends = jnp.cumsum(lengths)
    starts = jnp.sum(
        jnp.where(trace_ends[None, :] <= positions[:, None], lengths[None, :], 0), axis=1
    )
    key_pos = lax.axis_index(DP_SEQ) * count_of_keys + jnp.arange(count_of_keys, dtype=jnp.int32)
    allowed = (key_pos[None, :] <= positions[:, None]) & (key_pos[None, :] >= starts[:, None])
    score_list = []
    for head_cluster in range(KEY_VALUE_HEADS):
        query_part = query_all[
            :,
            head_cluster
            * query_groups
            * HEAD_WIDTH : (head_cluster + 1)
            * query_groups
            * HEAD_WIDTH,
        ].reshape(number_of_steps * query_groups, HEAD_WIDTH)
        key_part = keys[0, :, head_cluster * HEAD_WIDTH : (head_cluster + 1) * HEAD_WIDTH]
        score_part = lax.dot_general(
            query_part, key_part, (((1,), (1,)), ((), ())), preferred_element_type=jnp.float32
        ) * HEAD_WIDTH ** (-0.5)
        score_part = score_part.reshape(number_of_steps, query_groups, count_of_keys)
        score_list.append(jnp.where(allowed[:, None, :], score_part, MASKED))
    scores = jnp.stack(score_list, axis=1).reshape(number_of_steps, QUERY_HEADS, count_of_keys)
    local_peak = jnp.max(scores, axis=2)
    heads_of_values = values[0].reshape(count_of_keys, KEY_VALUE_HEADS, HEAD_WIDTH)
    complete_weight_rows = jnp.where(
        allowed[:, None, :], jnp.exp(scores - local_peak[:, :, None]), 0.0
    )
    totals = jnp.sum(complete_weight_rows, axis=2)
    reduced_weight_rows = complete_weight_rows.astype(jnp.bfloat16).reshape(
        number_of_steps, KEY_VALUE_HEADS, query_groups, count_of_keys
    )
    weighted = jnp.einsum(
        "skgt,tkd->skgd", reduced_weight_rows, heads_of_values, preferred_element_type=jnp.float32
    ).reshape(number_of_steps, QUERY_HEADS, HEAD_WIDTH)
    totals_hi, totals_lo = split_pair(totals)
    peak_hi, peak_lo = split_pair(local_peak)
    packed = jnp.concatenate(
        [
            weighted.astype(jnp.bfloat16),
            totals_hi[..., None],
            totals_lo[..., None],
            peak_hi[..., None],
            peak_lo[..., None],
        ],
        axis=-1,
    )
    arrived = lax.all_to_all(
        packed.reshape(1, *packed.shape), DP_SEQ, split_axis=2, concat_axis=0, tiled=True
    )
    attn = merge_heads(
        arrived[..., :HEAD_WIDTH].astype(jnp.float32),
        join_pair(arrived[..., HEAD_WIDTH], arrived[..., HEAD_WIDTH + 1]),
        join_pair(arrived[..., HEAD_WIDTH + 2], arrived[..., HEAD_WIDTH + 3]),
    )
    mixed = sent_and_summed(
        jnp.dot(attn, out_proj, preferred_element_type=jnp.float32).astype(jnp.bfloat16), DP_SEQ, 0
    )
    stream = residual[0].astype(jnp.float32) + mixed
    normed = (stream * rms_scale(stream) * norm_gain.astype(jnp.float32)[None, :]).astype(
        jnp.bfloat16
    )
    normed_all = lax.all_gather(normed, ROWS, axis=0, tiled=True)
    experts = router.shape[1]
    logits = jnp.dot(normed_all, router, preferred_element_type=jnp.float32)
    chosen = (routes_all[:, :, None] == jnp.arange(experts, dtype=jnp.int32)[None, None, :]).astype(
        jnp.float32
    )
    picked = jnp.sum(chosen * logits[:, None, :], axis=2)
    gate_weight = jax.nn.softmax(picked, axis=-1)
    mine = routes_all == lax.axis_index(DP_EXPERT)
    coef = jnp.sum(jnp.where(mine, gate_weight, 0.0), axis=1)
    gate_act = jnp.dot(normed_all, w_gate[0], preferred_element_type=jnp.float32)
    up_act = jnp.dot(normed_all, w_up[0], preferred_element_type=jnp.float32)
    hidden = (jax.nn.silu(gate_act) * up_act).astype(jnp.bfloat16)
    expert_out = jnp.dot(hidden, w_down[0], preferred_element_type=jnp.float32)
    expert_mix = lax.psum_scatter(
        coef[:, None] * expert_out, ROWS, scatter_dimension=0, tiled=True
    )
    final = stream + expert_mix
    reward, pull = jax.vjp(lambda value: head_logit(value, head_vec), final)
    target = labels[0].astype(jnp.float32)
    loss_term = jax.nn.softplus(reward) - target * reward
    logit_grad = jax.nn.sigmoid(reward) - target
    (final_grad,) = pull(logit_grad)
    d_mix = final_grad.astype(jnp.bfloat16)
    d_mix_all = lax.all_gather(d_mix, ROWS, axis=0, tiled=True)
    d_mix_wide = d_mix_all.astype(jnp.float32)
    contract_rows = (((0,), (0,)), ((), ()))
    d_out = (coef[:, None] * d_mix_wide).astype(jnp.bfloat16)
    grad_down = lax.dot_general(hidden, d_out, contract_rows, preferred_element_type=jnp.float32)
    grad_down = grad_down.astype(jnp.bfloat16).reshape((1,) + grad_down.shape)
    share_dot = jnp.sum(d_mix_wide * expert_out, axis=1)
    row_count = normed_all.shape[0]
    own_row = jnp.arange(row_count, dtype=jnp.int32) == lax.axis_index(ROWS)
    payload = jnp.concatenate(
        [
            jnp.where(mine, share_dot[:, None], 0.0),
            jnp.where(own_row, loss_term, 0.0)[:, None],
        ],
        axis=1,
    )
    summed = lax.psum(payload, ROWS)
    route_dot = summed[:, :-1]
    loss = jnp.sum(summed[:, -1])
    pick_grad = gate_weight * (route_dot - jnp.sum(gate_weight * route_dot, axis=1, keepdims=True))
    d_logits = jnp.sum(chosen * pick_grad[:, :, None], axis=1)
    router_grad_all = lax.dot_general(
        normed_all.astype(jnp.float32), d_logits, contract_rows, precision=lax.Precision.HIGHEST
    )
    own_rows = router_grad_all.shape[0] // lax.axis_size(DP_SEQ_EXPERT)
    grad_router = lax.dynamic_slice_in_dim(
        router_grad_all, lax.axis_index(DP_SEQ_EXPERT) * own_rows, own_rows, axis=0
    ).astype(jnp.bfloat16)
    return (loss, grad_down, grad_router)


def solution(mesh):
    finer = Mesh(
        mesh.devices.reshape(mesh.shape["dp"], 2, 2, 4, 4),
        ("dp", "seq_0", "seq_1", "expert_0", "expert_1"),
    )
    return jax.shard_map(
        shards,
        mesh=finer,
        in_specs=(
            P(EXPERT, DP_SEQ, None),
            P(EXPERT, DP_SEQ, None),
            P(EXPERT, DP_SEQ, None),
            P(EXPERT, DP_SEQ, None),
            P(DP_SEQ, None),
            P(),
            P(),
            P(DP_EXPERT, None, SEQ),
            P(DP_EXPERT, None, SEQ),
            P(DP_EXPERT, SEQ, None),
            P(),
            P(EXPERT, "dp", None),
            P(EXPERT, None),
            P(EXPERT, DP_SEQ),
            P(EXPERT, None),
        ),
        out_specs=(P(), P(DP_EXPERT, SEQ, None), P(DP_SEQ_EXPERT, None)),
        check_vma=False,
    )
```

time: 519 us -> 3210 us (6.18)
  waiting for transfers between devices: 159 us -> 2490 us
  blocking collectives: 239 us -> 602 us
    all_gather x0 -> x2, waiting for transfers between devices: none -> 1980 us  [the longest x1 1380 us: shards(): d_mix_all = lax.all_gather(d_mix, ROWS, axis=0, tiled=True)]
    unnamed x2 -> x4, waiting for transfers between devices: 0.03 us -> 480 us
    all_gather x0 -> x1, blocking collectives: none -> 463 us  [shards(): block_routes = lax.all_gather(routes[0], DP_EXPERT, axis=0)]
    all_to_all x3 -> x1, blocking collectives: 144 us -> 32.4 us  [shards(): lax.all_to_all(packed.reshape(1, *packed.shape), DP_SEQ, split_axis=2, co...]
    reduce_scatter x2 -> x0, waiting for transfers between devices: 52.8 us -> none  [reduced_to_own(): blocks = lax.psum_scatter(blocks, axes[k], scatter_dimension=0, tiled=True)]
    all_to_all x4 -> x0, waiting for transfers between devices: 40.2 us -> none  [the longest x1 19.1 us: shards(): lax.all_to_all(weighted.reshape(1, number_of_steps, QUERY_HEADS, HEAD_WID...]
    psum x5 -> x1, blocking collectives: 94.8 us -> 107 us  [shards(): summed = lax.psum(payload, ROWS)]
  transfers between devices with their start and end apart: 11 -> 5, of which waited for: 10 -> 5; matrix products, arithmetic and copies ran while one was open for 2% -> 0% of each run, Pallas kernels for 0% -> 0%
where the time goes in v1:
time: 3210 us
  waiting for transfers between devices  2490 us (78%)
  blocking collectives  602 us (19%)
    all_gather x1, waiting for transfers between devices, shards(): d_mix_all = lax.all_gather(d_mix, ROWS, axis=0, tiled=True)  1380 us
    all_gather x1, waiting for transfers between devices, shards(): normed_all = lax.all_gather(normed, ROWS, axis=0, tiled=True)  593 us
    unnamed x4, waiting for transfers between devices  480 us
    all_gather x1, blocking collectives, shards(): block_routes = lax.all_gather(routes[0], DP_EXPERT, axis=0)  463 us
    psum x1, blocking collectives, shards(): summed = lax.psum(payload, ROWS)  107 us
  transfers between devices with their start and end apart: 5, of which 5 were waited for; matrix products, arithmetic and copies ran while one was open for 0% of the time, Pallas kernels for 0%

profile of v1, /device:TPU:1, one launch (start us, length us, event | category | flops | bytes accessed | tf_op | source)
XLA Modules:
  0.0 3206.8 jit_solution(4722802899857417348)
XLA Ops:
  7.2 0.8 reduce.14
  9.0 2.2 reduce.15
  11.3 0.9 reshape.490
  12.1 16.7 all-to-all-start
  29.3 18.7 all-to-all-done
  53.0 32.4 %all_to_all.28 = bf16[1,32,32,132]{3,1,0,2:T(8,128)(2,1)S(1)} all-to-all(bf16[1,32,32,132]{3,1,0,2:T(8,128)(2,1)S(1)} %copy.165), channel_id=1, replica_groups=mesh['dp'=8,'seq_0'=2,'seq_1'=2,'expert_0'=4,'expert_1'=4] {'dp','seq_0'..., dimensions={2} | all-to-all | bytes 540672 | tf_op jit(solution)/shard_map/all_to_all | solution.py:151
  85.4 1.1 copy.166
  88.0 0.7 reshape.492
  88.7 9.7 all-to-all-start.2
  98.5 15.2 all-to-all-done.2
  116.6 462.9 %all_gather.9 = s32[128,4,8]{2,1,0:T(4,128)S(1)} all-gather(s32[1,4,8]{2,1,0:T(4,128)S(1)} %copy-done.17), channel_id=1, replica_groups=mesh['dp'=8,'seq_0'=2,'seq_1'=2,'expert_0'=4,'expert_1'=4] {'dp','expert..., dimensions={0}, use_global_device_ids=true | all-gather | bytes 16512 | tf_op jit(solution)/shard_map/all_gather | solution.py:93
  580.5 593.1 %all-gather.5.cloned.1.call-done = bf16[1048576]{0:T(1024)(128)(2,1)} async-done(((bf16[2048]{0:T(1024)(128)(2,1)}), bf16[1048576]{0:T(1024)(128)(2,1)}) %all-gather.5.cloned.1.call-update) | async-done | bytes 2097168 | tf_op jit(solution)/shard_map/all_gather | solution.py:166
  1173.6 2.8 reshape.484
  1176.4 2.8 fusion.21
  1179.9 7.3 select_reduce_fusion.1
  1187.3 0.8 reduce_max.32
  1188.1 1.4 sub.91
  1189.4 1.3 fusion.45
  1190.7 1.4 div.48
  1192.1 1.3 copy.173
  1193.4 0.8 copy.171
  1194.9 0.9 select_reduce_fusion.2
  1195.9 2.1 fusion.7
  1198.0 4.1 broadcast_multiply_fusion
  1203.5 480.3 %all-reduce.3.cloned.1.call-done = f32[512,2048]{1,0:T(8,128)} async-done(((f32[512,2048]{1,0:T(8,128)}), f32[512,2048]{1,0:T(8,128)}) %all-reduce.3.cloned.1.call-update) | async-done | bytes 4194320
  1683.8 1.5 multiply_reduce_fusion.4
  1693.2 1384.5 %all-gather.7.cloned.1.call-done = bf16[512,1,2048]{2,1,0:T(2,128)(2,1)} async-done(((bf16[1,1,2048]{2,1,0:T(2,128)(2,1)}), bf16[512,1,2048]{2,1,0:T(2,128)(2,1)}) %all-gather.7.cloned.1.call-update) | async-done | bytes 2097168 | tf_op jit(solution)/shard_map/all_gather | solution.py:190
  3077.8 4.8 fusion
  3082.6 106.9 %psum.7 = f32[512,9]{0,1:T(8,128)S(1)} all-reduce(f32[512,9]{0,1:T(8,128)S(1)} %pad_maximum_fusion.2), channel_id=1, replica_groups=mesh['dp'=8,'seq_0'=2,'seq_1'=2,'expert_0'=4,'expert_1'=4] {'dp','seq_0'..., use_global_device_ids=true, to_apply=%region_18.19 | all-reduce | flops 4608 | bytes 36864 | tf_op jit(solution)/shard_map/psum | solution.py:206
  3190.3 2.5 select_reduce_fusion
  3192.8 2.3 fusion.52
  3195.7 4.6 fusion.2
  (113 shorter events, 16.4 us)
Async XLA Ops:
  7.2 1190.9 %copy-start = (bf16[1,192,2048]{2,1,0:T(8,128)(2,1)S(1)}, bf16[1,192,2048]{2,1,0:T(8,128)(2,1)}, u32[]{:S(2)}) copy-start(bf16[1,192,2048]{2,1,0:T(8,128)(2,1)} %param.24) | copy-start | bytes 2359300
  7.2 21.7 copy-start.8
  7.2 21.8 copy-start.19
  7.2 22.0 copy-start.18
  9.0 39.7 %copy-start.7 = (bf16[1,128,512]{2,1,0:T(8,128)(2,1)S(1)}, bf16[1,128,512]{2,1,0:T(8,128)(2,1)}, u32[]{:S(2)}) copy-start(bf16[1,128,512]{2,1,0:T(8,128)(2,1)} %param.15) | copy-start | bytes 393220
  12.1 35.9 %all-to-all-start = ((bf16[32,2,2048]{2,1,0:T(2,128)(2,1)}), bf16[32,2,2048]{2,1,0:T(2,128)(2,1)S(1)}, u32[]{:S(2)}, u32[]{:S(2)}) async-start(bf16[32,2,2048]{2,1,0:T(2,128)(2,1)} %reshape.490), calls=%async_computation | async-start | bytes 524288 | tf_op jit(solution)/shard_map/all_to_all | solution.py:30
  53.0 34.1 %copy-start.1 = (bf16[128,2048]{1,0:T(8,128)(2,1)S(1)}, bf16[128,2048]{1,0:T(8,128)(2,1)}, u32[]{:S(2)}) copy-start(bf16[128,2048]{1,0:T(8,128)(2,1)} %param.19) | copy-start | bytes 1572868
  85.3 13.1 copy-start.13
  86.5 29.4 copy-start.16
  86.5 30.1 copy-start.17
  88.7 25.0 all-to-all-start.2
  98.4 1075.2 %all-gather.5.cloned.1.call-start = ((), (), s32[]{:S(2)}) async-start(), calls=%async_computation.3 | async-start | bytes 2101248 | tf_op jit(solution)/shard_map/all_gather | solution.py:166
  114.0 0.6 copy-start.9
  116.5 1567.2 %all-reduce.3.cloned.1.call-start = ((), (), s32[]{:S(2)}) async-start(), calls=%async_computation.5 | async-start | bytes 8388608
  579.9 0.6 copy-start.5
  1176.4 2.8 copy-start.2
  1198.0 4.1 copy-start.3
  1202.1 0.7 copy-start.15
  1202.1 481.7 %copy-start.10 = (f32[2048]{0:T(1024)S(1)}, f32[2048]{0:T(1024)}, u32[]{:S(2)}) copy-start(f32[2048]{0:T(1024)} %copy-done.9) | copy-start | bytes 24580
  1202.1 481.7 %copy-start.14 = (bf16[1,1,2048]{2,1,0:T(2,128)(2,1)S(1)}, bf16[1,1,2048]{2,1,0:T(2,128)(2,1)}, u32[]{:S(2)}) copy-start(bf16[1,1,2048]{2,1,0:T(2,128)(2,1)} %param.18) | copy-start | bytes 12292
  1202.2 1875.6 %all-gather.7.cloned.1.call-start = ((), (), s32[]{:S(2)}) async-start(), calls=%async_computation.4 | async-start | bytes 4202496 | tf_op jit(solution)/shard_map/all_gather | solution.py:190
  3077.8 4.8 copy-start.6
  3077.8 111.8 %copy-start.11 = (f32[512]{0:T(512)S(1)}, f32[512]{0:T(512)}, u32[]{:S(2)}) copy-start(f32[512]{0:T(512)} %reduce_max.32) | copy-start | bytes 6148
  3077.8 111.8 %copy-start.12 = (f32[512]{0:T(512)S(1)}, f32[512]{0:T(512)}, u32[]{:S(2)}) copy-start(f32[512]{0:T(512)} %fusion.45) | copy-start | bytes 6148
  3190.3 5.4 copy-start.4
Sparse Core Ops, SparseCore 0:
  116.7 1056.8 all-gather.4
  1202.3 481.4 all-reduce.2
  1689.4 1388.3 all-gather.6

commit v2 on v1

--- a/solution.py
+++ b/solution.py
@@ -12,7 +12,6 @@
 SEQ = ("seq_0", "seq_1")
 DP_SEQ_EXPERT = ("dp", "seq_0", "seq_1", "expert_0", "expert_1")
 EXPERT = ("expert_0", "expert_1")
-ROWS = DP_SEQ_EXPERT
 
 
 MASKED = -1e30
@@ -52,6 +51,10 @@
 
 def head_logit(final, head_vec):
     return jnp.sum(final * rms_scale(final) * head_vec.astype(jnp.float32)[None, :], axis=1)
+
+
+def move_rows(buffer):
+    return lax.all_to_all(buffer, DP_EXPERT, split_axis=0, concat_axis=0, tiled=True)
 
 
 def split_pair(value):
@@ -90,11 +93,6 @@
     labels,
     trace_len,
 ):
-    block_routes = lax.all_gather(routes[0], DP_EXPERT, axis=0)
-    block_routes = block_routes.reshape(
-        lax.axis_size("dp"), lax.axis_size(EXPERT), *routes.shape[1:]
-    )
-    routes_all = jnp.swapaxes(block_routes, 1, 2).reshape(-1, routes.shape[2])
     count_of_keys = keys.shape[1]
     query_groups = QUERY_HEADS // KEY_VALUE_HEADS
     query_all = gather_directly(queries, DP_SEQ, 1)[0]
@@ -163,58 +161,110 @@
     normed = (stream * rms_scale(stream) * norm_gain.astype(jnp.float32)[None, :]).astype(
         jnp.bfloat16
     )
-    normed_all = lax.all_gather(normed, ROWS, axis=0, tiled=True)
+    block_normed = gather_directly(normed, SEQ, 0)
+    block_rows = routes.shape[1]
+    topk = routes.shape[2]
     experts = router.shape[1]
-    logits = jnp.dot(normed_all, router, preferred_element_type=jnp.float32)
-    chosen = (routes_all[:, :, None] == jnp.arange(experts, dtype=jnp.int32)[None, None, :]).astype(
+    width = block_normed.shape[1]
+    capacity = min(block_rows, 2 * ((block_rows * topk + experts - 1) // experts))
+    route_ids = routes[0]
+    logits = jnp.dot(block_normed, router, preferred_element_type=jnp.float32)
+    chosen = (route_ids[:, :, None] == jnp.arange(experts, dtype=jnp.int32)[None, None, :]).astype(
         jnp.float32
     )
     picked = jnp.sum(chosen * logits[:, None, :], axis=2)
     gate_weight = jax.nn.softmax(picked, axis=-1)
-    mine = routes_all == lax.axis_index(DP_EXPERT)
-    coef = jnp.sum(jnp.where(mine, gate_weight, 0.0), axis=1)
-    gate_act = jnp.dot(normed_all, w_gate[0], preferred_element_type=jnp.float32)
-    up_act = jnp.dot(normed_all, w_up[0], preferred_element_type=jnp.float32)
+    flat_routes = route_ids.reshape(-1)
+    onehot = (flat_routes[:, None] == jnp.arange(experts, dtype=jnp.int32)[None, :]).astype(
+        jnp.int32
+    )
+    order_rank = jnp.sum((jnp.cumsum(onehot, axis=0) - 1) * onehot, axis=1)
+    slot_index = flat_routes * capacity + order_rank
+    slot_map = (
+        slot_index[:, None] == jnp.arange(experts * capacity, dtype=jnp.int32)[None, :]
+    ).astype(jnp.float32)
+    place_map = slot_map.reshape(block_rows, topk, experts * capacity)
+    row_map = jnp.sum(place_map, axis=1)
+    weight_map = jnp.sum(gate_weight[:, :, None] * place_map, axis=1)
+    contract_rows = (((0,), (0,)), ((), ()))
+    send_rows = lax.dot_general(
+        row_map.astype(jnp.bfloat16),
+        block_normed,
+        contract_rows,
+        preferred_element_type=jnp.float32,
+    ).astype(jnp.bfloat16)
+    arrived = move_rows(send_rows.reshape(experts, capacity, width))
+    arrived = arrived.reshape(experts * capacity, width)
+    gate_act = jnp.dot(arrived, w_gate[0], preferred_element_type=jnp.float32)
+    up_act = jnp.dot(arrived, w_up[0], preferred_element_type=jnp.float32)
     hidden = (jax.nn.silu(gate_act) * up_act).astype(jnp.bfloat16)
-    expert_out = jnp.dot(hidden, w_down[0], preferred_element_type=jnp.float32)
-    expert_mix = lax.psum_scatter(
-        coef[:, None] * expert_out, ROWS, scatter_dimension=0, tiled=True
-    )
+    partial_value = jnp.dot(hidden, w_down[0], preferred_element_type=jnp.float32)
+    returned = move_rows(partial_value.astype(jnp.bfloat16).reshape(experts, capacity, width))
+    returned = returned.reshape(experts * capacity, width)
+    route_part = jnp.dot(
+        slot_map.astype(jnp.bfloat16), returned, preferred_element_type=jnp.float32
+    ).astype(jnp.bfloat16)
+    shares = lax.all_to_all(
+        route_part.reshape(block_rows, topk, width), SEQ, split_axis=0, concat_axis=0, tiled=True
+    )
+    expert_out = jnp.sum(shares.astype(jnp.float32), axis=0)
+    me = lax.axis_index(SEQ)
+    own_gate = lax.dynamic_index_in_dim(gate_weight, me, 0, keepdims=False)
+    expert_mix = jnp.sum(own_gate[:, None] * expert_out, axis=0, keepdims=True)
     final = stream + expert_mix
     reward, pull = jax.vjp(lambda value: head_logit(value, head_vec), final)
     target = labels[0].astype(jnp.float32)
-    loss_term = jax.nn.softplus(reward) - target * reward
+    loss_term = jnp.sum(jax.nn.softplus(reward) - target * reward)
     logit_grad = jax.nn.sigmoid(reward) - target
     (final_grad,) = pull(logit_grad)
     d_mix = final_grad.astype(jnp.bfloat16)
-    d_mix_all = lax.all_gather(d_mix, ROWS, axis=0, tiled=True)
-    d_mix_wide = d_mix_all.astype(jnp.float32)
-    contract_rows = (((0,), (0,)), ((), ()))
-    d_out = (coef[:, None] * d_mix_wide).astype(jnp.bfloat16)
-    grad_down = lax.dot_general(hidden, d_out, contract_rows, preferred_element_type=jnp.float32)
-    grad_down = grad_down.astype(jnp.bfloat16).reshape((1,) + grad_down.shape)
-    share_dot = jnp.sum(d_mix_wide * expert_out, axis=1)
-    row_count = normed_all.shape[0]
-    own_row = jnp.arange(row_count, dtype=jnp.int32) == lax.axis_index(ROWS)
-    payload = jnp.concatenate(
+    route_dot = jnp.sum(d_mix.astype(jnp.float32) * expert_out, axis=1)
+    pick_grad = own_gate * (route_dot - jnp.sum(own_gate * route_dot))
+    pick_hi, pick_lo = split_pair(pick_grad)
+    loss_hi, loss_lo = split_pair(loss_term)
+    side = jnp.concatenate([pick_hi, pick_lo, loss_hi[None], loss_lo[None]])
+    side = jnp.pad(side, (0, width - side.shape[0]))
+    bundle = jnp.stack([d_mix[0], side])
+    block_bundle = from_everyone(bundle, SEQ)
+    block_grads = block_bundle[:, 0, :]
+    block_pick = join_pair(block_bundle[:, 1, :topk], block_bundle[:, 1, topk : 2 * topk])
+    block_loss = jnp.sum(join_pair(block_bundle[:, 1, 2 * topk], block_bundle[:, 1, 2 * topk + 1]))
+    d_out = lax.dot_general(
+        weight_map, block_grads.astype(jnp.float32), contract_rows, precision=lax.Precision.HIGHEST
+    ).astype(jnp.bfloat16)
+    d_logits = jnp.sum(chosen * block_pick[:, :, None], axis=1)
+    columns = block_normed.reshape(
+        block_rows, lax.axis_size("dp"), lax.axis_size(SEQ), lax.axis_size(EXPERT), -1
+    )
+    my_columns = lax.dynamic_index_in_dim(columns, me, 2, keepdims=False).reshape(block_rows, -1)
+    router_part = lax.dot_general(
+        my_columns.astype(jnp.float32), d_logits, contract_rows, precision=lax.Precision.HIGHEST
+    )
+    owners = lax.axis_size(DP_EXPERT)
+    router_chunks = router_part.reshape(owners, -1)
+    chunk = router_chunks.shape[1]
+    router_hi, router_lo = split_pair(router_chunks)
+    block_hi, block_lo = split_pair(block_loss)
+    extra_row = jnp.concatenate(
         [
-            jnp.where(mine, share_dot[:, None], 0.0),
-            jnp.where(own_row, loss_term, 0.0)[:, None],
+            router_hi,
+            router_lo,
+            jnp.broadcast_to(block_hi, (owners, 1)),
+            jnp.broadcast_to(block_lo, (owners, 1)),
+            jnp.zeros((owners, width - 2 * chunk - 2), jnp.bfloat16),
         ],
         axis=1,
     )
-    summed = lax.psum(payload, ROWS)
-    route_dot = summed[:, :-1]
-    loss = jnp.sum(summed[:, -1])
-    pick_grad = gate_weight * (route_dot - jnp.sum(gate_weight * route_dot, axis=1, keepdims=True))
-    d_logits = jnp.sum(chosen * pick_grad[:, :, None], axis=1)
-    router_grad_all = lax.dot_general(
-        normed_all.astype(jnp.float32), d_logits, contract_rows, precision=lax.Precision.HIGHEST
-    )
-    own_rows = router_grad_all.shape[0] // lax.axis_size(DP_SEQ_EXPERT)
-    grad_router = lax.dynamic_slice_in_dim(
-        router_grad_all, lax.axis_index(DP_SEQ_EXPERT) * own_rows, own_rows, axis=0
-    ).astype(jnp.bfloat16)
+    sent = jnp.concatenate([d_out.reshape(experts, capacity, width), extra_row[:, None, :]], axis=1)
+    got = move_rows(sent)
+    grads_arrived = got[:, :capacity].reshape(experts * capacity, width)
+    grad_down = lax.dot_general(
+        hidden, grads_arrived, contract_rows, preferred_element_type=jnp.float32
+    )
+    grad_down = grad_down.astype(jnp.bfloat16).reshape((1,) + grad_down.shape)
+    router_sum = jnp.sum(join_pair(got[:, capacity, :chunk], got[:, capacity, chunk : 2 * chunk]), axis=0)
+    grad_router = router_sum.reshape(-1, experts).astype(jnp.bfloat16)
+    loss = jnp.sum(join_pair(got[:, capacity, 2 * chunk], got[:, capacity, 2 * chunk + 1]))
     return (loss, grad_down, grad_router)
 
 

time: 3210 us -> 434 us (0.14)
  waiting for transfers between devices: 2490 us -> 120 us
  blocking collectives: 602 us -> 207 us
    all_gather x2 -> x0, waiting for transfers between devices: 1980 us -> none  [the longest x1 1380 us: shards(): d_mix_all = lax.all_gather(d_mix, ROWS, axis=0, tiled=True)]
    unnamed x4 -> x0, waiting for transfers between devices: 480 us -> none
    all_gather x1 -> x0, blocking collectives: 463 us -> none  [shards(): block_routes = lax.all_gather(routes[0], DP_EXPERT, axis=0)]
    all_to_all x0 -> x2, blocking collectives: none -> 174 us  [move_rows(): lax.all_to_all(buffer, DP_EXPERT, split_axis=0, concat_axis=0, tiled=True)]
    psum x1 -> x0, blocking collectives: 107 us -> none  [shards(): summed = lax.psum(payload, ROWS)]
    all_to_all x0 -> x2, waiting for transfers between devices: none -> 63.5 us  [the longest x1 53.1 us: move_rows(): lax.all_to_all(buffer, DP_EXPERT, split_axis=0, concat_axis=0, tiled=True)]
  transfers between devices with their start and end apart: 5 -> 6, of which waited for: 5 -> 6; matrix products, arithmetic and copies ran while one was open for 0% -> 1% of each run, Pallas kernels for 0% -> 0%
where the time goes in v2:
time: 434 us; the launch traced here: 433 us
  blocking collectives  207 us (48%)
  waiting for transfers between devices  120 us (28%)
  starting transfers between devices  47.6 us (11%)
  local copies, waits for them, and re-layouts  21 us (5%)
  other arithmetic  17.4 us (4%)
  between operations  9.91 us (2%)
  matrix products  9.34 us (2%)
    all_to_all x2, blocking collectives, move_rows(): lax.all_to_all(buffer, DP_EXPERT, split_axis=0, concat_axis=0, tiled=True)  174 us
    all_to_all x1, waiting for transfers between devices, move_rows(): lax.all_to_all(buffer, DP_EXPERT, split_axis=0, concat_axis=0, tiled=True)  53.1 us
    all_to_all x3, waiting for transfers between devices, from_everyone(): return lax.all_to_all(copies, axis, split_axis=0, concat_axis=0, tiled=True)  42.2 us
    all_to_all x1, blocking collectives, shards(): lax.all_to_all(packed.reshape(1, *packed.shape), DP_SEQ, split_axis=2, co...  32.4 us
    all_to_all x3, starting transfers between devices, from_everyone(): return lax.all_to_all(copies, axis, split_axis=0, concat_axis=0, tiled=True)  24.6 us
    all_to_all x1, waiting for transfers between devices, sent_and_summed(): lax.all_to_all(in_blocks(array, dim, count), axis, 0, 0, tiled=True)  14.8 us
    all_to_all x1, waiting for transfers between devices, shards(): lax.all_to_all(route_part.reshape(block_rows, topk, width), SEQ, split_ax...  10.4 us
    all_to_all x1, starting transfers between devices, sent_and_summed(): lax.all_to_all(in_blocks(array, dim, count), axis, 0, 0, tiled=True)  9.68 us
  transfers between devices with their start and end apart: 6, of which 6 were waited for; matrix products, arithmetic and copies ran while one was open for 1% of the time, Pallas kernels for 0%

profile of v2, /device:TPU:1, one launch (start us, length us, event | category | flops | bytes accessed | tf_op | source)
XLA Modules:
  0.0 432.6 jit_solution(12878074573683487067)
XLA Ops:
  0.7 0.8 reduce.17
  2.5 2.2 reduce.19
  4.7 0.9 reshape.576
  5.6 16.7 %all-to-all-start = ((bf16[32,2,2048]{2,1,0:T(2,128)(2,1)}), bf16[32,2,2048]{2,1,0:T(2,128)(2,1)S(1)}, u32[]{:S(2)}, u32[]{:S(2)}) async-start(bf16[32,2,2048]{2,1,0:T(2,128)(2,1)} %reshape.576), calls=%async_computation | async-start | bytes 524288 | tf_op jit(solution)/shard_map/all_to_all | solution.py:29
  22.8 18.7 %all-to-all-done = bf16[32,2,2048]{2,1,0:T(2,128)(2,1)S(1)} async-done(((bf16[32,2,2048]{2,1,0:T(2,128)(2,1)}), bf16[32,2,2048]{2,1,0:T(2,128)(2,1)S(1)}, u32[]{:S(2)}, u32[]{:S(2)}) %all-to-all-start) | async-done | bytes 262176 | tf_op jit(solution)/shard_map/all_to_all | solution.py:29
  46.4 32.4 %all_to_all.58 = bf16[1,32,32,132]{3,1,0,2:T(8,128)(2,1)S(1)} all-to-all(bf16[1,32,32,132]{3,1,0,2:T(8,128)(2,1)S(1)} %copy.103), channel_id=1, replica_groups=mesh['dp'=8,'seq_0'=2,'seq_1'=2,'expert_0'=4,'expert_1'=4] {'dp','seq_0'..., dimensions={2} | all-to-all | bytes 540672 | tf_op jit(solution)/shard_map/all_to_all | solution.py:149
  78.8 1.1 copy.104
  82.2 9.7 %all-to-all-start.2 = ((bf16[32,2,1024]{2,1,0:T(2,128)(2,1)}), bf16[32,2,1024]{2,1,0:T(2,128)(2,1)S(1)}, u32[]{:S(2)}, u32[]{:S(2)}) async-start(bf16[32,2,1024]{2,1,0:T(2,128)(2,1)} %reshape.578), calls=%async_computation.2 | async-start | bytes 262144 | tf_op jit(solution)/shard_map/all_to_all | solution.py:44
  92.4 14.8 %all-to-all-done.2 = bf16[32,2,1024]{2,1,0:T(2,128)(2,1)S(1)} async-done(((bf16[32,2,1024]{2,1,0:T(2,128)(2,1)}), bf16[32,2,1024]{2,1,0:T(2,128)(2,1)S(1)}, u32[]{:S(2)}, u32[]{:S(2)}) %all-to-all-start.2) | async-done | bytes 131104 | tf_op jit(solution)/shard_map/all_to_all | solution.py:44
  110.2 3.6 all-to-all-start.3
  113.8 11.8 %all-to-all-done.3 = bf16[4,2,1024]{2,1,0:T(2,128)(2,1)S(1)} async-done(((bf16[4,2,1024]{2,1,0:T(2,128)(2,1)}), bf16[4,2,1024]{2,1,0:T(2,128)(2,1)S(1)}, u32[]{:S(2)}, u32[]{:S(2)}) %all-to-all-start.3) | async-done | bytes 16416 | tf_op jit(solution)/shard_map/all_to_all | solution.py:29
  127.7 68.4 %all_to_all.59 = bf16[128,2,2048]{2,1,0:T(2,128)(2,1)} all-to-all(bf16[128,2,2048]{2,1,0:T(2,128)(2,1)S(1)} %reshape.561), channel_id=1, replica_groups=mesh['dp'=8,'seq_0'=2,'seq_1'=2,'expert_0'=4,'expert_1'=4] {'dp','expert..., dimensions={0} | all-to-all | bytes 2097152 | tf_op jit(solution)/shard_map/all_to_all | solution.py:57
  196.1 1.5 reshape.562
  198.1 1.6 fusion.4
  200.3 1.5 reshape.563
  201.8 7.8 %all-to-all-start.5 = ((bf16[128,2,2048]{2,1,0:T(2,128)(2,1)}), bf16[128,2,2048]{2,1,0:T(2,128)(2,1)S(1)}, u32[]{:S(2)}, u32[]{:S(2)}) async-start(bf16[128,2,2048]{2,1,0:T(2,128)(2,1)} %reshape.563), calls=%async_computation.5 | async-start | bytes 2097152 | tf_op jit(solution)/shard_map/all_to_all | solution.py:57
  209.6 53.1 %all-to-all-done.5 = bf16[128,2,2048]{2,1,0:T(2,128)(2,1)S(1)} async-done(((bf16[128,2,2048]{2,1,0:T(2,128)(2,1)}), bf16[128,2,2048]{2,1,0:T(2,128)(2,1)S(1)}, u32[]{:S(2)}, u32[]{:S(2)}) %all-to-all-start.5) | async-done | bytes 1048608 | tf_op jit(solution)/shard_map/all_to_all | solution.py:57
  263.1 1.0 fusion.2
  264.1 5.5 %all-to-all-start.6 = ((bf16[4,8,2048]{2,1,0:T(8,128)(2,1)}), bf16[4,8,2048]{2,1,0:T(8,128)(2,1)S(1)}, u32[]{:S(2)}, u32[]{:S(2)}) async-start(bf16[4,8,2048]{2,1,0:T(8,128)(2,1)} %fusion.2), calls=%async_computation.6 | async-start | bytes 262144 | tf_op jit(solution)/shard_map/all_to_all | solution.py:207
  270.4 1.1 reshape_reshape.3
  271.5 10.4 %all-to-all-done.6 = bf16[4,8,2048]{2,1,0:T(8,128)(2,1)S(1)} async-done(((bf16[4,8,2048]{2,1,0:T(8,128)(2,1)}), bf16[4,8,2048]{2,1,0:T(8,128)(2,1)S(1)}, u32[]{:S(2)}, u32[]{:S(2)}) %all-to-all-start.6) | async-done | bytes 131104 | tf_op jit(solution)/shard_map/all_to_all | solution.py:207
  292.0 4.3 all-to-all-start.7
  296.5 11.7 %all-to-all-done.7 = bf16[4,2,2048]{2,1,0:T(2,128)(2,1)S(1)} async-done(((bf16[4,2,2048]{2,1,0:T(2,128)(2,1)}), bf16[4,2,2048]{2,1,0:T(2,128)(2,1)S(1)}, u32[]{:S(2)}, u32[]{:S(2)}) %all-to-all-start.7) | async-done | bytes 32800 | tf_op jit(solution)/shard_map/all_to_all | solution.py:29
  311.2 0.8 copy.106
  312.0 1.0 convolution_convert_fusion
  313.1 1.5 reshape.567
  314.6 3.2 pad_maximum_fusion
  317.9 106.1 %all_to_all.60 = bf16[128,3,2048]{2,1,0:T(4,128)(2,1)S(1)} all-to-all(bf16[128,3,2048]{2,1,0:T(4,128)(2,1)S(1)} %pad_maximum_fusion), channel_id=1, replica_groups=mesh['dp'=8,'seq_0'=2,'seq_1'=2,'expert_0'=4,'expert_1'=4] {'dp','expert..., dimensions={0} | all-to-all | bytes 3145728 | tf_op jit(solution)/shard_map/all_to_all | solution.py:57
  424.0 1.9 slice.108
  425.9 2.3 reshape.570
  428.2 2.5 fusion
  431.5 1.2 fusion.24
  (121 shorter events, 21.5 us)
Async XLA Ops:
  0.6 199.1 %copy-start = (bf16[1,192,2048]{2,1,0:T(8,128)(2,1)S(1)}, bf16[1,192,2048]{2,1,0:T(8,128)(2,1)}, u32[]{:S(2)}) copy-start(bf16[1,192,2048]{2,1,0:T(8,128)(2,1)} %param.24) | copy-start | bytes 2359300
  0.6 21.7 %copy-start.5 = (bf16[1,128,512]{2,1,0:T(8,128)(2,1)S(1)}, bf16[1,128,512]{2,1,0:T(8,128)(2,1)}, u32[]{:S(2)}) copy-start(bf16[1,128,512]{2,1,0:T(8,128)(2,1)} %param.16) | copy-start | bytes 393220
  0.7 21.8 %copy-start.11 = (s32[1,8]{1,0:T(1,128)S(1)}, s32[1,8]{1,0:T(1,128)}, u32[]{:S(2)}) copy-start(s32[1,8]{1,0:T(1,128)} %param.29) | copy-start | bytes 100
  0.7 22.0 %copy-start.10 = (s32[1,32]{1,0:T(1,128)S(1)}, s32[1,32]{1,0:T(1,128)}, u32[]{:S(2)}) copy-start(s32[1,32]{1,0:T(1,128)} %param.27) | copy-start | bytes 388
  2.5 39.7 %copy-start.4 = (bf16[1,128,512]{2,1,0:T(8,128)(2,1)S(1)}, bf16[1,128,512]{2,1,0:T(8,128)(2,1)}, u32[]{:S(2)}) copy-start(bf16[1,128,512]{2,1,0:T(8,128)(2,1)} %param.15) | copy-start | bytes 393220
  5.6 35.9 %all-to-all-start = ((bf16[32,2,2048]{2,1,0:T(2,128)(2,1)}), bf16[32,2,2048]{2,1,0:T(2,128)(2,1)S(1)}, u32[]{:S(2)}, u32[]{:S(2)}) async-start(bf16[32,2,2048]{2,1,0:T(2,128)(2,1)} %reshape.576), calls=%async_computation | async-start | bytes 524288 | tf_op jit(solution)/shard_map/all_to_all | solution.py:29
  46.4 34.1 %copy-start.2 = (bf16[128,2048]{1,0:T(8,128)(2,1)S(1)}, bf16[128,2048]{1,0:T(8,128)(2,1)}, u32[]{:S(2)}) copy-start(bf16[128,2048]{1,0:T(8,128)(2,1)} %param.19) | copy-start | bytes 1572868
  78.8 13.1 %copy-start.7 = (s32[1,4,8]{2,1,0:T(4,128)S(1)}, s32[1,4,8]{2,1,0:T(4,128)}, u32[]{:S(2)}) copy-start(s32[1,4,8]{2,1,0:T(4,128)} %param.26) | copy-start | bytes 388
  78.8 13.2 %copy-start.8 = (bf16[1,1,2048]{2,1,0:T(2,128)(2,1)S(1)}, bf16[1,1,2048]{2,1,0:T(2,128)(2,1)}, u32[]{:S(2)}) copy-start(bf16[1,1,2048]{2,1,0:T(2,128)(2,1)} %param.18) | copy-start | bytes 12292
  79.9 28.9 %copy-start.9 = (bf16[2048]{0:T(1024)(128)(2,1)S(1)}, bf16[2048]{0:T(1024)(128)(2,1)}, u32[]{:S(2)}) copy-start(bf16[2048]{0:T(1024)(128)(2,1)} %param.20) | copy-start | bytes 12292
  79.9 45.7 %copy-start.3 = (bf16[2048,128]{1,0:T(8,128)(2,1)S(1)}, bf16[2048,128]{1,0:T(8,128)(2,1)}, u32[]{:S(2)}) copy-start(bf16[2048,128]{1,0:T(8,128)(2,1)} %param.21) | copy-start | bytes 1572868
  82.2 25.0 %all-to-all-start.2 = ((bf16[32,2,1024]{2,1,0:T(2,128)(2,1)}), bf16[32,2,1024]{2,1,0:T(2,128)(2,1)S(1)}, u32[]{:S(2)}, u32[]{:S(2)}) async-start(bf16[32,2,1024]{2,1,0:T(2,128)(2,1)} %reshape.578), calls=%async_computation.2 | async-start | bytes 262144 | tf_op jit(solution)/shard_map/all_to_all | solution.py:44
  110.2 15.4 %all-to-all-start.3 = ((bf16[4,2,1024]{2,1,0:T(2,128)(2,1)}), bf16[4,2,1024]{2,1,0:T(2,128)(2,1)S(1)}, u32[]{:S(2)}, u32[]{:S(2)}) async-start(bf16[4,2,1024]{2,1,0:T(2,128)(2,1)} %reshape.580), calls=%async_computation.3 | async-start | bytes 32768 | tf_op jit(solution)/shard_map/all_to_all | solution.py:29
  196.1 1.5 copy-start.1
  201.8 60.9 %all-to-all-start.5 = ((bf16[128,2,2048]{2,1,0:T(2,128)(2,1)}), bf16[128,2,2048]{2,1,0:T(2,128)(2,1)S(1)}, u32[]{:S(2)}, u32[]{:S(2)}) async-start(bf16[128,2,2048]{2,1,0:T(2,128)(2,1)} %reshape.563), calls=%async_computation.5 | async-start | bytes 2097152 | tf_op jit(solution)/shard_map/all_to_all | solution.py:57
  209.6 73.8 %copy-start.6 = (bf16[2048]{0:T(1024)(128)(2,1)S(1)}, bf16[2048]{0:T(1024)(128)(2,1)}, u32[]{:S(2)}) copy-start(bf16[2048]{0:T(1024)(128)(2,1)} %param.25) | copy-start | bytes 12292
  264.1 17.8 %all-to-all-start.6 = ((bf16[4,8,2048]{2,1,0:T(8,128)(2,1)}), bf16[4,8,2048]{2,1,0:T(8,128)(2,1)S(1)}, u32[]{:S(2)}, u32[]{:S(2)}) async-start(bf16[4,8,2048]{2,1,0:T(8,128)(2,1)} %fusion.2), calls=%async_computation.6 | async-start | bytes 262144 | tf_op jit(solution)/shard_map/all_to_all | solution.py:207
  292.0 16.2 %all-to-all-start.7 = ((bf16[4,2,2048]{2,1,0:T(2,128)(2,1)}), bf16[4,2,2048]{2,1,0:T(2,128)(2,1)S(1)}, u32[]{:S(2)}, u32[]{:S(2)}) async-start(bf16[4,2,2048]{2,1,0:T(2,128)(2,1)} %broadcast_in_dim.132), calls=%async_computation.7 | async-start | bytes 65536 | tf_op jit(solution)/shard_map/all_to_all | solution.py:29

commit v3 on v1

--- a/solution.py
+++ b/solution.py
@@ -12,7 +12,6 @@
 SEQ = ("seq_0", "seq_1")
 DP_SEQ_EXPERT = ("dp", "seq_0", "seq_1", "expert_0", "expert_1")
 EXPERT = ("expert_0", "expert_1")
-ROWS = DP_SEQ_EXPERT
 
 
 MASKED = -1e30
@@ -52,6 +51,14 @@
 
 def head_logit(final, head_vec):
     return jnp.sum(final * rms_scale(final) * head_vec.astype(jnp.float32)[None, :], axis=1)
+
+
+def across_group(buffer):
+    return lax.all_to_all(buffer, EXPERT, split_axis=0, concat_axis=0, tiled=True)
+
+
+def taken_together(array, axis):
+    return from_everyone(array, axis).sum(axis=0)
 
 
 def split_pair(value):
@@ -90,11 +97,7 @@
     labels,
     trace_len,
 ):
-    block_routes = lax.all_gather(routes[0], DP_EXPERT, axis=0)
-    block_routes = block_routes.reshape(
-        lax.axis_size("dp"), lax.axis_size(EXPERT), *routes.shape[1:]
-    )
-    routes_all = jnp.swapaxes(block_routes, 1, 2).reshape(-1, routes.shape[2])
+    pack_routes = gather_directly(routes[0], "dp", 0)
     count_of_keys = keys.shape[1]
     query_groups = QUERY_HEADS // KEY_VALUE_HEADS
     query_all = gather_directly(queries, DP_SEQ, 1)[0]
@@ -163,58 +166,95 @@
     normed = (stream * rms_scale(stream) * norm_gain.astype(jnp.float32)[None, :]).astype(
         jnp.bfloat16
     )
-    normed_all = lax.all_gather(normed, ROWS, axis=0, tiled=True)
+    pack_normed = gather_directly(normed, DP_SEQ, 0)
+    rows = pack_normed.shape[0]
+    width = pack_normed.shape[1]
+    block_rows = routes.shape[1]
+    topk = routes.shape[2]
     experts = router.shape[1]
-    logits = jnp.dot(normed_all, router, preferred_element_type=jnp.float32)
-    chosen = (routes_all[:, :, None] == jnp.arange(experts, dtype=jnp.int32)[None, None, :]).astype(
+    blocks = rows // block_rows
+    group_size = lax.axis_size(EXPERT)
+    capacity = min(block_rows, 2 * ((block_rows * topk + experts - 1) // experts))
+    per_source = blocks * capacity
+    slots = group_size * per_source
+    logits = jnp.dot(pack_normed, router, preferred_element_type=jnp.float32)
+    chosen = (pack_routes[:, :, None] == jnp.arange(experts, dtype=jnp.int32)[None, None, :]).astype(
         jnp.float32
     )
     picked = jnp.sum(chosen * logits[:, None, :], axis=2)
     gate_weight = jax.nn.softmax(picked, axis=-1)
-    mine = routes_all == lax.axis_index(DP_EXPERT)
-    coef = jnp.sum(jnp.where(mine, gate_weight, 0.0), axis=1)
-    gate_act = jnp.dot(normed_all, w_gate[0], preferred_element_type=jnp.float32)
-    up_act = jnp.dot(normed_all, w_up[0], preferred_element_type=jnp.float32)
+    row_has = jnp.sum(chosen, axis=1).reshape(blocks, block_rows, experts)
+    earlier = (jnp.cumsum(row_has, axis=1) - row_has).reshape(rows, experts)
+    rank = jnp.sum(chosen * earlier[:, None, :], axis=2).astype(jnp.int32)
+    block_of = (jnp.arange(rows, dtype=jnp.int32) // block_rows)[:, None]
+    in_group = (pack_routes // group_size) == lax.axis_index("dp")
+    dest_slot = (pack_routes % group_size) * per_source + block_of * capacity + rank
+    slot_map = (
+        (dest_slot[:, :, None] == jnp.arange(slots, dtype=jnp.int32)[None, None, :])
+        & in_group[:, :, None]
+    ).astype(jnp.float32)
+    row_map = jnp.sum(slot_map, axis=1)
+    weight_map = jnp.sum(gate_weight[:, :, None] * slot_map, axis=1)
+    contract_rows = (((0,), (0,)), ((), ()))
+    send_rows = lax.dot_general(
+        row_map.astype(jnp.bfloat16), pack_normed, contract_rows, preferred_element_type=jnp.float32
+    ).astype(jnp.bfloat16)
+    arrived = across_group(send_rows.reshape(group_size, per_source, width)).reshape(slots, width)
+    gate_act = jnp.dot(arrived, w_gate[0], preferred_element_type=jnp.float32)
+    up_act = jnp.dot(arrived, w_up[0], preferred_element_type=jnp.float32)
     hidden = (jax.nn.silu(gate_act) * up_act).astype(jnp.bfloat16)
-    expert_out = jnp.dot(hidden, w_down[0], preferred_element_type=jnp.float32)
-    expert_mix = lax.psum_scatter(
-        coef[:, None] * expert_out, ROWS, scatter_dimension=0, tiled=True
-    )
+    partial_value = jnp.dot(hidden, w_down[0], preferred_element_type=jnp.float32)
+    returned = across_group(
+        partial_value.astype(jnp.bfloat16).reshape(group_size, per_source, width)
+    ).reshape(slots, width)
+    group_mix = lax.dot_general(
+        weight_map,
+        returned.astype(jnp.float32),
+        (((1,), (0,)), ((), ())),
+        precision=lax.Precision.HIGHEST,
+    )
+    expert_mix = sent_and_summed(group_mix.astype(jnp.bfloat16), DP_SEQ, 0)
     final = stream + expert_mix
     reward, pull = jax.vjp(lambda value: head_logit(value, head_vec), final)
     target = labels[0].astype(jnp.float32)
-    loss_term = jax.nn.softplus(reward) - target * reward
+    loss_term = jnp.sum(jax.nn.softplus(reward) - target * reward)
     logit_grad = jax.nn.sigmoid(reward) - target
     (final_grad,) = pull(logit_grad)
     d_mix = final_grad.astype(jnp.bfloat16)
-    d_mix_all = lax.all_gather(d_mix, ROWS, axis=0, tiled=True)
-    d_mix_wide = d_mix_all.astype(jnp.float32)
-    contract_rows = (((0,), (0,)), ((), ()))
-    d_out = (coef[:, None] * d_mix_wide).astype(jnp.bfloat16)
-    grad_down = lax.dot_general(hidden, d_out, contract_rows, preferred_element_type=jnp.float32)
+    pack_grads = gather_directly(d_mix, DP_SEQ, 0)
+    d_out = lax.dot_general(
+        weight_map, pack_grads.astype(jnp.float32), contract_rows, precision=lax.Precision.HIGHEST
+    ).astype(jnp.bfloat16)
+    grads_arrived = across_group(d_out.reshape(group_size, per_source, width)).reshape(slots, width)
+    grad_down = lax.dot_general(
+        hidden, grads_arrived, contract_rows, preferred_element_type=jnp.float32
+    )
     grad_down = grad_down.astype(jnp.bfloat16).reshape((1,) + grad_down.shape)
-    share_dot = jnp.sum(d_mix_wide * expert_out, axis=1)
-    row_count = normed_all.shape[0]
-    own_row = jnp.arange(row_count, dtype=jnp.int32) == lax.axis_index(ROWS)
-    payload = jnp.concatenate(
-        [
-            jnp.where(mine, share_dot[:, None], 0.0),
-            jnp.where(own_row, loss_term, 0.0)[:, None],
-        ],
-        axis=1,
-    )
-    summed = lax.psum(payload, ROWS)
-    route_dot = summed[:, :-1]
-    loss = jnp.sum(summed[:, -1])
+    slot_grads = lax.dot_general(
+        row_map.astype(jnp.bfloat16), pack_grads, contract_rows, preferred_element_type=jnp.float32
+    )
+    slot_dots = jnp.sum(slot_grads * returned.astype(jnp.float32), axis=1)
+    dots_part = jnp.sum(slot_map * slot_dots[None, None, :], axis=2)
+    own_row = jnp.arange(rows, dtype=jnp.int32) == lax.axis_index(DP_SEQ)
+    payload = jnp.concatenate([dots_part, jnp.where(own_row, loss_term, 0.0)[:, None]], axis=1)
+    summed = taken_together(payload, DP_SEQ)
+    route_dot = summed[:, :topk]
+    pack_loss = jnp.sum(summed[:, topk])
     pick_grad = gate_weight * (route_dot - jnp.sum(gate_weight * route_dot, axis=1, keepdims=True))
     d_logits = jnp.sum(chosen * pick_grad[:, :, None], axis=1)
-    router_grad_all = lax.dot_general(
-        normed_all.astype(jnp.float32), d_logits, contract_rows, precision=lax.Precision.HIGHEST
-    )
-    own_rows = router_grad_all.shape[0] // lax.axis_size(DP_SEQ_EXPERT)
-    grad_router = lax.dynamic_slice_in_dim(
-        router_grad_all, lax.axis_index(DP_SEQ_EXPERT) * own_rows, own_rows, axis=0
-    ).astype(jnp.bfloat16)
+    columns = pack_normed.reshape(rows, lax.axis_size(DP_SEQ), -1)
+    my_columns = lax.dynamic_index_in_dim(columns, lax.axis_index(DP_SEQ), 1, keepdims=False)
+    router_part = lax.dot_general(
+        my_columns.astype(jnp.float32), d_logits, contract_rows, precision=lax.Precision.HIGHEST
+    )
+    router_part = router_part.reshape(group_size, -1)
+    chunk = router_part.shape[1]
+    sent = jnp.concatenate(
+        [router_part, jnp.broadcast_to(pack_loss, (group_size, 1))], axis=1
+    )
+    got = across_group(sent)
+    grad_router = jnp.sum(got[:, :chunk], axis=0).reshape(-1, experts).astype(jnp.bfloat16)
+    loss = jnp.sum(got[:, chunk])
     return (loss, grad_down, grad_router)
 
 

time: 3210 us -> 295 us (0.09)
  waiting for transfers between devices: 2490 us -> 110 us
  blocking collectives: 602 us -> 74.3 us
  starting transfers between devices: 26.6 us -> 61.1 us
    all_gather x2 -> x0, waiting for transfers between devices: 1980 us -> none  [the longest x1 1380 us: shards(): d_mix_all = lax.all_gather(d_mix, ROWS, axis=0, tiled=True)]
    unnamed x4 -> x0, waiting for transfers between devices: 480 us -> none
    all_gather x1 -> x0, blocking collectives: 463 us -> none  [shards(): block_routes = lax.all_gather(routes[0], DP_EXPERT, axis=0)]
    psum x1 -> x0, blocking collectives: 107 us -> none  [shards(): summed = lax.psum(payload, ROWS)]
    all_to_all x1 -> x5, waiting for transfers between devices: 18.7 us -> 62 us  [from_everyone(): return lax.all_to_all(copies, axis, split_axis=0, concat_axis=0, tiled=True)]
    all_to_all x0 -> x2, blocking collectives: none -> 42.1 us  [across_group(): lax.all_to_all(buffer, EXPERT, split_axis=0, concat_axis=0, tiled=True)]
  transfers between devices with their start and end apart: 5 -> 9, of which waited for: 5 -> 9; matrix products, arithmetic and copies ran while one was open for 0% -> 3% of each run, Pallas kernels for 0% -> 0%
where the time goes in v3:
time: 295 us; the launch traced here: 294 us
  waiting for transfers between devices  110 us (37%)
  blocking collectives  74.3 us (25%)
  starting transfers between devices  61.1 us (21%)
  other arithmetic  16.8 us (6%)
  local copies, waits for them, and re-layouts  14.2 us (5%)
  between operations  8.76 us (3%)
  matrix products  7.99 us (3%)
    all_to_all x5, waiting for transfers between devices, from_everyone(): return lax.all_to_all(copies, axis, split_axis=0, concat_axis=0, tiled=True)  62 us
    all_to_all x2, blocking collectives, across_group(): lax.all_to_all(buffer, EXPERT, split_axis=0, concat_axis=0, tiled=True)  42.1 us
    all_to_all x5, starting transfers between devices, from_everyone(): return lax.all_to_all(copies, axis, split_axis=0, concat_axis=0, tiled=True)  38 us
    all_to_all x1, blocking collectives, shards(): lax.all_to_all(packed.reshape(1, *packed.shape), DP_SEQ, split_axis=2, co...  32.2 us
    all_to_all x2, waiting for transfers between devices, sent_and_summed(): lax.all_to_all(in_blocks(array, dim, count), axis, 0, 0, tiled=True)  29.9 us
    all_to_all x2, waiting for transfers between devices, across_group(): lax.all_to_all(buffer, EXPERT, split_axis=0, concat_axis=0, tiled=True)  18.5 us
    all_to_all x2, starting transfers between devices, sent_and_summed(): lax.all_to_all(in_blocks(array, dim, count), axis, 0, 0, tiled=True)  16 us
    all_to_all x2, starting transfers between devices, across_group(): lax.all_to_all(buffer, EXPERT, split_axis=0, concat_axis=0, tiled=True)  7.16 us
  transfers between devices with their start and end apart: 9, of which 9 were waited for; matrix products, arithmetic and copies ran while one was open for 3% of the time, Pallas kernels for 0%

profile of v3, /device:TPU:1, one launch (start us, length us, event | category | flops | bytes accessed | tf_op | source)
XLA Modules:
  0.0 293.6 jit_solution(18202063471854159705)
XLA Ops:
  0.6 0.8 reduce.18
  2.5 2.2 reduce.20
  4.7 0.9 reshape.645
  5.6 16.7 %all-to-all-start = ((bf16[32,2,2048]{2,1,0:T(2,128)(2,1)}), bf16[32,2,2048]{2,1,0:T(2,128)(2,1)S(1)}, u32[]{:S(2)}, u32[]{:S(2)}) async-start(bf16[32,2,2048]{2,1,0:T(2,128)(2,1)} %reshape.645), calls=%async_computation | async-start | bytes 524288 | tf_op jit(solution)/shard_map/all_to_all | solution.py:29
  22.9 18.6 %all-to-all-done = bf16[32,2,2048]{2,1,0:T(2,128)(2,1)S(1)} async-done(((bf16[32,2,2048]{2,1,0:T(2,128)(2,1)}), bf16[32,2,2048]{2,1,0:T(2,128)(2,1)S(1)}, u32[]{:S(2)}, u32[]{:S(2)}) %all-to-all-start) | async-done | bytes 262176 | tf_op jit(solution)/shard_map/all_to_all | solution.py:29
  46.3 32.2 %all_to_all.80 = bf16[1,32,32,132]{3,1,0,2:T(8,128)(2,1)S(1)} all-to-all(bf16[1,32,32,132]{3,1,0,2:T(8,128)(2,1)S(1)} %copy.95), channel_id=1, replica_groups=mesh['dp'=8,'seq_0'=2,'seq_1'=2,'expert_0'=4,'expert_1'=4] {'dp','seq_0'..., dimensions={2} | all-to-all | bytes 540672 | tf_op jit(solution)/shard_map/all_to_all | solution.py:154
  78.6 1.1 copy.96
  81.2 0.7 reshape.647
  82.0 9.7 %all-to-all-start.2 = ((bf16[32,2,1024]{2,1,0:T(2,128)(2,1)}), bf16[32,2,1024]{2,1,0:T(2,128)(2,1)S(1)}, u32[]{:S(2)}, u32[]{:S(2)}) async-start(bf16[32,2,1024]{2,1,0:T(2,128)(2,1)} %reshape.647), calls=%async_computation.2 | async-start | bytes 262144 | tf_op jit(solution)/shard_map/all_to_all | solution.py:44
  91.7 15.2 %all-to-all-done.2 = bf16[32,2,1024]{2,1,0:T(2,128)(2,1)S(1)} async-done(((bf16[32,2,1024]{2,1,0:T(2,128)(2,1)}), bf16[32,2,1024]{2,1,0:T(2,128)(2,1)S(1)}, u32[]{:S(2)}, u32[]{:S(2)}) %all-to-all-start.2) | async-done | bytes 131104 | tf_op jit(solution)/shard_map/all_to_all | solution.py:44
  107.5 3.3 %all-to-all-start.4 = ((s32[8,4,8]{2,1,0:T(4,128)}), s32[8,4,8]{2,1,0:T(4,128)S(1)}, u32[]{:S(2)}, u32[]{:S(2)}) async-start(s32[8,4,8]{2,1,0:T(4,128)} %broadcast_in_dim.126), calls=%async_computation.4 | async-start | bytes 32768 | tf_op jit(solution)/shard_map/all_to_all | solution.py:29
  112.7 1.4 reduce.22
  114.8 5.3 %all-to-all-done.4 = s32[8,4,8]{2,1,0:T(4,128)S(1)} async-done(((s32[8,4,8]{2,1,0:T(4,128)}), s32[8,4,8]{2,1,0:T(4,128)S(1)}, u32[]{:S(2)}, u32[]{:S(2)}) %all-to-all-start.4) | async-done | bytes 1056 | tf_op jit(solution)/shard_map/all_to_all | solution.py:29
  120.2 9.6 %all-to-all-start.3 = ((bf16[32,2,1024]{2,1,0:T(2,128)(2,1)}), bf16[32,2,1024]{2,1,0:T(2,128)(2,1)S(1)}, u32[]{:S(2)}, u32[]{:S(2)}) async-start(bf16[32,2,1024]{2,1,0:T(2,128)(2,1)} %reshape.649), calls=%async_computation.3 | async-start | bytes 262144 | tf_op jit(solution)/shard_map/all_to_all | solution.py:29
  130.0 15.1 %all-to-all-done.3 = bf16[32,2,1024]{2,1,0:T(2,128)(2,1)S(1)} async-done(((bf16[32,2,1024]{2,1,0:T(2,128)(2,1)}), bf16[32,2,1024]{2,1,0:T(2,128)(2,1)S(1)}, u32[]{:S(2)}, u32[]{:S(2)}) %all-to-all-start.3) | async-done | bytes 131104 | tf_op jit(solution)/shard_map/all_to_all | solution.py:29
  146.8 23.3 %all_to_all.81 = bf16[16,16,2048]{2,1,0:T(8,128)(2,1)S(1)} all-to-all(bf16[16,16,2048]{2,1,0:T(8,128)(2,1)S(1)} %bitcast.143), channel_id=1, replica_groups=mesh['dp'=8,'seq_0'=2,'seq_1'=2,'expert_0'=4,'expert_1'=4] {'expert_0','..., dimensions={0} | all-to-all | bytes 2097152 | tf_op jit(solution)/shard_map/all_to_all | solution.py:57
  172.2 18.8 %all_to_all.82 = bf16[16,16,2048]{2,1,0:T(8,128)(2,1)S(1)} all-to-all(bf16[16,16,2048]{2,1,0:T(8,128)(2,1)S(1)} %bitcast.145), channel_id=1, replica_groups=mesh['dp'=8,'seq_0'=2,'seq_1'=2,'expert_0'=4,'expert_1'=4] {'expert_0','..., dimensions={0} | all-to-all | bytes 2097152 | tf_op jit(solution)/shard_map/all_to_all | solution.py:57
  193.0 6.3 %all-to-all-start.7 = ((bf16[32,2,1024]{2,1,0:T(2,128)(2,1)}), bf16[32,2,1024]{2,1,0:T(2,128)(2,1)S(1)}, u32[]{:S(2)}, u32[]{:S(2)}) async-start(bf16[32,2,1024]{2,1,0:T(2,128)(2,1)} %reshape.651), calls=%async_computation.7 | async-start | bytes 262144 | tf_op jit(solution)/shard_map/all_to_all | solution.py:44
  199.9 14.6 %all-to-all-done.7 = bf16[32,2,1024]{2,1,0:T(2,128)(2,1)S(1)} async-done(((bf16[32,2,1024]{2,1,0:T(2,128)(2,1)}), bf16[32,2,1024]{2,1,0:T(2,128)(2,1)S(1)}, u32[]{:S(2)}, u32[]{:S(2)}) %all-to-all-start.7) | async-done | bytes 131104 | tf_op jit(solution)/shard_map/all_to_all | solution.py:44
  219.0 1.4 reduce.24
  221.2 4.2 %all-to-all-start.8 = ((bf16[32,2,1024]{2,1,0:T(2,128)(2,1)}), bf16[32,2,1024]{2,1,0:T(2,128)(2,1)S(1)}, u32[]{:S(2)}, u32[]{:S(2)}) async-start(bf16[32,2,1024]{2,1,0:T(2,128)(2,1)} %reshape.653), calls=%async_computation.8 | async-start | bytes 262144 | tf_op jit(solution)/shard_map/all_to_all | solution.py:29
  229.3 11.3 %all-to-all-done.8 = bf16[32,2,1024]{2,1,0:T(2,128)(2,1)S(1)} async-done(((bf16[32,2,1024]{2,1,0:T(2,128)(2,1)}), bf16[32,2,1024]{2,1,0:T(2,128)(2,1)S(1)}, u32[]{:S(2)}, u32[]{:S(2)}) %all-to-all-start.8) | async-done | bytes 131104 | tf_op jit(solution)/shard_map/all_to_all | solution.py:29
  241.7 0.7 reshape.655
  242.4 4.2 %all-to-all-start.9 = ((f32[32,1,288]{2,1,0:T(1,128)}), f32[32,1,288]{2,1,0:T(1,128)S(1)}, u32[]{:S(2)}, u32[]{:S(2)}) async-start(f32[32,1,288]{2,1,0:T(1,128)} %reshape.655), calls=%async_computation.9 | async-start | bytes 98304 | tf_op jit(solution)/shard_map/all_to_all | solution.py:29
  247.6 11.7 %all-to-all-done.9 = f32[32,1,288]{2,1,0:T(1,128)S(1)} async-done(((f32[32,1,288]{2,1,0:T(1,128)}), f32[32,1,288]{2,1,0:T(1,128)S(1)}, u32[]{:S(2)}, u32[]{:S(2)}) %all-to-all-start.9) | async-done | bytes 36896 | tf_op jit(solution)/shard_map/all_to_all | solution.py:29
  259.9 0.8 reduce.25
  263.4 3.5 %all-to-all-start.10 = ((f32[16,1,513]{2,1,0:T(1,128)}), f32[16,1,513]{2,1,0:T(1,128)S(1)}, u32[]{:S(2)}, u32[]{:S(2)}) async-start(f32[16,1,513]{2,1,0:T(1,128)} %all_to_all.64), calls=%async_computation.10 | async-start | bytes 81920 | tf_op jit(solution)/shard_map/all_to_all | solution.py:57
  266.9 2.0 convolution_convert_fusion.1
  269.0 4.5 %all-to-all-done.10 = f32[16,1,513]{2,1,0:T(1,128)S(1)} async-done(((f32[16,1,513]{2,1,0:T(1,128)}), f32[16,1,513]{2,1,0:T(1,128)S(1)}, u32[]{:S(2)}, u32[]{:S(2)}) %all-to-all-start.10) | async-done | bytes 32864 | tf_op jit(solution)/shard_map/all_to_all | solution.py:57
  273.4 3.7 %all-to-all-start.11 = ((bf16[16,16,2048]{2,1,0:T(8,128)(2,1)}), bf16[16,16,2048]{2,1,0:T(8,128)(2,1)S(1)}, u32[]{:S(2)}, u32[]{:S(2)}) async-start(bf16[16,16,2048]{2,1,0:T(8,128)(2,1)} %bitcast.48), calls=%async_computation.11 | async-start | bytes 2097152 | tf_op jit(solution)/shard_map/all_to_all | solution.py:57
  278.3 14.0 %all-to-all-done.11 = bf16[16,16,2048]{2,1,0:T(8,128)(2,1)S(1)} async-done(((bf16[16,16,2048]{2,1,0:T(8,128)(2,1)}), bf16[16,16,2048]{2,1,0:T(8,128)(2,1)S(1)}, u32[]{:S(2)}, u32[]{:S(2)}) %all-to-all-start.11) | async-done | bytes 1048608 | tf_op jit(solution)/shard_map/all_to_all | solution.py:57
  292.3 1.3 fusion
  (128 shorter events, 25.7 us)
Async XLA Ops:
  0.6 171.1 %copy-start = (bf16[1,192,2048]{2,1,0:T(8,128)(2,1)S(1)}, bf16[1,192,2048]{2,1,0:T(8,128)(2,1)}, u32[]{:S(2)}) copy-start(bf16[1,192,2048]{2,1,0:T(8,128)(2,1)} %param.24) | copy-start | bytes 2359300
  1.5 20.8 %copy-start.5 = (bf16[1,128,512]{2,1,0:T(8,128)(2,1)S(1)}, bf16[1,128,512]{2,1,0:T(8,128)(2,1)}, u32[]{:S(2)}) copy-start(bf16[1,128,512]{2,1,0:T(8,128)(2,1)} %param.16) | copy-start | bytes 393220
  2.0 20.4 %copy-start.11 = (s32[1,8]{1,0:T(1,128)S(1)}, s32[1,8]{1,0:T(1,128)}, u32[]{:S(2)}) copy-start(s32[1,8]{1,0:T(1,128)} %param.29) | copy-start | bytes 100
  2.0 20.6 %copy-start.10 = (s32[1,32]{1,0:T(1,128)S(1)}, s32[1,32]{1,0:T(1,128)}, u32[]{:S(2)}) copy-start(s32[1,32]{1,0:T(1,128)} %param.27) | copy-start | bytes 388
  5.6 35.9 %all-to-all-start = ((bf16[32,2,2048]{2,1,0:T(2,128)(2,1)}), bf16[32,2,2048]{2,1,0:T(2,128)(2,1)S(1)}, u32[]{:S(2)}, u32[]{:S(2)}) async-start(bf16[32,2,2048]{2,1,0:T(2,128)(2,1)} %reshape.645), calls=%async_computation | async-start | bytes 524288 | tf_op jit(solution)/shard_map/all_to_all | solution.py:29
  22.8 19.3 %copy-start.4 = (bf16[1,128,512]{2,1,0:T(8,128)(2,1)S(1)}, bf16[1,128,512]{2,1,0:T(8,128)(2,1)}, u32[]{:S(2)}) copy-start(bf16[1,128,512]{2,1,0:T(8,128)(2,1)} %param.15) | copy-start | bytes 393220
  78.6 1.7 copy-start.2
  79.8 11.9 %copy-start.7 = (bf16[1,1,2048]{2,1,0:T(2,128)(2,1)S(1)}, bf16[1,1,2048]{2,1,0:T(2,128)(2,1)}, u32[]{:S(2)}) copy-start(bf16[1,1,2048]{2,1,0:T(2,128)(2,1)} %param.18) | copy-start | bytes 12292
  79.8 27.1 %copy-start.9 = (s32[1,4,8]{2,1,0:T(4,128)S(1)}, s32[1,4,8]{2,1,0:T(4,128)}, u32[]{:S(2)}) copy-start(s32[1,4,8]{2,1,0:T(4,128)} %param.26) | copy-start | bytes 388
  80.3 32.2 %copy-start.8 = (bf16[2048]{0:T(1024)(128)(2,1)S(1)}, bf16[2048]{0:T(1024)(128)(2,1)}, u32[]{:S(2)}) copy-start(bf16[2048]{0:T(1024)(128)(2,1)} %param.20) | copy-start | bytes 12292
  82.0 25.0 %all-to-all-start.2 = ((bf16[32,2,1024]{2,1,0:T(2,128)(2,1)}), bf16[32,2,1024]{2,1,0:T(2,128)(2,1)S(1)}, u32[]{:S(2)}, u32[]{:S(2)}) async-start(bf16[32,2,1024]{2,1,0:T(2,128)(2,1)} %reshape.647), calls=%async_computation.2 | async-start | bytes 262144 | tf_op jit(solution)/shard_map/all_to_all | solution.py:44
  107.5 12.6 %all-to-all-start.4 = ((s32[8,4,8]{2,1,0:T(4,128)}), s32[8,4,8]{2,1,0:T(4,128)S(1)}, u32[]{:S(2)}, u32[]{:S(2)}) async-start(s32[8,4,8]{2,1,0:T(4,128)} %broadcast_in_dim.126), calls=%async_computation.4 | async-start | bytes 32768 | tf_op jit(solution)/shard_map/all_to_all | solution.py:29
  111.0 34.1 %copy-start.3 = (bf16[2048,128]{1,0:T(8,128)(2,1)S(1)}, bf16[2048,128]{1,0:T(8,128)(2,1)}, u32[]{:S(2)}) copy-start(bf16[2048,128]{1,0:T(8,128)(2,1)} %param.21) | copy-start | bytes 1572868
  120.2 24.8 %all-to-all-start.3 = ((bf16[32,2,1024]{2,1,0:T(2,128)(2,1)}), bf16[32,2,1024]{2,1,0:T(2,128)(2,1)S(1)}, u32[]{:S(2)}, u32[]{:S(2)}) async-start(bf16[32,2,1024]{2,1,0:T(2,128)(2,1)} %reshape.649), calls=%async_computation.3 | async-start | bytes 262144 | tf_op jit(solution)/shard_map/all_to_all | solution.py:29
  146.8 23.3 %copy-start.1 = (bf16[1,2048,192]{1,2,0:T(8,128)(2,1)S(1)}, bf16[1,2048,192]{1,2,0:T(8,128)(2,1)}, u32[]{:S(2)}) copy-start(bf16[1,2048,192]{1,2,0:T(8,128)(2,1)} %param.22) | copy-start | bytes 2359300
  170.0 1.1 copy-start.12
  191.0 25.3 %copy-start.6 = (bf16[2048]{0:T(1024)(128)(2,1)S(1)}, bf16[2048]{0:T(1024)(128)(2,1)}, u32[]{:S(2)}) copy-start(bf16[2048]{0:T(1024)(128)(2,1)} %param.25) | copy-start | bytes 12292
  193.0 21.6 %all-to-all-start.7 = ((bf16[32,2,1024]{2,1,0:T(2,128)(2,1)}), bf16[32,2,1024]{2,1,0:T(2,128)(2,1)S(1)}, u32[]{:S(2)}, u32[]{:S(2)}) async-start(bf16[32,2,1024]{2,1,0:T(2,128)(2,1)} %reshape.651), calls=%async_computation.7 | async-start | bytes 262144 | tf_op jit(solution)/shard_map/all_to_all | solution.py:44
  221.2 19.5 %all-to-all-start.8 = ((bf16[32,2,1024]{2,1,0:T(2,128)(2,1)}), bf16[32,2,1024]{2,1,0:T(2,128)(2,1)S(1)}, u32[]{:S(2)}, u32[]{:S(2)}) async-start(bf16[32,2,1024]{2,1,0:T(2,128)(2,1)} %reshape.653), calls=%async_computation.8 | async-start | bytes 262144 | tf_op jit(solution)/shard_map/all_to_all | solution.py:29
  242.4 16.9 %all-to-all-start.9 = ((f32[32,1,288]{2,1,0:T(1,128)}), f32[32,1,288]{2,1,0:T(1,128)S(1)}, u32[]{:S(2)}, u32[]{:S(2)}) async-start(f32[32,1,288]{2,1,0:T(1,128)} %reshape.655), calls=%async_computation.9 | async-start | bytes 98304 | tf_op jit(solution)/shard_map/all_to_all | solution.py:29
  263.4 10.0 %all-to-all-start.10 = ((f32[16,1,513]{2,1,0:T(1,128)}), f32[16,1,513]{2,1,0:T(1,128)S(1)}, u32[]{:S(2)}, u32[]{:S(2)}) async-start(f32[16,1,513]{2,1,0:T(1,128)} %all_to_all.64), calls=%async_computation.10 | async-start | bytes 81920 | tf_op jit(solution)/shard_map/all_to_all | solution.py:57
  273.4 18.9 %all-to-all-start.11 = ((bf16[16,16,2048]{2,1,0:T(8,128)(2,1)}), bf16[16,16,2048]{2,1,0:T(8,128)(2,1)S(1)}, u32[]{:S(2)}, u32[]{:S(2)}) async-start(bf16[16,16,2048]{2,1,0:T(8,128)(2,1)} %bitcast.48), calls=%async_computation.11 | async-start | bytes 2097152 | tf_op jit(solution)/shard_map/all_to_all | solution.py:57

commit v4 on v3

--- a/solution.py
+++ b/solution.py
@@ -97,10 +97,21 @@
     labels,
     trace_len,
 ):
-    pack_routes = gather_directly(routes[0], "dp", 0)
     count_of_keys = keys.shape[1]
     query_groups = QUERY_HEADS // KEY_VALUE_HEADS
-    query_all = gather_directly(queries, DP_SEQ, 1)[0]
+    query_width = queries.shape[2]
+    own_routes = lax.dynamic_index_in_dim(routes[0], lax.axis_index(SEQ), 0, keepdims=False)
+    query_row = jnp.concatenate(
+        [
+            queries[0],
+            own_routes.astype(jnp.bfloat16)[None, :],
+            jnp.zeros((1, HEAD_WIDTH - own_routes.shape[0]), jnp.bfloat16),
+        ],
+        axis=1,
+    )
+    query_rows = gather_directly(query_row, DP_SEQ, 0)
+    query_all = query_rows[:, :query_width]
+    pack_routes = query_rows[:, query_width : query_width + routes.shape[2]].astype(jnp.int32)
     positions = step_pos[0]
     number_of_steps = positions.shape[0]
     lengths = trace_len[0]
@@ -225,11 +236,6 @@
     d_out = lax.dot_general(
         weight_map, pack_grads.astype(jnp.float32), contract_rows, precision=lax.Precision.HIGHEST
     ).astype(jnp.bfloat16)
-    grads_arrived = across_group(d_out.reshape(group_size, per_source, width)).reshape(slots, width)
-    grad_down = lax.dot_general(
-        hidden, grads_arrived, contract_rows, preferred_element_type=jnp.float32
-    )
-    grad_down = grad_down.astype(jnp.bfloat16).reshape((1,) + grad_down.shape)
     slot_grads = lax.dot_general(
         row_map.astype(jnp.bfloat16), pack_grads, contract_rows, preferred_element_type=jnp.float32
     )
@@ -249,12 +255,31 @@
     )
     router_part = router_part.reshape(group_size, -1)
     chunk = router_part.shape[1]
+    router_hi, router_lo = split_pair(router_part)
+    loss_hi, loss_lo = split_pair(pack_loss)
+    extra_row = jnp.concatenate(
+        [
+            router_hi,
+            router_lo,
+            jnp.broadcast_to(loss_hi, (group_size, 1)),
+            jnp.broadcast_to(loss_lo, (group_size, 1)),
+            jnp.zeros((group_size, width - 2 * chunk - 2), jnp.bfloat16),
+        ],
+        axis=1,
+    )
     sent = jnp.concatenate(
-        [router_part, jnp.broadcast_to(pack_loss, (group_size, 1))], axis=1
+        [d_out.reshape(group_size, per_source, width), extra_row[:, None, :]], axis=1
     )
     got = across_group(sent)
-    grad_router = jnp.sum(got[:, :chunk], axis=0).reshape(-1, experts).astype(jnp.bfloat16)
-    loss = jnp.sum(got[:, chunk])
+    grads_arrived = got[:, :per_source].reshape(slots, width)
+    grad_down = lax.dot_general(
+        hidden, grads_arrived, contract_rows, preferred_element_type=jnp.float32
+    )
+    grad_down = grad_down.astype(jnp.bfloat16).reshape((1,) + grad_down.shape)
+    tail = got[:, per_source]
+    grad_router = jnp.sum(join_pair(tail[:, :chunk], tail[:, chunk : 2 * chunk]), axis=0)
+    grad_router = grad_router.reshape(-1, experts).astype(jnp.bfloat16)
+    loss = jnp.sum(join_pair(tail[:, 2 * chunk], tail[:, 2 * chunk + 1]))
     return (loss, grad_down, grad_router)
 
 

time: 295 us -> 278 us (0.942)
  blocking collectives: 74.3 us -> 99.3 us
  waiting for transfers between devices: 110 us -> 86 us
  starting transfers between devices: 61.1 us -> 45.4 us
    all_to_all x2 -> x3, blocking collectives: 42.1 us -> 66.8 us  [across_group(): lax.all_to_all(buffer, EXPERT, split_axis=0, concat_axis=0, tiled=True)]
    all_to_all x2 -> x0, waiting for transfers between devices: 18.5 us -> none  [across_group(): lax.all_to_all(buffer, EXPERT, split_axis=0, concat_axis=0, tiled=True)]
    all_to_all x5 -> x4, starting transfers between devices: 38 us -> 29.4 us  [from_everyone(): return lax.all_to_all(copies, axis, split_axis=0, concat_axis=0, tiled=True)]
    all_to_all x2 -> x0, starting transfers between devices: 7.16 us -> none  [across_group(): lax.all_to_all(buffer, EXPERT, split_axis=0, concat_axis=0, tiled=True)]
    all_to_all x5 -> x4, waiting for transfers between devices: 62 us -> 56.1 us  [from_everyone(): return lax.all_to_all(copies, axis, split_axis=0, concat_axis=0, tiled=True)]
    unnamed x42 -> x40, local copies, waits for them, and re-layouts: 6.41 us -> 5.64 us
  transfers between devices with their start and end apart: 9 -> 6, of which waited for: 9 -> 6; matrix products, arithmetic and copies ran while one was open for 3% -> 1% of each run, Pallas kernels for 0% -> 0%
where the time goes in v4:
time: 278 us; the launch traced here: 277 us
  blocking collectives  99.3 us (36%)
  waiting for transfers between devices  86 us (31%)
  starting transfers between devices  45.4 us (16%)
  other arithmetic  17.2 us (6%)
  local copies, waits for them, and re-layouts  12.5 us (4%)
  between operations  10.1 us (4%)
  matrix products  7 us (3%)
    all_to_all x3, blocking collectives, across_group(): lax.all_to_all(buffer, EXPERT, split_axis=0, concat_axis=0, tiled=True)  66.8 us
    all_to_all x4, waiting for transfers between devices, from_everyone(): return lax.all_to_all(copies, axis, split_axis=0, concat_axis=0, tiled=True)  56.1 us
    all_to_all x1, blocking collectives, shards(): lax.all_to_all(packed.reshape(1, *packed.shape), DP_SEQ, split_axis=2, co...  32.5 us
    all_to_all x2, waiting for transfers between devices, sent_and_summed(): lax.all_to_all(in_blocks(array, dim, count), axis, 0, 0, tiled=True)  29.9 us
    all_to_all x4, starting transfers between devices, from_everyone(): return lax.all_to_all(copies, axis, split_axis=0, concat_axis=0, tiled=True)  29.4 us
    all_to_all x2, starting transfers between devices, sent_and_summed(): lax.all_to_all(in_blocks(array, dim, count), axis, 0, 0, tiled=True)  16 us
    unnamed x40, local copies, waits for them, and re-layouts  5.64 us
  transfers between devices with their start and end apart: 6, of which 6 were waited for; matrix products, arithmetic and copies ran while one was open for 1% of the time, Pallas kernels for 0%

profile of v4, /device:TPU:1, one launch (start us, length us, event | category | flops | bytes accessed | tf_op | source)
XLA Modules:
  0.0 277.5 jit_solution(5178849851113183875)
XLA Ops:
  0.7 0.8 convert_bitcast_fusion.1
  1.5 0.8 concatenate.17
  3.1 2.2 reduce.20
  5.4 0.9 reshape.596
  6.3 16.9 %all-to-all-start = ((bf16[32,2,2112]{2,1,0:T(2,128)(2,1)}), bf16[32,2,2112]{2,1,0:T(2,128)(2,1)S(1)}, u32[]{:S(2)}, u32[]{:S(2)}) async-start(bf16[32,2,2112]{2,1,0:T(2,128)(2,1)} %reshape.596), calls=%async_computation | async-start | bytes 557056 | tf_op jit(solution)/shard_map/all_to_all | solution.py:29
  23.7 19.1 %all-to-all-done = bf16[32,2,2112]{2,1,0:T(2,128)(2,1)S(1)} async-done(((bf16[32,2,2112]{2,1,0:T(2,128)(2,1)}), bf16[32,2,2112]{2,1,0:T(2,128)(2,1)S(1)}, u32[]{:S(2)}, u32[]{:S(2)}) %all-to-all-start) | async-done | bytes 270368 | tf_op jit(solution)/shard_map/all_to_all | solution.py:29
  47.4 32.5 %all_to_all.63 = bf16[1,32,32,132]{3,1,0,2:T(8,128)(2,1)S(1)} all-to-all(bf16[1,32,32,132]{3,1,0,2:T(8,128)(2,1)S(1)} %copy.102), channel_id=1, replica_groups=mesh['dp'=8,'seq_0'=2,'seq_1'=2,'expert_0'=4,'expert_1'=4] {'dp','seq_0'..., dimensions={2} | all-to-all | bytes 540672 | tf_op jit(solution)/shard_map/all_to_all | solution.py:165
  79.9 1.1 copy.103
  81.9 0.7 reduce.21
  82.6 0.7 reshape.598
  83.4 9.7 %all-to-all-start.2 = ((bf16[32,2,1024]{2,1,0:T(2,128)(2,1)}), bf16[32,2,1024]{2,1,0:T(2,128)(2,1)S(1)}, u32[]{:S(2)}, u32[]{:S(2)}) async-start(bf16[32,2,1024]{2,1,0:T(2,128)(2,1)} %reshape.598), calls=%async_computation.2 | async-start | bytes 262144 | tf_op jit(solution)/shard_map/all_to_all | solution.py:44
  93.1 15.2 %all-to-all-done.2 = bf16[32,2,1024]{2,1,0:T(2,128)(2,1)S(1)} async-done(((bf16[32,2,1024]{2,1,0:T(2,128)(2,1)}), bf16[32,2,1024]{2,1,0:T(2,128)(2,1)S(1)}, u32[]{:S(2)}, u32[]{:S(2)}) %all-to-all-start.2) | async-done | bytes 131104 | tf_op jit(solution)/shard_map/all_to_all | solution.py:44
  110.1 1.4 reduce.22
  111.5 0.7 reshape.600
  112.3 4.2 %all-to-all-start.3 = ((bf16[32,2,1024]{2,1,0:T(2,128)(2,1)}), bf16[32,2,1024]{2,1,0:T(2,128)(2,1)S(1)}, u32[]{:S(2)}, u32[]{:S(2)}) async-start(bf16[32,2,1024]{2,1,0:T(2,128)(2,1)} %reshape.600), calls=%async_computation.3 | async-start | bytes 262144 | tf_op jit(solution)/shard_map/all_to_all | solution.py:29
  116.7 15.1 %all-to-all-done.3 = bf16[32,2,1024]{2,1,0:T(2,128)(2,1)S(1)} async-done(((bf16[32,2,1024]{2,1,0:T(2,128)(2,1)}), bf16[32,2,1024]{2,1,0:T(2,128)(2,1)S(1)}, u32[]{:S(2)}, u32[]{:S(2)}) %all-to-all-start.3) | async-done | bytes 131104 | tf_op jit(solution)/shard_map/all_to_all | solution.py:29
  133.5 23.3 %all_to_all.64 = bf16[16,16,2048]{2,1,0:T(8,128)(2,1)S(1)} all-to-all(bf16[16,16,2048]{2,1,0:T(8,128)(2,1)S(1)} %bitcast.146), channel_id=1, replica_groups=mesh['dp'=8,'seq_0'=2,'seq_1'=2,'expert_0'=4,'expert_1'=4] {'expert_0','..., dimensions={0} | all-to-all | bytes 2097152 | tf_op jit(solution)/shard_map/all_to_all | solution.py:57
  158.3 18.8 %all_to_all.65 = bf16[16,16,2048]{2,1,0:T(8,128)(2,1)S(1)} all-to-all(bf16[16,16,2048]{2,1,0:T(8,128)(2,1)S(1)} %bitcast.148), channel_id=1, replica_groups=mesh['dp'=8,'seq_0'=2,'seq_1'=2,'expert_0'=4,'expert_1'=4] {'expert_0','..., dimensions={0} | all-to-all | bytes 2097152 | tf_op jit(solution)/shard_map/all_to_all | solution.py:57
  178.4 0.7 reshape.602
  179.1 6.3 %all-to-all-start.6 = ((bf16[32,2,1024]{2,1,0:T(2,128)(2,1)}), bf16[32,2,1024]{2,1,0:T(2,128)(2,1)S(1)}, u32[]{:S(2)}, u32[]{:S(2)}) async-start(bf16[32,2,1024]{2,1,0:T(2,128)(2,1)} %reshape.602), calls=%async_computation.6 | async-start | bytes 262144 | tf_op jit(solution)/shard_map/all_to_all | solution.py:44
  186.0 14.6 %all-to-all-done.6 = bf16[32,2,1024]{2,1,0:T(2,128)(2,1)S(1)} async-done(((bf16[32,2,1024]{2,1,0:T(2,128)(2,1)}), bf16[32,2,1024]{2,1,0:T(2,128)(2,1)S(1)}, u32[]{:S(2)}, u32[]{:S(2)}) %all-to-all-start.6) | async-done | bytes 131104 | tf_op jit(solution)/shard_map/all_to_all | solution.py:44
  205.1 1.4 reduce.24
  206.5 0.7 reshape.604
  207.3 4.2 %all-to-all-start.7 = ((bf16[32,2,1024]{2,1,0:T(2,128)(2,1)}), bf16[32,2,1024]{2,1,0:T(2,128)(2,1)S(1)}, u32[]{:S(2)}, u32[]{:S(2)}) async-start(bf16[32,2,1024]{2,1,0:T(2,128)(2,1)} %reshape.604), calls=%async_computation.7 | async-start | bytes 262144 | tf_op jit(solution)/shard_map/all_to_all | solution.py:29
  216.4 10.3 %all-to-all-done.7 = bf16[32,2,1024]{2,1,0:T(2,128)(2,1)S(1)} async-done(((bf16[32,2,1024]{2,1,0:T(2,128)(2,1)}), bf16[32,2,1024]{2,1,0:T(2,128)(2,1)S(1)}, u32[]{:S(2)}, u32[]{:S(2)}) %all-to-all-start.7) | async-done | bytes 131104 | tf_op jit(solution)/shard_map/all_to_all | solution.py:29
  227.8 0.7 reshape.606
  228.5 4.2 %all-to-all-start.8 = ((f32[32,1,288]{2,1,0:T(1,128)}), f32[32,1,288]{2,1,0:T(1,128)S(1)}, u32[]{:S(2)}, u32[]{:S(2)}) async-start(f32[32,1,288]{2,1,0:T(1,128)} %reshape.606), calls=%async_computation.8 | async-start | bytes 98304 | tf_op jit(solution)/shard_map/all_to_all | solution.py:29
  232.7 1.0 convolution_convert_fusion.1
  233.7 11.7 %all-to-all-done.8 = f32[32,1,288]{2,1,0:T(1,128)S(1)} async-done(((f32[32,1,288]{2,1,0:T(1,128)}), f32[32,1,288]{2,1,0:T(1,128)S(1)}, u32[]{:S(2)}, u32[]{:S(2)}) %all-to-all-start.8) | async-done | bytes 36896 | tf_op jit(solution)/shard_map/all_to_all | solution.py:29
  245.9 0.8 reduce.25
  250.0 24.7 %all_to_all.66 = bf16[16,17,2048]{2,1,0:T(8,128)(2,1)S(1)} all-to-all(bf16[16,17,2048]{2,1,0:T(8,128)(2,1)S(1)} %pad_maximum_fusion), channel_id=1, replica_groups=mesh['dp'=8,'seq_0'=2,'seq_1'=2,'expert_0'=4,'expert_1'=4] {'expert_0','..., dimensions={0} | all-to-all | bytes 2228224 | tf_op jit(solution)/shard_map/all_to_all | solution.py:57
  276.2 1.3 fusion
  (131 shorter events, 20.7 us)
Async XLA Ops:
  0.6 157.1 %copy-start = (bf16[1,192,2048]{2,1,0:T(8,128)(2,1)S(1)}, bf16[1,192,2048]{2,1,0:T(8,128)(2,1)}, u32[]{:S(2)}) copy-start(bf16[1,192,2048]{2,1,0:T(8,128)(2,1)} %param.24) | copy-start | bytes 2359300
  0.6 22.5 %copy-start.10 = (s32[1,8]{1,0:T(1,128)S(1)}, s32[1,8]{1,0:T(1,128)}, u32[]{:S(2)}) copy-start(s32[1,8]{1,0:T(1,128)} %param.29) | copy-start | bytes 100
  0.7 22.7 %copy-start.5 = (bf16[1,128,512]{2,1,0:T(8,128)(2,1)S(1)}, bf16[1,128,512]{2,1,0:T(8,128)(2,1)}, u32[]{:S(2)}) copy-start(bf16[1,128,512]{2,1,0:T(8,128)(2,1)} %param.16) | copy-start | bytes 393220
  0.7 22.8 %copy-start.9 = (s32[1,32]{1,0:T(1,128)S(1)}, s32[1,32]{1,0:T(1,128)}, u32[]{:S(2)}) copy-start(s32[1,32]{1,0:T(1,128)} %param.27) | copy-start | bytes 388
  6.3 36.9 %copy-start.4 = (bf16[1,128,512]{2,1,0:T(8,128)(2,1)S(1)}, bf16[1,128,512]{2,1,0:T(8,128)(2,1)}, u32[]{:S(2)}) copy-start(bf16[1,128,512]{2,1,0:T(8,128)(2,1)} %param.15) | copy-start | bytes 393220
  6.3 36.5 %all-to-all-start = ((bf16[32,2,2112]{2,1,0:T(2,128)(2,1)}), bf16[32,2,2112]{2,1,0:T(2,128)(2,1)S(1)}, u32[]{:S(2)}, u32[]{:S(2)}) async-start(bf16[32,2,2112]{2,1,0:T(2,128)(2,1)} %reshape.596), calls=%async_computation | async-start | bytes 557056 | tf_op jit(solution)/shard_map/all_to_all | solution.py:29
  79.9 1.7 copy-start.2
  81.1 12.0 %copy-start.7 = (bf16[1,1,2048]{2,1,0:T(2,128)(2,1)S(1)}, bf16[1,1,2048]{2,1,0:T(2,128)(2,1)}, u32[]{:S(2)}) copy-start(bf16[1,1,2048]{2,1,0:T(2,128)(2,1)} %param.18) | copy-start | bytes 12292
  81.1 28.8 %copy-start.8 = (bf16[2048]{0:T(1024)(128)(2,1)S(1)}, bf16[2048]{0:T(1024)(128)(2,1)}, u32[]{:S(2)}) copy-start(bf16[2048]{0:T(1024)(128)(2,1)} %param.20) | copy-start | bytes 12292
  81.9 49.9 %copy-start.3 = (bf16[2048,128]{1,0:T(8,128)(2,1)S(1)}, bf16[2048,128]{1,0:T(8,128)(2,1)}, u32[]{:S(2)}) copy-start(bf16[2048,128]{1,0:T(8,128)(2,1)} %param.21) | copy-start | bytes 1572868
  83.4 25.0 %all-to-all-start.2 = ((bf16[32,2,1024]{2,1,0:T(2,128)(2,1)}), bf16[32,2,1024]{2,1,0:T(2,128)(2,1)S(1)}, u32[]{:S(2)}, u32[]{:S(2)}) async-start(bf16[32,2,1024]{2,1,0:T(2,128)(2,1)} %reshape.598), calls=%async_computation.2 | async-start | bytes 262144 | tf_op jit(solution)/shard_map/all_to_all | solution.py:44
  112.3 19.5 %all-to-all-start.3 = ((bf16[32,2,1024]{2,1,0:T(2,128)(2,1)}), bf16[32,2,1024]{2,1,0:T(2,128)(2,1)S(1)}, u32[]{:S(2)}, u32[]{:S(2)}) async-start(bf16[32,2,1024]{2,1,0:T(2,128)(2,1)} %reshape.600), calls=%async_computation.3 | async-start | bytes 262144 | tf_op jit(solution)/shard_map/all_to_all | solution.py:29
  133.0 23.7 %copy-start.1 = (bf16[1,2048,192]{1,2,0:T(8,128)(2,1)S(1)}, bf16[1,2048,192]{1,2,0:T(8,128)(2,1)}, u32[]{:S(2)}) copy-start(bf16[1,2048,192]{1,2,0:T(8,128)(2,1)} %param.22) | copy-start | bytes 2359300
  133.5 23.8 %copy-start.11 = (bf16[1,2048,192]{1,2,0:T(8,128)(2,1)S(1)}, bf16[1,2048,192]{1,2,0:T(8,128)(2,1)}, u32[]{:S(2)}) copy-start(bf16[1,2048,192]{1,2,0:T(8,128)(2,1)} %param.23) | copy-start | bytes 2359300
  177.1 25.3 %copy-start.6 = (bf16[2048]{0:T(1024)(128)(2,1)S(1)}, bf16[2048]{0:T(1024)(128)(2,1)}, u32[]{:S(2)}) copy-start(bf16[2048]{0:T(1024)(128)(2,1)} %param.25) | copy-start | bytes 12292
  179.1 21.6 %all-to-all-start.6 = ((bf16[32,2,1024]{2,1,0:T(2,128)(2,1)}), bf16[32,2,1024]{2,1,0:T(2,128)(2,1)S(1)}, u32[]{:S(2)}, u32[]{:S(2)}) async-start(bf16[32,2,1024]{2,1,0:T(2,128)(2,1)} %reshape.602), calls=%async_computation.6 | async-start | bytes 262144 | tf_op jit(solution)/shard_map/all_to_all | solution.py:44
  207.3 19.4 %all-to-all-start.7 = ((bf16[32,2,1024]{2,1,0:T(2,128)(2,1)}), bf16[32,2,1024]{2,1,0:T(2,128)(2,1)S(1)}, u32[]{:S(2)}, u32[]{:S(2)}) async-start(bf16[32,2,1024]{2,1,0:T(2,128)(2,1)} %reshape.604), calls=%async_computation.7 | async-start | bytes 262144 | tf_op jit(solution)/shard_map/all_to_all | solution.py:29
  228.5 16.9 %all-to-all-start.8 = ((f32[32,1,288]{2,1,0:T(1,128)}), f32[32,1,288]{2,1,0:T(1,128)S(1)}, u32[]{:S(2)}, u32[]{:S(2)}) async-start(f32[32,1,288]{2,1,0:T(1,128)} %reshape.606), calls=%async_computation.8 | async-start | bytes 98304 | tf_op jit(solution)/shard_map/all_to_all | solution.py:29

commit v5 on v4

--- a/solution.py
+++ b/solution.py
@@ -152,23 +152,17 @@
     ).reshape(number_of_steps, QUERY_HEADS, HEAD_WIDTH)
     totals_hi, totals_lo = split_pair(totals)
     peak_hi, peak_lo = split_pair(local_peak)
-    packed = jnp.concatenate(
-        [
-            weighted.astype(jnp.bfloat16),
-            totals_hi[..., None],
-            totals_lo[..., None],
-            peak_hi[..., None],
-            peak_lo[..., None],
-        ],
-        axis=-1,
-    )
+    stats = jnp.stack([totals_hi, totals_lo, peak_hi, peak_lo], axis=-1)
+    stats = jnp.swapaxes(stats, 0, 1).reshape(1, QUERY_HEADS, -1)
+    packed = jnp.concatenate([weighted.astype(jnp.bfloat16), stats], axis=0)
     arrived = lax.all_to_all(
         packed.reshape(1, *packed.shape), DP_SEQ, split_axis=2, concat_axis=0, tiled=True
     )
+    got_stats = arrived[:, number_of_steps].reshape(arrived.shape[0], number_of_steps, 1, 4)
     attn = merge_heads(
-        arrived[..., :HEAD_WIDTH].astype(jnp.float32),
-        join_pair(arrived[..., HEAD_WIDTH], arrived[..., HEAD_WIDTH + 1]),
-        join_pair(arrived[..., HEAD_WIDTH + 2], arrived[..., HEAD_WIDTH + 3]),
+        arrived[:, :number_of_steps].astype(jnp.float32),
+        join_pair(got_stats[..., 0], got_stats[..., 1]),
+        join_pair(got_stats[..., 2], got_stats[..., 3]),
     )
     mixed = sent_and_summed(
         jnp.dot(attn, out_proj, preferred_element_type=jnp.float32).astype(jnp.bfloat16), DP_SEQ, 0

time: 278 us -> 269 us (0.968)
  blocking collectives: 99.3 us -> 93.6 us
    all_to_all x1, blocking collectives: 32.5 us -> 26.8 us  [shards(): lax.all_to_all(packed.reshape(1, *packed.shape), DP_SEQ, split_axis=2, co...]
    unnamed x40 -> x42, local copies, waits for them, and re-layouts: 5.64 us -> 5.81 us
where the time goes in v5:
time: 269 us; the launch traced here: 268 us
  blocking collectives  93.6 us (35%)
  waiting for transfers between devices  86 us (32%)
  starting transfers between devices  42.7 us (16%)
  other arithmetic  18 us (7%)
  local copies, waits for them, and re-layouts  10.3 us (4%)
  between operations  10.1 us (4%)
  matrix products  7.03 us (3%)
    all_to_all x3, blocking collectives, across_group(): lax.all_to_all(buffer, EXPERT, split_axis=0, concat_axis=0, tiled=True)  66.8 us
    all_to_all x4, waiting for transfers between devices, from_everyone(): return lax.all_to_all(copies, axis, split_axis=0, concat_axis=0, tiled=True)  56.1 us
    all_to_all x2, waiting for transfers between devices, sent_and_summed(): lax.all_to_all(in_blocks(array, dim, count), axis, 0, 0, tiled=True)  29.9 us
    all_to_all x4, starting transfers between devices, from_everyone(): return lax.all_to_all(copies, axis, split_axis=0, concat_axis=0, tiled=True)  29.4 us
    all_to_all x1, blocking collectives, shards(): lax.all_to_all(packed.reshape(1, *packed.shape), DP_SEQ, split_axis=2, co...  26.8 us
    all_to_all x2, starting transfers between devices, sent_and_summed(): lax.all_to_all(in_blocks(array, dim, count), axis, 0, 0, tiled=True)  13.3 us
    unnamed x42, local copies, waits for them, and re-layouts  5.81 us
  transfers between devices with their start and end apart: 6, of which 6 were waited for; matrix products, arithmetic and copies ran while one was open for 1% of the time, Pallas kernels for 0%

profile of v5, /device:TPU:1, one launch (start us, length us, event | category | flops | bytes accessed | tf_op | source)
XLA Modules:
  0.0 267.7 jit_solution(12907198798185655852)
XLA Ops:
  0.7 0.8 convert_bitcast_fusion.1
  1.5 0.8 concatenate.17
  3.1 2.2 reduce.20
  5.4 0.9 reshape.600
  6.3 16.9 %all-to-all-start = ((bf16[32,2,2112]{2,1,0:T(2,128)(2,1)}), bf16[32,2,2112]{2,1,0:T(2,128)(2,1)S(1)}, u32[]{:S(2)}, u32[]{:S(2)}) async-start(bf16[32,2,2112]{2,1,0:T(2,128)(2,1)} %reshape.600), calls=%async_computation | async-start | bytes 557056 | tf_op jit(solution)/shard_map/all_to_all | solution.py:29
  23.7 19.1 %all-to-all-done = bf16[32,2,2112]{2,1,0:T(2,128)(2,1)S(1)} async-done(((bf16[32,2,2112]{2,1,0:T(2,128)(2,1)}), bf16[32,2,2112]{2,1,0:T(2,128)(2,1)S(1)}, u32[]{:S(2)}, u32[]{:S(2)}) %all-to-all-start) | async-done | bytes 270368 | tf_op jit(solution)/shard_map/all_to_all | solution.py:29
  45.6 26.8 %all_to_all.63 = bf16[1,33,32,128]{3,1,0,2:T(8,128)(2,1)S(1)} all-to-all(bf16[1,33,32,128]{3,1,0,2:T(8,128)(2,1)S(1)} %copy.93), channel_id=1, replica_groups=mesh['dp'=8,'seq_0'=2,'seq_1'=2,'expert_0'=4,'expert_1'=4] {'dp','seq_0'..., dimensions={2} | all-to-all | bytes 540672 | tf_op jit(solution)/shard_map/all_to_all | solution.py:158
  74.8 0.7 reduce.21
  75.5 0.7 reshape.602
  76.3 7.0 %all-to-all-start.2 = ((bf16[32,2,1024]{2,1,0:T(2,128)(2,1)}), bf16[32,2,1024]{2,1,0:T(2,128)(2,1)S(1)}, u32[]{:S(2)}, u32[]{:S(2)}) async-start(bf16[32,2,1024]{2,1,0:T(2,128)(2,1)} %reshape.602), calls=%async_computation.2 | async-start | bytes 262144 | tf_op jit(solution)/shard_map/all_to_all | solution.py:44
  83.3 15.2 %all-to-all-done.2 = bf16[32,2,1024]{2,1,0:T(2,128)(2,1)S(1)} async-done(((bf16[32,2,1024]{2,1,0:T(2,128)(2,1)}), bf16[32,2,1024]{2,1,0:T(2,128)(2,1)S(1)}, u32[]{:S(2)}, u32[]{:S(2)}) %all-to-all-start.2) | async-done | bytes 131104 | tf_op jit(solution)/shard_map/all_to_all | solution.py:44
  100.3 1.4 reduce.22
  101.7 0.7 reshape.604
  102.5 4.2 %all-to-all-start.3 = ((bf16[32,2,1024]{2,1,0:T(2,128)(2,1)}), bf16[32,2,1024]{2,1,0:T(2,128)(2,1)S(1)}, u32[]{:S(2)}, u32[]{:S(2)}) async-start(bf16[32,2,1024]{2,1,0:T(2,128)(2,1)} %reshape.604), calls=%async_computation.3 | async-start | bytes 262144 | tf_op jit(solution)/shard_map/all_to_all | solution.py:29
  106.9 15.1 %all-to-all-done.3 = bf16[32,2,1024]{2,1,0:T(2,128)(2,1)S(1)} async-done(((bf16[32,2,1024]{2,1,0:T(2,128)(2,1)}), bf16[32,2,1024]{2,1,0:T(2,128)(2,1)S(1)}, u32[]{:S(2)}, u32[]{:S(2)}) %all-to-all-start.3) | async-done | bytes 131104 | tf_op jit(solution)/shard_map/all_to_all | solution.py:29
  123.7 23.3 %all_to_all.64 = bf16[16,16,2048]{2,1,0:T(8,128)(2,1)S(1)} all-to-all(bf16[16,16,2048]{2,1,0:T(8,128)(2,1)S(1)} %bitcast.151), channel_id=1, replica_groups=mesh['dp'=8,'seq_0'=2,'seq_1'=2,'expert_0'=4,'expert_1'=4] {'expert_0','..., dimensions={0} | all-to-all | bytes 2097152 | tf_op jit(solution)/shard_map/all_to_all | solution.py:57
  148.4 18.8 %all_to_all.65 = bf16[16,16,2048]{2,1,0:T(8,128)(2,1)S(1)} all-to-all(bf16[16,16,2048]{2,1,0:T(8,128)(2,1)S(1)} %bitcast.153), channel_id=1, replica_groups=mesh['dp'=8,'seq_0'=2,'seq_1'=2,'expert_0'=4,'expert_1'=4] {'expert_0','..., dimensions={0} | all-to-all | bytes 2097152 | tf_op jit(solution)/shard_map/all_to_all | solution.py:57
  168.6 0.7 reshape.606
  169.3 6.3 %all-to-all-start.6 = ((bf16[32,2,1024]{2,1,0:T(2,128)(2,1)}), bf16[32,2,1024]{2,1,0:T(2,128)(2,1)S(1)}, u32[]{:S(2)}, u32[]{:S(2)}) async-start(bf16[32,2,1024]{2,1,0:T(2,128)(2,1)} %reshape.606), calls=%async_computation.6 | async-start | bytes 262144 | tf_op jit(solution)/shard_map/all_to_all | solution.py:44
  176.2 14.6 %all-to-all-done.6 = bf16[32,2,1024]{2,1,0:T(2,128)(2,1)S(1)} async-done(((bf16[32,2,1024]{2,1,0:T(2,128)(2,1)}), bf16[32,2,1024]{2,1,0:T(2,128)(2,1)S(1)}, u32[]{:S(2)}, u32[]{:S(2)}) %all-to-all-start.6) | async-done | bytes 131104 | tf_op jit(solution)/shard_map/all_to_all | solution.py:44
  195.3 1.4 reduce.24
  196.7 0.7 reshape.608
  197.5 4.2 %all-to-all-start.7 = ((bf16[32,2,1024]{2,1,0:T(2,128)(2,1)}), bf16[32,2,1024]{2,1,0:T(2,128)(2,1)S(1)}, u32[]{:S(2)}, u32[]{:S(2)}) async-start(bf16[32,2,1024]{2,1,0:T(2,128)(2,1)} %reshape.608), calls=%async_computation.7 | async-start | bytes 262144 | tf_op jit(solution)/shard_map/all_to_all | solution.py:29
  201.6 0.7 reduce.19
  206.6 10.3 %all-to-all-done.7 = bf16[32,2,1024]{2,1,0:T(2,128)(2,1)S(1)} async-done(((bf16[32,2,1024]{2,1,0:T(2,128)(2,1)}), bf16[32,2,1024]{2,1,0:T(2,128)(2,1)S(1)}, u32[]{:S(2)}, u32[]{:S(2)}) %all-to-all-start.7) | async-done | bytes 131104 | tf_op jit(solution)/shard_map/all_to_all | solution.py:29
  218.0 0.7 reshape.610
  218.7 4.2 %all-to-all-start.8 = ((f32[32,1,288]{2,1,0:T(1,128)}), f32[32,1,288]{2,1,0:T(1,128)S(1)}, u32[]{:S(2)}, u32[]{:S(2)}) async-start(f32[32,1,288]{2,1,0:T(1,128)} %reshape.610), calls=%async_computation.8 | async-start | bytes 98304 | tf_op jit(solution)/shard_map/all_to_all | solution.py:29
  222.9 1.0 convolution_convert_fusion.1
  223.9 11.7 %all-to-all-done.8 = f32[32,1,288]{2,1,0:T(1,128)S(1)} async-done(((f32[32,1,288]{2,1,0:T(1,128)}), f32[32,1,288]{2,1,0:T(1,128)S(1)}, u32[]{:S(2)}, u32[]{:S(2)}) %all-to-all-start.8) | async-done | bytes 36896 | tf_op jit(solution)/shard_map/all_to_all | solution.py:29
  236.2 0.8 reduce.25
  240.2 24.7 %all_to_all.66 = bf16[16,17,2048]{2,1,0:T(8,128)(2,1)S(1)} all-to-all(bf16[16,17,2048]{2,1,0:T(8,128)(2,1)S(1)} %pad_maximum_fusion), channel_id=1, replica_groups=mesh['dp'=8,'seq_0'=2,'seq_1'=2,'expert_0'=4,'expert_1'=4] {'expert_0','..., dimensions={0} | all-to-all | bytes 2228224 | tf_op jit(solution)/shard_map/all_to_all | solution.py:57
  266.4 1.3 fusion
  (133 shorter events, 19.6 us)
Async XLA Ops:
  0.6 147.3 %copy-start = (bf16[1,192,2048]{2,1,0:T(8,128)(2,1)S(1)}, bf16[1,192,2048]{2,1,0:T(8,128)(2,1)}, u32[]{:S(2)}) copy-start(bf16[1,192,2048]{2,1,0:T(8,128)(2,1)} %param.24) | copy-start | bytes 2359300
  0.6 22.5 %copy-start.10 = (s32[1,8]{1,0:T(1,128)S(1)}, s32[1,8]{1,0:T(1,128)}, u32[]{:S(2)}) copy-start(s32[1,8]{1,0:T(1,128)} %param.29) | copy-start | bytes 100
  0.7 22.7 %copy-start.5 = (bf16[1,128,512]{2,1,0:T(8,128)(2,1)S(1)}, bf16[1,128,512]{2,1,0:T(8,128)(2,1)}, u32[]{:S(2)}) copy-start(bf16[1,128,512]{2,1,0:T(8,128)(2,1)} %param.16) | copy-start | bytes 393220
  0.7 22.8 %copy-start.9 = (s32[1,32]{1,0:T(1,128)S(1)}, s32[1,32]{1,0:T(1,128)}, u32[]{:S(2)}) copy-start(s32[1,32]{1,0:T(1,128)} %param.27) | copy-start | bytes 388
  6.3 36.9 %copy-start.4 = (bf16[1,128,512]{2,1,0:T(8,128)(2,1)S(1)}, bf16[1,128,512]{2,1,0:T(8,128)(2,1)}, u32[]{:S(2)}) copy-start(bf16[1,128,512]{2,1,0:T(8,128)(2,1)} %param.15) | copy-start | bytes 393220
  6.3 36.5 %all-to-all-start = ((bf16[32,2,2112]{2,1,0:T(2,128)(2,1)}), bf16[32,2,2112]{2,1,0:T(2,128)(2,1)S(1)}, u32[]{:S(2)}, u32[]{:S(2)}) async-start(bf16[32,2,2112]{2,1,0:T(2,128)(2,1)} %reshape.600), calls=%async_computation | async-start | bytes 557056 | tf_op jit(solution)/shard_map/all_to_all | solution.py:29
  72.4 2.1 copy-start.2
  72.9 10.3 %copy-start.7 = (bf16[1,1,2048]{2,1,0:T(2,128)(2,1)S(1)}, bf16[1,1,2048]{2,1,0:T(2,128)(2,1)}, u32[]{:S(2)}) copy-start(bf16[1,1,2048]{2,1,0:T(2,128)(2,1)} %param.18) | copy-start | bytes 12292
  73.7 26.5 %copy-start.8 = (bf16[2048]{0:T(1024)(128)(2,1)S(1)}, bf16[2048]{0:T(1024)(128)(2,1)}, u32[]{:S(2)}) copy-start(bf16[2048]{0:T(1024)(128)(2,1)} %param.20) | copy-start | bytes 12292
  74.8 47.2 %copy-start.3 = (bf16[2048,128]{1,0:T(8,128)(2,1)S(1)}, bf16[2048,128]{1,0:T(8,128)(2,1)}, u32[]{:S(2)}) copy-start(bf16[2048,128]{1,0:T(8,128)(2,1)} %param.21) | copy-start | bytes 1572868
  76.3 22.3 %all-to-all-start.2 = ((bf16[32,2,1024]{2,1,0:T(2,128)(2,1)}), bf16[32,2,1024]{2,1,0:T(2,128)(2,1)S(1)}, u32[]{:S(2)}, u32[]{:S(2)}) async-start(bf16[32,2,1024]{2,1,0:T(2,128)(2,1)} %reshape.602), calls=%async_computation.2 | async-start | bytes 262144 | tf_op jit(solution)/shard_map/all_to_all | solution.py:44
  102.5 19.5 %all-to-all-start.3 = ((bf16[32,2,1024]{2,1,0:T(2,128)(2,1)}), bf16[32,2,1024]{2,1,0:T(2,128)(2,1)S(1)}, u32[]{:S(2)}, u32[]{:S(2)}) async-start(bf16[32,2,1024]{2,1,0:T(2,128)(2,1)} %reshape.604), calls=%async_computation.3 | async-start | bytes 262144 | tf_op jit(solution)/shard_map/all_to_all | solution.py:29
  123.2 23.8 %copy-start.1 = (bf16[1,2048,192]{1,2,0:T(8,128)(2,1)S(1)}, bf16[1,2048,192]{1,2,0:T(8,128)(2,1)}, u32[]{:S(2)}) copy-start(bf16[1,2048,192]{1,2,0:T(8,128)(2,1)} %param.22) | copy-start | bytes 2359300
  123.7 23.8 %copy-start.11 = (bf16[1,2048,192]{1,2,0:T(8,128)(2,1)S(1)}, bf16[1,2048,192]{1,2,0:T(8,128)(2,1)}, u32[]{:S(2)}) copy-start(bf16[1,2048,192]{1,2,0:T(8,128)(2,1)} %param.23) | copy-start | bytes 2359300
  167.3 25.3 %copy-start.6 = (bf16[2048]{0:T(1024)(128)(2,1)S(1)}, bf16[2048]{0:T(1024)(128)(2,1)}, u32[]{:S(2)}) copy-start(bf16[2048]{0:T(1024)(128)(2,1)} %param.25) | copy-start | bytes 12292
  169.3 21.6 %all-to-all-start.6 = ((bf16[32,2,1024]{2,1,0:T(2,128)(2,1)}), bf16[32,2,1024]{2,1,0:T(2,128)(2,1)S(1)}, u32[]{:S(2)}, u32[]{:S(2)}) async-start(bf16[32,2,1024]{2,1,0:T(2,128)(2,1)} %reshape.606), calls=%async_computation.6 | async-start | bytes 262144 | tf_op jit(solution)/shard_map/all_to_all | solution.py:44
  197.5 19.5 %all-to-all-start.7 = ((bf16[32,2,1024]{2,1,0:T(2,128)(2,1)}), bf16[32,2,1024]{2,1,0:T(2,128)(2,1)S(1)}, u32[]{:S(2)}, u32[]{:S(2)}) async-start(bf16[32,2,1024]{2,1,0:T(2,128)(2,1)} %reshape.608), calls=%async_computation.7 | async-start | bytes 262144 | tf_op jit(solution)/shard_map/all_to_all | solution.py:29
  218.7 16.9 %all-to-all-start.8 = ((f32[32,1,288]{2,1,0:T(1,128)}), f32[32,1,288]{2,1,0:T(1,128)S(1)}, u32[]{:S(2)}, u32[]{:S(2)}) async-start(f32[32,1,288]{2,1,0:T(1,128)} %reshape.610), calls=%async_computation.8 | async-start | bytes 98304 | tf_op jit(solution)/shard_map/all_to_all | solution.py:29

commit v6 on v5

--- a/solution.py
+++ b/solution.py
@@ -155,9 +155,9 @@
     stats = jnp.stack([totals_hi, totals_lo, peak_hi, peak_lo], axis=-1)
     stats = jnp.swapaxes(stats, 0, 1).reshape(1, QUERY_HEADS, -1)
     packed = jnp.concatenate([weighted.astype(jnp.bfloat16), stats], axis=0)
-    arrived = lax.all_to_all(
-        packed.reshape(1, *packed.shape), DP_SEQ, split_axis=2, concat_axis=0, tiled=True
-    )
+    packed = jnp.swapaxes(packed, 0, 1).reshape(1, QUERY_HEADS, -1)
+    arrived = lax.all_to_all(packed, DP_SEQ, split_axis=1, concat_axis=0, tiled=True)
+    arrived = arrived.reshape(arrived.shape[0], number_of_steps + 1, 1, HEAD_WIDTH)
     got_stats = arrived[:, number_of_steps].reshape(arrived.shape[0], number_of_steps, 1, 4)
     attn = merge_heads(
         arrived[:, :number_of_steps].astype(jnp.float32),
@@ -251,26 +251,31 @@
     chunk = router_part.shape[1]
     router_hi, router_lo = split_pair(router_part)
     loss_hi, loss_lo = split_pair(pack_loss)
-    extra_row = jnp.concatenate(
+    side = jnp.concatenate(
         [
             router_hi,
             router_lo,
             jnp.broadcast_to(loss_hi, (group_size, 1)),
             jnp.broadcast_to(loss_lo, (group_size, 1)),
-            jnp.zeros((group_size, width - 2 * chunk - 2), jnp.bfloat16),
         ],
         axis=1,
     )
+    side_width = -(-side.shape[1] // (per_source * HEAD_WIDTH)) * HEAD_WIDTH
+    side = jnp.pad(side, ((0, 0), (0, per_source * side_width - side.shape[1])))
     sent = jnp.concatenate(
-        [d_out.reshape(group_size, per_source, width), extra_row[:, None, :]], axis=1
+        [
+            d_out.reshape(group_size, per_source, width),
+            side.reshape(group_size, per_source, side_width),
+        ],
+        axis=2,
     )
     got = across_group(sent)
-    grads_arrived = got[:, :per_source].reshape(slots, width)
+    grads_arrived = got[:, :, :width].reshape(slots, width)
     grad_down = lax.dot_general(
         hidden, grads_arrived, contract_rows, preferred_element_type=jnp.float32
     )
     grad_down = grad_down.astype(jnp.bfloat16).reshape((1,) + grad_down.shape)
-    tail = got[:, per_source]
+    tail = got[:, :, width:].reshape(group_size, -1)
     grad_router = jnp.sum(join_pair(tail[:, :chunk], tail[:, chunk : 2 * chunk]), axis=0)
     grad_router = grad_router.reshape(-1, experts).astype(jnp.bfloat16)
     loss = jnp.sum(join_pair(tail[:, 2 * chunk], tail[:, 2 * chunk + 1]))

time: 269 us -> 266 us (0.989)
  blocking collectives: 93.6 us -> 88.2 us
    all_to_all x3, blocking collectives: 66.8 us -> 62.7 us  [across_group(): lax.all_to_all(buffer, EXPERT, split_axis=0, concat_axis=0, tiled=True)]
    unnamed x42 -> x46, local copies, waits for them, and re-layouts: 5.81 us -> 6.94 us
where the time goes in v6:
time: 266 us; the launch traced here: 265 us
  blocking collectives  88.2 us (33%)
  waiting for transfers between devices  86 us (32%)
  starting transfers between devices  41.7 us (16%)
  other arithmetic  19.6 us (7%)
  local copies, waits for them, and re-layouts  12.8 us (5%)
  between operations  10.1 us (4%)
  matrix products  7.04 us (3%)
    all_to_all x3, blocking collectives, across_group(): lax.all_to_all(buffer, EXPERT, split_axis=0, concat_axis=0, tiled=True)  62.7 us
    all_to_all x4, waiting for transfers between devices, from_everyone(): return lax.all_to_all(copies, axis, split_axis=0, concat_axis=0, tiled=True)  56.1 us
    all_to_all x2, waiting for transfers between devices, sent_and_summed(): lax.all_to_all(in_blocks(array, dim, count), axis, 0, 0, tiled=True)  29.9 us
    all_to_all x4, starting transfers between devices, from_everyone(): return lax.all_to_all(copies, axis, split_axis=0, concat_axis=0, tiled=True)  29.3 us
    all_to_all x1, blocking collectives, shards(): lax.all_to_all(packed, DP_SEQ, split_axis=1, concat_axis=0, tiled=True)  25.5 us
    all_to_all x2, starting transfers between devices, sent_and_summed(): lax.all_to_all(in_blocks(array, dim, count), axis, 0, 0, tiled=True)  12.4 us
    unnamed x46, local copies, waits for them, and re-layouts  6.94 us
  transfers between devices with their start and end apart: 6, of which 6 were waited for; matrix products, arithmetic and copies ran while one was open for 1% of the time, Pallas kernels for 0%

profile of v6, /device:TPU:1, one launch (start us, length us, event | category | flops | bytes accessed | tf_op | source)
XLA Modules:
  0.0 265.4 jit_solution(12288529739178511030)
XLA Ops:
  0.7 0.8 convert_bitcast_fusion.1
  1.4 0.8 concatenate.17
  3.1 2.2 reduce.22
  5.4 0.9 reshape.618
  6.3 16.8 %all-to-all-start = ((bf16[32,2,2112]{2,1,0:T(2,128)(2,1)}), bf16[32,2,2112]{2,1,0:T(2,128)(2,1)S(1)}, u32[]{:S(2)}, u32[]{:S(2)}) async-start(bf16[32,2,2112]{2,1,0:T(2,128)(2,1)} %reshape.618), calls=%async_computation | async-start | bytes 557056 | tf_op jit(solution)/shard_map/all_to_all | solution.py:29
  23.6 19.0 %all-to-all-done = bf16[32,2,2112]{2,1,0:T(2,128)(2,1)S(1)} async-done(((bf16[32,2,2112]{2,1,0:T(2,128)(2,1)}), bf16[32,2,2112]{2,1,0:T(2,128)(2,1)S(1)}, u32[]{:S(2)}, u32[]{:S(2)}) %all-to-all-start) | async-done | bytes 270368 | tf_op jit(solution)/shard_map/all_to_all | solution.py:29
  45.6 2.2 reduce.23
  48.1 25.5 %all_to_all.54 = bf16[32,2,2112]{2,1,0:T(2,128)(2,1)S(1)} all-to-all(bf16[32,2,2112]{2,1,0:T(2,128)(2,1)S(1)} %reshape.620), channel_id=1, replica_groups=mesh['dp'=8,'seq_0'=2,'seq_1'=2,'expert_0'=4,'expert_1'=4] {'dp','seq_0'..., dimensions={0} | all-to-all | bytes 540672 | tf_op jit(solution)/shard_map/all_to_all | solution.py:159
  73.9 1.5 bitcast_reduce_fusion
  77.9 0.7 reshape.622
  78.7 6.2 %all-to-all-start.2 = ((bf16[32,2,1024]{2,1,0:T(2,128)(2,1)}), bf16[32,2,1024]{2,1,0:T(2,128)(2,1)S(1)}, u32[]{:S(2)}, u32[]{:S(2)}) async-start(bf16[32,2,1024]{2,1,0:T(2,128)(2,1)} %reshape.622), calls=%async_computation.2 | async-start | bytes 262144 | tf_op jit(solution)/shard_map/all_to_all | solution.py:44
  84.9 15.2 %all-to-all-done.2 = bf16[32,2,1024]{2,1,0:T(2,128)(2,1)S(1)} async-done(((bf16[32,2,1024]{2,1,0:T(2,128)(2,1)}), bf16[32,2,1024]{2,1,0:T(2,128)(2,1)S(1)}, u32[]{:S(2)}, u32[]{:S(2)}) %all-to-all-start.2) | async-done | bytes 131104 | tf_op jit(solution)/shard_map/all_to_all | solution.py:44
  101.9 1.4 reduce.25
  103.3 0.7 reshape.624
  104.1 4.2 %all-to-all-start.3 = ((bf16[32,2,1024]{2,1,0:T(2,128)(2,1)}), bf16[32,2,1024]{2,1,0:T(2,128)(2,1)S(1)}, u32[]{:S(2)}, u32[]{:S(2)}) async-start(bf16[32,2,1024]{2,1,0:T(2,128)(2,1)} %reshape.624), calls=%async_computation.3 | async-start | bytes 262144 | tf_op jit(solution)/shard_map/all_to_all | solution.py:29
  108.5 15.1 %all-to-all-done.3 = bf16[32,2,1024]{2,1,0:T(2,128)(2,1)S(1)} async-done(((bf16[32,2,1024]{2,1,0:T(2,128)(2,1)}), bf16[32,2,1024]{2,1,0:T(2,128)(2,1)S(1)}, u32[]{:S(2)}, u32[]{:S(2)}) %all-to-all-start.3) | async-done | bytes 131104 | tf_op jit(solution)/shard_map/all_to_all | solution.py:29
  125.3 23.3 %all_to_all.55 = bf16[16,16,2048]{2,1,0:T(8,128)(2,1)S(1)} all-to-all(bf16[16,16,2048]{2,1,0:T(8,128)(2,1)S(1)} %bitcast.150), channel_id=1, replica_groups=mesh['dp'=8,'seq_0'=2,'seq_1'=2,'expert_0'=4,'expert_1'=4] {'expert_0','..., dimensions={0} | all-to-all | bytes 2097152 | tf_op jit(solution)/shard_map/all_to_all | solution.py:57
  150.6 18.8 %all_to_all.56 = bf16[16,16,2048]{2,1,0:T(8,128)(2,1)S(1)} all-to-all(bf16[16,16,2048]{2,1,0:T(8,128)(2,1)S(1)} %bitcast.152), channel_id=1, replica_groups=mesh['dp'=8,'seq_0'=2,'seq_1'=2,'expert_0'=4,'expert_1'=4] {'expert_0','..., dimensions={0} | all-to-all | bytes 2097152 | tf_op jit(solution)/shard_map/all_to_all | solution.py:57
  170.7 0.7 reshape.626
  171.5 6.3 %all-to-all-start.6 = ((bf16[32,2,1024]{2,1,0:T(2,128)(2,1)}), bf16[32,2,1024]{2,1,0:T(2,128)(2,1)S(1)}, u32[]{:S(2)}, u32[]{:S(2)}) async-start(bf16[32,2,1024]{2,1,0:T(2,128)(2,1)} %reshape.626), calls=%async_computation.6 | async-start | bytes 262144 | tf_op jit(solution)/shard_map/all_to_all | solution.py:44
  178.4 14.6 %all-to-all-done.6 = bf16[32,2,1024]{2,1,0:T(2,128)(2,1)S(1)} async-done(((bf16[32,2,1024]{2,1,0:T(2,128)(2,1)}), bf16[32,2,1024]{2,1,0:T(2,128)(2,1)S(1)}, u32[]{:S(2)}, u32[]{:S(2)}) %all-to-all-start.6) | async-done | bytes 131104 | tf_op jit(solution)/shard_map/all_to_all | solution.py:44
  197.5 1.4 reduce.27
  198.9 0.7 reshape.628
  199.6 4.2 %all-to-all-start.7 = ((bf16[32,2,1024]{2,1,0:T(2,128)(2,1)}), bf16[32,2,1024]{2,1,0:T(2,128)(2,1)S(1)}, u32[]{:S(2)}, u32[]{:S(2)}) async-start(bf16[32,2,1024]{2,1,0:T(2,128)(2,1)} %reshape.628), calls=%async_computation.7 | async-start | bytes 262144 | tf_op jit(solution)/shard_map/all_to_all | solution.py:29
  208.8 10.3 %all-to-all-done.7 = bf16[32,2,1024]{2,1,0:T(2,128)(2,1)S(1)} async-done(((bf16[32,2,1024]{2,1,0:T(2,128)(2,1)}), bf16[32,2,1024]{2,1,0:T(2,128)(2,1)S(1)}, u32[]{:S(2)}, u32[]{:S(2)}) %all-to-all-start.7) | async-done | bytes 131104 | tf_op jit(solution)/shard_map/all_to_all | solution.py:29
  220.2 0.7 reshape.630
  220.9 4.2 %all-to-all-start.8 = ((f32[32,1,288]{2,1,0:T(1,128)}), f32[32,1,288]{2,1,0:T(1,128)S(1)}, u32[]{:S(2)}, u32[]{:S(2)}) async-start(f32[32,1,288]{2,1,0:T(1,128)} %reshape.630), calls=%async_computation.8 | async-start | bytes 98304 | tf_op jit(solution)/shard_map/all_to_all | solution.py:29
  225.1 1.0 convolution_convert_fusion.1
  226.1 11.7 %all-to-all-done.8 = f32[32,1,288]{2,1,0:T(1,128)S(1)} async-done(((f32[32,1,288]{2,1,0:T(1,128)}), f32[32,1,288]{2,1,0:T(1,128)S(1)}, u32[]{:S(2)}, u32[]{:S(2)}) %all-to-all-start.8) | async-done | bytes 36896 | tf_op jit(solution)/shard_map/all_to_all | solution.py:29
  238.3 0.8 reduce.28
  242.2 20.6 %all_to_all.57 = bf16[16,16,2176]{2,1,0:T(8,128)(2,1)S(1)} all-to-all(bf16[16,16,2176]{2,1,0:T(8,128)(2,1)S(1)} %pad_maximum_fusion), channel_id=1, replica_groups=mesh['dp'=8,'seq_0'=2,'seq_1'=2,'expert_0'=4,'expert_1'=4] {'expert_0','..., dimensions={0} | all-to-all | bytes 2228224 | tf_op jit(solution)/shard_map/all_to_all | solution.py:57
  264.2 1.3 fusion
  (140 shorter events, 21.4 us)
Async XLA Ops:
  0.6 149.5 %copy-start = (bf16[1,192,2048]{2,1,0:T(8,128)(2,1)S(1)}, bf16[1,192,2048]{2,1,0:T(8,128)(2,1)}, u32[]{:S(2)}) copy-start(bf16[1,192,2048]{2,1,0:T(8,128)(2,1)} %param.24) | copy-start | bytes 2359300
  2.3 20.8 %copy-start.10 = (s32[1,8]{1,0:T(1,128)S(1)}, s32[1,8]{1,0:T(1,128)}, u32[]{:S(2)}) copy-start(s32[1,8]{1,0:T(1,128)} %param.29) | copy-start | bytes 100
  2.3 21.0 %copy-start.5 = (bf16[1,128,512]{2,1,0:T(8,128)(2,1)S(1)}, bf16[1,128,512]{2,1,0:T(8,128)(2,1)}, u32[]{:S(2)}) copy-start(bf16[1,128,512]{2,1,0:T(8,128)(2,1)} %param.16) | copy-start | bytes 393220
  2.6 20.7 %copy-start.9 = (s32[1,32]{1,0:T(1,128)S(1)}, s32[1,32]{1,0:T(1,128)}, u32[]{:S(2)}) copy-start(s32[1,32]{1,0:T(1,128)} %param.27) | copy-start | bytes 388
  6.3 36.3 %all-to-all-start = ((bf16[32,2,2112]{2,1,0:T(2,128)(2,1)}), bf16[32,2,2112]{2,1,0:T(2,128)(2,1)S(1)}, u32[]{:S(2)}, u32[]{:S(2)}) async-start(bf16[32,2,2112]{2,1,0:T(2,128)(2,1)} %reshape.618), calls=%async_computation | async-start | bytes 557056 | tf_op jit(solution)/shard_map/all_to_all | solution.py:29
  23.6 19.5 %copy-start.4 = (bf16[1,128,512]{2,1,0:T(8,128)(2,1)S(1)}, bf16[1,128,512]{2,1,0:T(8,128)(2,1)}, u32[]{:S(2)}) copy-start(bf16[1,128,512]{2,1,0:T(8,128)(2,1)} %param.15) | copy-start | bytes 393220
  73.9 3.1 %copy-start.2 = (bf16[128,2048]{1,0:T(8,128)(2,1)S(1)}, bf16[128,2048]{1,0:T(8,128)(2,1)}, u32[]{:S(2)}) copy-start(bf16[128,2048]{1,0:T(8,128)(2,1)} %param.19) | copy-start | bytes 1572868
  75.6 9.2 %copy-start.7 = (bf16[1,1,2048]{2,1,0:T(2,128)(2,1)S(1)}, bf16[1,1,2048]{2,1,0:T(2,128)(2,1)}, u32[]{:S(2)}) copy-start(bf16[1,1,2048]{2,1,0:T(2,128)(2,1)} %param.18) | copy-start | bytes 12292
  76.8 25.0 %copy-start.8 = (bf16[2048]{0:T(1024)(128)(2,1)S(1)}, bf16[2048]{0:T(1024)(128)(2,1)}, u32[]{:S(2)}) copy-start(bf16[2048]{0:T(1024)(128)(2,1)} %param.20) | copy-start | bytes 12292
  78.7 21.4 %all-to-all-start.2 = ((bf16[32,2,1024]{2,1,0:T(2,128)(2,1)}), bf16[32,2,1024]{2,1,0:T(2,128)(2,1)S(1)}, u32[]{:S(2)}, u32[]{:S(2)}) async-start(bf16[32,2,1024]{2,1,0:T(2,128)(2,1)} %reshape.622), calls=%async_computation.2 | async-start | bytes 262144 | tf_op jit(solution)/shard_map/all_to_all | solution.py:44
  100.2 23.4 %copy-start.3 = (bf16[2048,128]{1,0:T(8,128)(2,1)S(1)}, bf16[2048,128]{1,0:T(8,128)(2,1)}, u32[]{:S(2)}) copy-start(bf16[2048,128]{1,0:T(8,128)(2,1)} %param.21) | copy-start | bytes 1572868
  104.1 19.5 %all-to-all-start.3 = ((bf16[32,2,1024]{2,1,0:T(2,128)(2,1)}), bf16[32,2,1024]{2,1,0:T(2,128)(2,1)S(1)}, u32[]{:S(2)}, u32[]{:S(2)}) async-start(bf16[32,2,1024]{2,1,0:T(2,128)(2,1)} %reshape.624), calls=%async_computation.3 | async-start | bytes 262144 | tf_op jit(solution)/shard_map/all_to_all | solution.py:29
  125.2 23.3 %copy-start.1 = (bf16[1,2048,192]{1,2,0:T(8,128)(2,1)S(1)}, bf16[1,2048,192]{1,2,0:T(8,128)(2,1)}, u32[]{:S(2)}) copy-start(bf16[1,2048,192]{1,2,0:T(8,128)(2,1)} %param.22) | copy-start | bytes 2359300
  148.5 1.1 copy-start.11
  169.4 25.3 %copy-start.6 = (bf16[2048]{0:T(1024)(128)(2,1)S(1)}, bf16[2048]{0:T(1024)(128)(2,1)}, u32[]{:S(2)}) copy-start(bf16[2048]{0:T(1024)(128)(2,1)} %param.25) | copy-start | bytes 12292
  171.5 21.6 %all-to-all-start.6 = ((bf16[32,2,1024]{2,1,0:T(2,128)(2,1)}), bf16[32,2,1024]{2,1,0:T(2,128)(2,1)S(1)}, u32[]{:S(2)}, u32[]{:S(2)}) async-start(bf16[32,2,1024]{2,1,0:T(2,128)(2,1)} %reshape.626), calls=%async_computation.6 | async-start | bytes 262144 | tf_op jit(solution)/shard_map/all_to_all | solution.py:44
  199.6 19.5 %all-to-all-start.7 = ((bf16[32,2,1024]{2,1,0:T(2,128)(2,1)}), bf16[32,2,1024]{2,1,0:T(2,128)(2,1)S(1)}, u32[]{:S(2)}, u32[]{:S(2)}) async-start(bf16[32,2,1024]{2,1,0:T(2,128)(2,1)} %reshape.628), calls=%async_computation.7 | async-start | bytes 262144 | tf_op jit(solution)/shard_map/all_to_all | solution.py:29
  220.9 16.9 %all-to-all-start.8 = ((f32[32,1,288]{2,1,0:T(1,128)}), f32[32,1,288]{2,1,0:T(1,128)S(1)}, u32[]{:S(2)}, u32[]{:S(2)}) async-start(f32[32,1,288]{2,1,0:T(1,128)} %reshape.630), calls=%async_computation.8 | async-start | bytes 98304 | tf_op jit(solution)/shard_map/all_to_all | solution.py:29

commit v7 on v6

--- a/solution.py
+++ b/solution.py
@@ -140,8 +140,9 @@
     scores = jnp.stack(score_list, axis=1).reshape(number_of_steps, QUERY_HEADS, count_of_keys)
     local_peak = jnp.max(scores, axis=2)
     heads_of_values = values[0].reshape(count_of_keys, KEY_VALUE_HEADS, HEAD_WIDTH)
+    shift = local_peak.astype(jnp.bfloat16)
     complete_weight_rows = jnp.where(
-        allowed[:, None, :], jnp.exp(scores - local_peak[:, :, None]), 0.0
+        allowed[:, None, :], jnp.exp(scores - shift.astype(jnp.float32)[:, :, None]), 0.0
     )
     totals = jnp.sum(complete_weight_rows, axis=2)
     reduced_weight_rows = complete_weight_rows.astype(jnp.bfloat16).reshape(
@@ -151,8 +152,7 @@
         "skgt,tkd->skgd", reduced_weight_rows, heads_of_values, preferred_element_type=jnp.float32
     ).reshape(number_of_steps, QUERY_HEADS, HEAD_WIDTH)
     totals_hi, totals_lo = split_pair(totals)
-    peak_hi, peak_lo = split_pair(local_peak)
-    stats = jnp.stack([totals_hi, totals_lo, peak_hi, peak_lo], axis=-1)
+    stats = jnp.stack([totals_hi, totals_lo, shift, jnp.zeros_like(shift)], axis=-1)
     stats = jnp.swapaxes(stats, 0, 1).reshape(1, QUERY_HEADS, -1)
     packed = jnp.concatenate([weighted.astype(jnp.bfloat16), stats], axis=0)
     packed = jnp.swapaxes(packed, 0, 1).reshape(1, QUERY_HEADS, -1)
@@ -162,7 +162,7 @@
     attn = merge_heads(
         arrived[:, :number_of_steps].astype(jnp.float32),
         join_pair(got_stats[..., 0], got_stats[..., 1]),
-        join_pair(got_stats[..., 2], got_stats[..., 3]),
+        got_stats[..., 2].astype(jnp.float32),
     )
     mixed = sent_and_summed(
         jnp.dot(attn, out_proj, preferred_element_type=jnp.float32).astype(jnp.bfloat16), DP_SEQ, 0

time: 266 us -> 267 us (level)
  no operation moved by 1% of the time
where the time goes in v7:
time: 267 us; the launch traced here: 266 us
  blocking collectives  88.2 us (33%)
  waiting for transfers between devices  85.9 us (32%)
  starting transfers between devices  41.7 us (16%)
  other arithmetic  19.7 us (7%)
  local copies, waits for them, and re-layouts  12.9 us (5%)
  between operations  10.1 us (4%)
  matrix products  7.05 us (3%)
    all_to_all x3, blocking collectives, across_group(): lax.all_to_all(buffer, EXPERT, split_axis=0, concat_axis=0, tiled=True)  62.7 us
    all_to_all x4, waiting for transfers between devices, from_everyone(): return lax.all_to_all(copies, axis, split_axis=0, concat_axis=0, tiled=True)  56 us
    all_to_all x2, waiting for transfers between devices, sent_and_summed(): lax.all_to_all(in_blocks(array, dim, count), axis, 0, 0, tiled=True)  29.9 us
    all_to_all x4, starting transfers between devices, from_everyone(): return lax.all_to_all(copies, axis, split_axis=0, concat_axis=0, tiled=True)  29.3 us
    all_to_all x1, blocking collectives, shards(): lax.all_to_all(packed, DP_SEQ, split_axis=1, concat_axis=0, tiled=True)  25.5 us
    all_to_all x2, starting transfers between devices, sent_and_summed(): lax.all_to_all(in_blocks(array, dim, count), axis, 0, 0, tiled=True)  12.5 us
    unnamed x46, local copies, waits for them, and re-layouts  6.94 us
  transfers between devices with their start and end apart: 6, of which 6 were waited for; matrix products, arithmetic and copies ran while one was open for 1% of the time, Pallas kernels for 0%

profile of v7, /device:TPU:1, one launch (start us, length us, event | category | flops | bytes accessed | tf_op | source)
XLA Modules:
  0.0 265.6 jit_solution(4019602528548046425)
XLA Ops:
  0.7 0.8 convert_bitcast_fusion.2
  1.4 0.8 concatenate.17
  3.1 2.2 reduce.23
  5.4 0.9 reshape.586
  6.3 16.8 %all-to-all-start = ((bf16[32,2,2112]{2,1,0:T(2,128)(2,1)}), bf16[32,2,2112]{2,1,0:T(2,128)(2,1)S(1)}, u32[]{:S(2)}, u32[]{:S(2)}) async-start(bf16[32,2,2112]{2,1,0:T(2,128)(2,1)} %reshape.586), calls=%async_computation | async-start | bytes 557056 | tf_op jit(solution)/shard_map/all_to_all | solution.py:29
  23.6 19.0 %all-to-all-done = bf16[32,2,2112]{2,1,0:T(2,128)(2,1)S(1)} async-done(((bf16[32,2,2112]{2,1,0:T(2,128)(2,1)}), bf16[32,2,2112]{2,1,0:T(2,128)(2,1)S(1)}, u32[]{:S(2)}, u32[]{:S(2)}) %all-to-all-start) | async-done | bytes 270368 | tf_op jit(solution)/shard_map/all_to_all | solution.py:29
  45.8 2.2 reduce.24
  48.3 25.5 %all_to_all.54 = bf16[32,2,2112]{2,1,0:T(2,128)(2,1)S(1)} all-to-all(bf16[32,2,2112]{2,1,0:T(2,128)(2,1)S(1)} %reshape.588), channel_id=1, replica_groups=mesh['dp'=8,'seq_0'=2,'seq_1'=2,'expert_0'=4,'expert_1'=4] {'dp','seq_0'..., dimensions={0} | all-to-all | bytes 540672 | tf_op jit(solution)/shard_map/all_to_all | solution.py:159
  74.1 1.5 bitcast_reduce_fusion
  78.1 0.7 reshape.590
  78.8 6.1 %all-to-all-start.2 = ((bf16[32,2,1024]{2,1,0:T(2,128)(2,1)}), bf16[32,2,1024]{2,1,0:T(2,128)(2,1)S(1)}, u32[]{:S(2)}, u32[]{:S(2)}) async-start(bf16[32,2,1024]{2,1,0:T(2,128)(2,1)} %reshape.590), calls=%async_computation.2 | async-start | bytes 262144 | tf_op jit(solution)/shard_map/all_to_all | solution.py:44
  85.0 15.2 %all-to-all-done.2 = bf16[32,2,1024]{2,1,0:T(2,128)(2,1)S(1)} async-done(((bf16[32,2,1024]{2,1,0:T(2,128)(2,1)}), bf16[32,2,1024]{2,1,0:T(2,128)(2,1)S(1)}, u32[]{:S(2)}, u32[]{:S(2)}) %all-to-all-start.2) | async-done | bytes 131104 | tf_op jit(solution)/shard_map/all_to_all | solution.py:44
  102.1 1.4 reduce.26
  103.5 0.7 reshape.592
  104.2 4.2 %all-to-all-start.3 = ((bf16[32,2,1024]{2,1,0:T(2,128)(2,1)}), bf16[32,2,1024]{2,1,0:T(2,128)(2,1)S(1)}, u32[]{:S(2)}, u32[]{:S(2)}) async-start(bf16[32,2,1024]{2,1,0:T(2,128)(2,1)} %reshape.592), calls=%async_computation.3 | async-start | bytes 262144 | tf_op jit(solution)/shard_map/all_to_all | solution.py:29
  108.6 15.1 %all-to-all-done.3 = bf16[32,2,1024]{2,1,0:T(2,128)(2,1)S(1)} async-done(((bf16[32,2,1024]{2,1,0:T(2,128)(2,1)}), bf16[32,2,1024]{2,1,0:T(2,128)(2,1)S(1)}, u32[]{:S(2)}, u32[]{:S(2)}) %all-to-all-start.3) | async-done | bytes 131104 | tf_op jit(solution)/shard_map/all_to_all | solution.py:29
  125.4 23.3 %all_to_all.55 = bf16[16,16,2048]{2,1,0:T(8,128)(2,1)S(1)} all-to-all(bf16[16,16,2048]{2,1,0:T(8,128)(2,1)S(1)} %bitcast.148), channel_id=1, replica_groups=mesh['dp'=8,'seq_0'=2,'seq_1'=2,'expert_0'=4,'expert_1'=4] {'expert_0','..., dimensions={0} | all-to-all | bytes 2097152 | tf_op jit(solution)/shard_map/all_to_all | solution.py:57
  150.8 18.8 %all_to_all.56 = bf16[16,16,2048]{2,1,0:T(8,128)(2,1)S(1)} all-to-all(bf16[16,16,2048]{2,1,0:T(8,128)(2,1)S(1)} %bitcast.150), channel_id=1, replica_groups=mesh['dp'=8,'seq_0'=2,'seq_1'=2,'expert_0'=4,'expert_1'=4] {'expert_0','..., dimensions={0} | all-to-all | bytes 2097152 | tf_op jit(solution)/shard_map/all_to_all | solution.py:57
  170.9 0.7 reshape.594
  171.6 6.3 %all-to-all-start.6 = ((bf16[32,2,1024]{2,1,0:T(2,128)(2,1)}), bf16[32,2,1024]{2,1,0:T(2,128)(2,1)S(1)}, u32[]{:S(2)}, u32[]{:S(2)}) async-start(bf16[32,2,1024]{2,1,0:T(2,128)(2,1)} %reshape.594), calls=%async_computation.6 | async-start | bytes 262144 | tf_op jit(solution)/shard_map/all_to_all | solution.py:44
  178.6 14.6 %all-to-all-done.6 = bf16[32,2,1024]{2,1,0:T(2,128)(2,1)S(1)} async-done(((bf16[32,2,1024]{2,1,0:T(2,128)(2,1)}), bf16[32,2,1024]{2,1,0:T(2,128)(2,1)S(1)}, u32[]{:S(2)}, u32[]{:S(2)}) %all-to-all-start.6) | async-done | bytes 131104 | tf_op jit(solution)/shard_map/all_to_all | solution.py:44
  197.7 1.4 reduce.28
  199.1 0.7 reshape.596
  199.8 4.2 %all-to-all-start.7 = ((bf16[32,2,1024]{2,1,0:T(2,128)(2,1)}), bf16[32,2,1024]{2,1,0:T(2,128)(2,1)S(1)}, u32[]{:S(2)}, u32[]{:S(2)}) async-start(bf16[32,2,1024]{2,1,0:T(2,128)(2,1)} %reshape.596), calls=%async_computation.7 | async-start | bytes 262144 | tf_op jit(solution)/shard_map/all_to_all | solution.py:29
  209.0 10.3 %all-to-all-done.7 = bf16[32,2,1024]{2,1,0:T(2,128)(2,1)S(1)} async-done(((bf16[32,2,1024]{2,1,0:T(2,128)(2,1)}), bf16[32,2,1024]{2,1,0:T(2,128)(2,1)S(1)}, u32[]{:S(2)}, u32[]{:S(2)}) %all-to-all-start.7) | async-done | bytes 131104 | tf_op jit(solution)/shard_map/all_to_all | solution.py:29
  220.3 0.7 reshape.598
  221.1 4.2 %all-to-all-start.8 = ((f32[32,1,288]{2,1,0:T(1,128)}), f32[32,1,288]{2,1,0:T(1,128)S(1)}, u32[]{:S(2)}, u32[]{:S(2)}) async-start(f32[32,1,288]{2,1,0:T(1,128)} %reshape.598), calls=%async_computation.8 | async-start | bytes 98304 | tf_op jit(solution)/shard_map/all_to_all | solution.py:29
  225.2 1.0 convolution_convert_fusion.1
  226.3 11.7 %all-to-all-done.8 = f32[32,1,288]{2,1,0:T(1,128)S(1)} async-done(((f32[32,1,288]{2,1,0:T(1,128)}), f32[32,1,288]{2,1,0:T(1,128)S(1)}, u32[]{:S(2)}, u32[]{:S(2)}) %all-to-all-start.8) | async-done | bytes 36896 | tf_op jit(solution)/shard_map/all_to_all | solution.py:29
  238.5 0.8 reduce.29
  242.3 20.6 %all_to_all.57 = bf16[16,16,2176]{2,1,0:T(8,128)(2,1)S(1)} all-to-all(bf16[16,16,2176]{2,1,0:T(8,128)(2,1)S(1)} %pad_maximum_fusion), channel_id=1, replica_groups=mesh['dp'=8,'seq_0'=2,'seq_1'=2,'expert_0'=4,'expert_1'=4] {'expert_0','..., dimensions={0} | all-to-all | bytes 2228224 | tf_op jit(solution)/shard_map/all_to_all | solution.py:57
  264.3 1.3 fusion
  (142 shorter events, 21.7 us)
Async XLA Ops:
  0.6 149.7 %copy-start = (bf16[1,192,2048]{2,1,0:T(8,128)(2,1)S(1)}, bf16[1,192,2048]{2,1,0:T(8,128)(2,1)}, u32[]{:S(2)}) copy-start(bf16[1,192,2048]{2,1,0:T(8,128)(2,1)} %param.24) | copy-start | bytes 2359300
  2.3 20.8 %copy-start.10 = (s32[1,8]{1,0:T(1,128)S(1)}, s32[1,8]{1,0:T(1,128)}, u32[]{:S(2)}) copy-start(s32[1,8]{1,0:T(1,128)} %param.29) | copy-start | bytes 100
  2.3 21.0 %copy-start.5 = (bf16[1,128,512]{2,1,0:T(8,128)(2,1)S(1)}, bf16[1,128,512]{2,1,0:T(8,128)(2,1)}, u32[]{:S(2)}) copy-start(bf16[1,128,512]{2,1,0:T(8,128)(2,1)} %param.16) | copy-start | bytes 393220
  2.6 20.8 %copy-start.9 = (s32[1,32]{1,0:T(1,128)S(1)}, s32[1,32]{1,0:T(1,128)}, u32[]{:S(2)}) copy-start(s32[1,32]{1,0:T(1,128)} %param.27) | copy-start | bytes 388
  6.3 36.3 %all-to-all-start = ((bf16[32,2,2112]{2,1,0:T(2,128)(2,1)}), bf16[32,2,2112]{2,1,0:T(2,128)(2,1)S(1)}, u32[]{:S(2)}, u32[]{:S(2)}) async-start(bf16[32,2,2112]{2,1,0:T(2,128)(2,1)} %reshape.586), calls=%async_computation | async-start | bytes 557056 | tf_op jit(solution)/shard_map/all_to_all | solution.py:29
  23.6 19.5 %copy-start.4 = (bf16[1,128,512]{2,1,0:T(8,128)(2,1)S(1)}, bf16[1,128,512]{2,1,0:T(8,128)(2,1)}, u32[]{:S(2)}) copy-start(bf16[1,128,512]{2,1,0:T(8,128)(2,1)} %param.15) | copy-start | bytes 393220
  74.1 3.0 %copy-start.2 = (bf16[128,2048]{1,0:T(8,128)(2,1)S(1)}, bf16[128,2048]{1,0:T(8,128)(2,1)}, u32[]{:S(2)}) copy-start(bf16[128,2048]{1,0:T(8,128)(2,1)} %param.19) | copy-start | bytes 1572868
  75.8 9.2 %copy-start.7 = (bf16[1,1,2048]{2,1,0:T(2,128)(2,1)S(1)}, bf16[1,1,2048]{2,1,0:T(2,128)(2,1)}, u32[]{:S(2)}) copy-start(bf16[1,1,2048]{2,1,0:T(2,128)(2,1)} %param.18) | copy-start | bytes 12292
  76.9 25.0 %copy-start.8 = (bf16[2048]{0:T(1024)(128)(2,1)S(1)}, bf16[2048]{0:T(1024)(128)(2,1)}, u32[]{:S(2)}) copy-start(bf16[2048]{0:T(1024)(128)(2,1)} %param.20) | copy-start | bytes 12292
  78.8 21.4 %all-to-all-start.2 = ((bf16[32,2,1024]{2,1,0:T(2,128)(2,1)}), bf16[32,2,1024]{2,1,0:T(2,128)(2,1)S(1)}, u32[]{:S(2)}, u32[]{:S(2)}) async-start(bf16[32,2,1024]{2,1,0:T(2,128)(2,1)} %reshape.590), calls=%async_computation.2 | async-start | bytes 262144 | tf_op jit(solution)/shard_map/all_to_all | solution.py:44
  100.4 23.4 %copy-start.3 = (bf16[2048,128]{1,0:T(8,128)(2,1)S(1)}, bf16[2048,128]{1,0:T(8,128)(2,1)}, u32[]{:S(2)}) copy-start(bf16[2048,128]{1,0:T(8,128)(2,1)} %param.21) | copy-start | bytes 1572868
  104.2 19.4 %all-to-all-start.3 = ((bf16[32,2,1024]{2,1,0:T(2,128)(2,1)}), bf16[32,2,1024]{2,1,0:T(2,128)(2,1)S(1)}, u32[]{:S(2)}, u32[]{:S(2)}) async-start(bf16[32,2,1024]{2,1,0:T(2,128)(2,1)} %reshape.592), calls=%async_computation.3 | async-start | bytes 262144 | tf_op jit(solution)/shard_map/all_to_all | solution.py:29
  125.4 23.3 %copy-start.1 = (bf16[1,2048,192]{1,2,0:T(8,128)(2,1)S(1)}, bf16[1,2048,192]{1,2,0:T(8,128)(2,1)}, u32[]{:S(2)}) copy-start(bf16[1,2048,192]{1,2,0:T(8,128)(2,1)} %param.22) | copy-start | bytes 2359300
  148.7 1.1 copy-start.11
  169.6 25.3 %copy-start.6 = (bf16[2048]{0:T(1024)(128)(2,1)S(1)}, bf16[2048]{0:T(1024)(128)(2,1)}, u32[]{:S(2)}) copy-start(bf16[2048]{0:T(1024)(128)(2,1)} %param.25) | copy-start | bytes 12292
  171.6 21.6 %all-to-all-start.6 = ((bf16[32,2,1024]{2,1,0:T(2,128)(2,1)}), bf16[32,2,1024]{2,1,0:T(2,128)(2,1)S(1)}, u32[]{:S(2)}, u32[]{:S(2)}) async-start(bf16[32,2,1024]{2,1,0:T(2,128)(2,1)} %reshape.594), calls=%async_computation.6 | async-start | bytes 262144 | tf_op jit(solution)/shard_map/all_to_all | solution.py:44
  199.8 19.5 %all-to-all-start.7 = ((bf16[32,2,1024]{2,1,0:T(2,128)(2,1)}), bf16[32,2,1024]{2,1,0:T(2,128)(2,1)S(1)}, u32[]{:S(2)}, u32[]{:S(2)}) async-start(bf16[32,2,1024]{2,1,0:T(2,128)(2,1)} %reshape.596), calls=%async_computation.7 | async-start | bytes 262144 | tf_op jit(solution)/shard_map/all_to_all | solution.py:29
  221.1 16.9 %all-to-all-start.8 = ((f32[32,1,288]{2,1,0:T(1,128)}), f32[32,1,288]{2,1,0:T(1,128)S(1)}, u32[]{:S(2)}, u32[]{:S(2)}) async-start(f32[32,1,288]{2,1,0:T(1,128)} %reshape.598), calls=%async_computation.8 | async-start | bytes 98304 | tf_op jit(solution)/shard_map/all_to_all | solution.py:29

commit v8 on v7

--- a/solution.py
+++ b/solution.py
@@ -149,13 +149,13 @@
         number_of_steps, KEY_VALUE_HEADS, query_groups, count_of_keys
     )
     weighted = jnp.einsum(
-        "skgt,tkd->skgd", reduced_weight_rows, heads_of_values, preferred_element_type=jnp.float32
-    ).reshape(number_of_steps, QUERY_HEADS, HEAD_WIDTH)
+        "skgt,tkd->kgsd", reduced_weight_rows, heads_of_values, preferred_element_type=jnp.float32
+    ).reshape(QUERY_HEADS, number_of_steps, HEAD_WIDTH)
     totals_hi, totals_lo = split_pair(totals)
     stats = jnp.stack([totals_hi, totals_lo, shift, jnp.zeros_like(shift)], axis=-1)
-    stats = jnp.swapaxes(stats, 0, 1).reshape(1, QUERY_HEADS, -1)
-    packed = jnp.concatenate([weighted.astype(jnp.bfloat16), stats], axis=0)
-    packed = jnp.swapaxes(packed, 0, 1).reshape(1, QUERY_HEADS, -1)
+    stats = jnp.swapaxes(stats, 0, 1).reshape(QUERY_HEADS, 1, -1)
+    packed = jnp.concatenate([weighted.astype(jnp.bfloat16), stats], axis=1)
+    packed = packed.reshape(1, QUERY_HEADS, -1)
     arrived = lax.all_to_all(packed, DP_SEQ, split_axis=1, concat_axis=0, tiled=True)
     arrived = arrived.reshape(arrived.shape[0], number_of_steps + 1, 1, HEAD_WIDTH)
     got_stats = arrived[:, number_of_steps].reshape(arrived.shape[0], number_of_steps, 1, 4)

time: 267 us -> 266 us (level)
  no operation moved by 1% of the time
where the time goes in v8:
time: 266 us; the launch traced here: 265 us
  blocking collectives  88.2 us (33%)
  waiting for transfers between devices  85.9 us (32%)
  starting transfers between devices  41.7 us (16%)
  other arithmetic  19.7 us (7%)
  local copies, waits for them, and re-layouts  12.8 us (5%)
  between operations  10.1 us (4%)
  matrix products  7.04 us (3%)
    all_to_all x3, blocking collectives, across_group(): lax.all_to_all(buffer, EXPERT, split_axis=0, concat_axis=0, tiled=True)  62.7 us
    all_to_all x4, waiting for transfers between devices, from_everyone(): return lax.all_to_all(copies, axis, split_axis=0, concat_axis=0, tiled=True)  56 us
    all_to_all x2, waiting for transfers between devices, sent_and_summed(): lax.all_to_all(in_blocks(array, dim, count), axis, 0, 0, tiled=True)  29.9 us
    all_to_all x4, starting transfers between devices, from_everyone(): return lax.all_to_all(copies, axis, split_axis=0, concat_axis=0, tiled=True)  29.3 us
    all_to_all x1, blocking collectives, shards(): lax.all_to_all(packed, DP_SEQ, split_axis=1, concat_axis=0, tiled=True)  25.5 us
    all_to_all x2, starting transfers between devices, sent_and_summed(): lax.all_to_all(in_blocks(array, dim, count), axis, 0, 0, tiled=True)  12.4 us
    unnamed x46, local copies, waits for them, and re-layouts  6.94 us
  transfers between devices with their start and end apart: 6, of which 6 were waited for; matrix products, arithmetic and copies ran while one was open for 1% of the time, Pallas kernels for 0%

profile of v8, /device:TPU:1, one launch (start us, length us, event | category | flops | bytes accessed | tf_op | source)
XLA Modules:
  0.0 265.5 jit_solution(13708273359047727959)
XLA Ops:
  0.7 0.8 convert_bitcast_fusion.2
  1.4 0.8 concatenate.17
  3.1 2.2 reduce.23
  5.4 0.9 reshape.586
  6.3 16.8 %all-to-all-start = ((bf16[32,2,2112]{2,1,0:T(2,128)(2,1)}), bf16[32,2,2112]{2,1,0:T(2,128)(2,1)S(1)}, u32[]{:S(2)}, u32[]{:S(2)}) async-start(bf16[32,2,2112]{2,1,0:T(2,128)(2,1)} %reshape.586), calls=%async_computation | async-start | bytes 557056 | tf_op jit(solution)/shard_map/all_to_all | solution.py:29
  23.6 19.0 %all-to-all-done = bf16[32,2,2112]{2,1,0:T(2,128)(2,1)S(1)} async-done(((bf16[32,2,2112]{2,1,0:T(2,128)(2,1)}), bf16[32,2,2112]{2,1,0:T(2,128)(2,1)S(1)}, u32[]{:S(2)}, u32[]{:S(2)}) %all-to-all-start) | async-done | bytes 270368 | tf_op jit(solution)/shard_map/all_to_all | solution.py:29
  45.7 2.2 reduce.24
  48.2 25.5 %all_to_all.54 = bf16[32,2,2112]{2,1,0:T(2,128)(2,1)S(1)} all-to-all(bf16[32,2,2112]{2,1,0:T(2,128)(2,1)S(1)} %reshape.588), channel_id=1, replica_groups=mesh['dp'=8,'seq_0'=2,'seq_1'=2,'expert_0'=4,'expert_1'=4] {'dp','seq_0'..., dimensions={0} | all-to-all | bytes 540672 | tf_op jit(solution)/shard_map/all_to_all | solution.py:159
  74.0 1.5 bitcast_reduce_fusion
  78.0 0.7 reshape.590
  78.7 6.1 %all-to-all-start.2 = ((bf16[32,2,1024]{2,1,0:T(2,128)(2,1)}), bf16[32,2,1024]{2,1,0:T(2,128)(2,1)S(1)}, u32[]{:S(2)}, u32[]{:S(2)}) async-start(bf16[32,2,1024]{2,1,0:T(2,128)(2,1)} %reshape.590), calls=%async_computation.2 | async-start | bytes 262144 | tf_op jit(solution)/shard_map/all_to_all | solution.py:44
  84.9 15.2 %all-to-all-done.2 = bf16[32,2,1024]{2,1,0:T(2,128)(2,1)S(1)} async-done(((bf16[32,2,1024]{2,1,0:T(2,128)(2,1)}), bf16[32,2,1024]{2,1,0:T(2,128)(2,1)S(1)}, u32[]{:S(2)}, u32[]{:S(2)}) %all-to-all-start.2) | async-done | bytes 131104 | tf_op jit(solution)/shard_map/all_to_all | solution.py:44
  102.0 1.4 reduce.26
  103.4 0.7 reshape.592
  104.1 4.2 %all-to-all-start.3 = ((bf16[32,2,1024]{2,1,0:T(2,128)(2,1)}), bf16[32,2,1024]{2,1,0:T(2,128)(2,1)S(1)}, u32[]{:S(2)}, u32[]{:S(2)}) async-start(bf16[32,2,1024]{2,1,0:T(2,128)(2,1)} %reshape.592), calls=%async_computation.3 | async-start | bytes 262144 | tf_op jit(solution)/shard_map/all_to_all | solution.py:29
  108.5 15.1 %all-to-all-done.3 = bf16[32,2,1024]{2,1,0:T(2,128)(2,1)S(1)} async-done(((bf16[32,2,1024]{2,1,0:T(2,128)(2,1)}), bf16[32,2,1024]{2,1,0:T(2,128)(2,1)S(1)}, u32[]{:S(2)}, u32[]{:S(2)}) %all-to-all-start.3) | async-done | bytes 131104 | tf_op jit(solution)/shard_map/all_to_all | solution.py:29
  125.3 23.3 %all_to_all.55 = bf16[16,16,2048]{2,1,0:T(8,128)(2,1)S(1)} all-to-all(bf16[16,16,2048]{2,1,0:T(8,128)(2,1)S(1)} %bitcast.144), channel_id=1, replica_groups=mesh['dp'=8,'seq_0'=2,'seq_1'=2,'expert_0'=4,'expert_1'=4] {'expert_0','..., dimensions={0} | all-to-all | bytes 2097152 | tf_op jit(solution)/shard_map/all_to_all | solution.py:57
  150.7 18.8 %all_to_all.56 = bf16[16,16,2048]{2,1,0:T(8,128)(2,1)S(1)} all-to-all(bf16[16,16,2048]{2,1,0:T(8,128)(2,1)S(1)} %bitcast.146), channel_id=1, replica_groups=mesh['dp'=8,'seq_0'=2,'seq_1'=2,'expert_0'=4,'expert_1'=4] {'expert_0','..., dimensions={0} | all-to-all | bytes 2097152 | tf_op jit(solution)/shard_map/all_to_all | solution.py:57
  170.8 0.7 reshape.594
  171.5 6.3 %all-to-all-start.6 = ((bf16[32,2,1024]{2,1,0:T(2,128)(2,1)}), bf16[32,2,1024]{2,1,0:T(2,128)(2,1)S(1)}, u32[]{:S(2)}, u32[]{:S(2)}) async-start(bf16[32,2,1024]{2,1,0:T(2,128)(2,1)} %reshape.594), calls=%async_computation.6 | async-start | bytes 262144 | tf_op jit(solution)/shard_map/all_to_all | solution.py:44
  178.5 14.6 %all-to-all-done.6 = bf16[32,2,1024]{2,1,0:T(2,128)(2,1)S(1)} async-done(((bf16[32,2,1024]{2,1,0:T(2,128)(2,1)}), bf16[32,2,1024]{2,1,0:T(2,128)(2,1)S(1)}, u32[]{:S(2)}, u32[]{:S(2)}) %all-to-all-start.6) | async-done | bytes 131104 | tf_op jit(solution)/shard_map/all_to_all | solution.py:44
  197.6 1.4 reduce.28
  199.0 0.7 reshape.596
  199.7 4.2 %all-to-all-start.7 = ((bf16[32,2,1024]{2,1,0:T(2,128)(2,1)}), bf16[32,2,1024]{2,1,0:T(2,128)(2,1)S(1)}, u32[]{:S(2)}, u32[]{:S(2)}) async-start(bf16[32,2,1024]{2,1,0:T(2,128)(2,1)} %reshape.596), calls=%async_computation.7 | async-start | bytes 262144 | tf_op jit(solution)/shard_map/all_to_all | solution.py:29
  208.9 10.3 %all-to-all-done.7 = bf16[32,2,1024]{2,1,0:T(2,128)(2,1)S(1)} async-done(((bf16[32,2,1024]{2,1,0:T(2,128)(2,1)}), bf16[32,2,1024]{2,1,0:T(2,128)(2,1)S(1)}, u32[]{:S(2)}, u32[]{:S(2)}) %all-to-all-start.7) | async-done | bytes 131104 | tf_op jit(solution)/shard_map/all_to_all | solution.py:29
  220.2 0.7 reshape.598
  221.0 4.2 %all-to-all-start.8 = ((f32[32,1,288]{2,1,0:T(1,128)}), f32[32,1,288]{2,1,0:T(1,128)S(1)}, u32[]{:S(2)}, u32[]{:S(2)}) async-start(f32[32,1,288]{2,1,0:T(1,128)} %reshape.598), calls=%async_computation.8 | async-start | bytes 98304 | tf_op jit(solution)/shard_map/all_to_all | solution.py:29
  225.1 1.0 convolution_convert_fusion.1
  226.2 11.7 %all-to-all-done.8 = f32[32,1,288]{2,1,0:T(1,128)S(1)} async-done(((f32[32,1,288]{2,1,0:T(1,128)}), f32[32,1,288]{2,1,0:T(1,128)S(1)}, u32[]{:S(2)}, u32[]{:S(2)}) %all-to-all-start.8) | async-done | bytes 36896 | tf_op jit(solution)/shard_map/all_to_all | solution.py:29
  238.4 0.8 reduce.29
  242.2 20.6 %all_to_all.57 = bf16[16,16,2176]{2,1,0:T(8,128)(2,1)S(1)} all-to-all(bf16[16,16,2176]{2,1,0:T(8,128)(2,1)S(1)} %pad_maximum_fusion), channel_id=1, replica_groups=mesh['dp'=8,'seq_0'=2,'seq_1'=2,'expert_0'=4,'expert_1'=4] {'expert_0','..., dimensions={0} | all-to-all | bytes 2228224 | tf_op jit(solution)/shard_map/all_to_all | solution.py:57
  264.2 1.3 fusion
  (141 shorter events, 21.6 us)
Async XLA Ops:
  0.6 149.6 %copy-start = (bf16[1,192,2048]{2,1,0:T(8,128)(2,1)S(1)}, bf16[1,192,2048]{2,1,0:T(8,128)(2,1)}, u32[]{:S(2)}) copy-start(bf16[1,192,2048]{2,1,0:T(8,128)(2,1)} %param.24) | copy-start | bytes 2359300
  2.3 20.8 %copy-start.10 = (s32[1,8]{1,0:T(1,128)S(1)}, s32[1,8]{1,0:T(1,128)}, u32[]{:S(2)}) copy-start(s32[1,8]{1,0:T(1,128)} %param.29) | copy-start | bytes 100
  2.3 21.0 %copy-start.5 = (bf16[1,128,512]{2,1,0:T(8,128)(2,1)S(1)}, bf16[1,128,512]{2,1,0:T(8,128)(2,1)}, u32[]{:S(2)}) copy-start(bf16[1,128,512]{2,1,0:T(8,128)(2,1)} %param.16) | copy-start | bytes 393220
  2.6 20.8 %copy-start.9 = (s32[1,32]{1,0:T(1,128)S(1)}, s32[1,32]{1,0:T(1,128)}, u32[]{:S(2)}) copy-start(s32[1,32]{1,0:T(1,128)} %param.27) | copy-start | bytes 388
  6.3 36.3 %all-to-all-start = ((bf16[32,2,2112]{2,1,0:T(2,128)(2,1)}), bf16[32,2,2112]{2,1,0:T(2,128)(2,1)S(1)}, u32[]{:S(2)}, u32[]{:S(2)}) async-start(bf16[32,2,2112]{2,1,0:T(2,128)(2,1)} %reshape.586), calls=%async_computation | async-start | bytes 557056 | tf_op jit(solution)/shard_map/all_to_all | solution.py:29
  23.6 19.5 %copy-start.4 = (bf16[1,128,512]{2,1,0:T(8,128)(2,1)S(1)}, bf16[1,128,512]{2,1,0:T(8,128)(2,1)}, u32[]{:S(2)}) copy-start(bf16[1,128,512]{2,1,0:T(8,128)(2,1)} %param.15) | copy-start | bytes 393220
  74.0 3.0 %copy-start.2 = (bf16[128,2048]{1,0:T(8,128)(2,1)S(1)}, bf16[128,2048]{1,0:T(8,128)(2,1)}, u32[]{:S(2)}) copy-start(bf16[128,2048]{1,0:T(8,128)(2,1)} %param.19) | copy-start | bytes 1572868
  75.7 9.2 %copy-start.7 = (bf16[1,1,2048]{2,1,0:T(2,128)(2,1)S(1)}, bf16[1,1,2048]{2,1,0:T(2,128)(2,1)}, u32[]{:S(2)}) copy-start(bf16[1,1,2048]{2,1,0:T(2,128)(2,1)} %param.18) | copy-start | bytes 12292
  76.8 25.0 %copy-start.8 = (bf16[2048]{0:T(1024)(128)(2,1)S(1)}, bf16[2048]{0:T(1024)(128)(2,1)}, u32[]{:S(2)}) copy-start(bf16[2048]{0:T(1024)(128)(2,1)} %param.20) | copy-start | bytes 12292
  78.7 21.4 %all-to-all-start.2 = ((bf16[32,2,1024]{2,1,0:T(2,128)(2,1)}), bf16[32,2,1024]{2,1,0:T(2,128)(2,1)S(1)}, u32[]{:S(2)}, u32[]{:S(2)}) async-start(bf16[32,2,1024]{2,1,0:T(2,128)(2,1)} %reshape.590), calls=%async_computation.2 | async-start | bytes 262144 | tf_op jit(solution)/shard_map/all_to_all | solution.py:44
  100.3 23.4 %copy-start.3 = (bf16[2048,128]{1,0:T(8,128)(2,1)S(1)}, bf16[2048,128]{1,0:T(8,128)(2,1)}, u32[]{:S(2)}) copy-start(bf16[2048,128]{1,0:T(8,128)(2,1)} %param.21) | copy-start | bytes 1572868
  104.1 19.5 %all-to-all-start.3 = ((bf16[32,2,1024]{2,1,0:T(2,128)(2,1)}), bf16[32,2,1024]{2,1,0:T(2,128)(2,1)S(1)}, u32[]{:S(2)}, u32[]{:S(2)}) async-start(bf16[32,2,1024]{2,1,0:T(2,128)(2,1)} %reshape.592), calls=%async_computation.3 | async-start | bytes 262144 | tf_op jit(solution)/shard_map/all_to_all | solution.py:29
  125.3 23.3 %copy-start.1 = (bf16[1,2048,192]{1,2,0:T(8,128)(2,1)S(1)}, bf16[1,2048,192]{1,2,0:T(8,128)(2,1)}, u32[]{:S(2)}) copy-start(bf16[1,2048,192]{1,2,0:T(8,128)(2,1)} %param.22) | copy-start | bytes 2359300
  148.6 1.1 copy-start.11
  169.5 25.3 %copy-start.6 = (bf16[2048]{0:T(1024)(128)(2,1)S(1)}, bf16[2048]{0:T(1024)(128)(2,1)}, u32[]{:S(2)}) copy-start(bf16[2048]{0:T(1024)(128)(2,1)} %param.25) | copy-start | bytes 12292
  171.5 21.6 %all-to-all-start.6 = ((bf16[32,2,1024]{2,1,0:T(2,128)(2,1)}), bf16[32,2,1024]{2,1,0:T(2,128)(2,1)S(1)}, u32[]{:S(2)}, u32[]{:S(2)}) async-start(bf16[32,2,1024]{2,1,0:T(2,128)(2,1)} %reshape.594), calls=%async_computation.6 | async-start | bytes 262144 | tf_op jit(solution)/shard_map/all_to_all | solution.py:44
  199.7 19.5 %all-to-all-start.7 = ((bf16[32,2,1024]{2,1,0:T(2,128)(2,1)}), bf16[32,2,1024]{2,1,0:T(2,128)(2,1)S(1)}, u32[]{:S(2)}, u32[]{:S(2)}) async-start(bf16[32,2,1024]{2,1,0:T(2,128)(2,1)} %reshape.596), calls=%async_computation.7 | async-start | bytes 262144 | tf_op jit(solution)/shard_map/all_to_all | solution.py:29
  221.0 16.9 %all-to-all-start.8 = ((f32[32,1,288]{2,1,0:T(1,128)}), f32[32,1,288]{2,1,0:T(1,128)S(1)}, u32[]{:S(2)}, u32[]{:S(2)}) async-start(f32[32,1,288]{2,1,0:T(1,128)} %reshape.598), calls=%async_computation.8 | async-start | bytes 98304 | tf_op jit(solution)/shard_map/all_to_all | solution.py:29

commit v9 on v8

--- a/solution.py
+++ b/solution.py
@@ -105,11 +105,11 @@
         [
             queries[0],
             own_routes.astype(jnp.bfloat16)[None, :],
-            jnp.zeros((1, HEAD_WIDTH - own_routes.shape[0]), jnp.bfloat16),
+            jnp.zeros((1, 2 * HEAD_WIDTH - own_routes.shape[0]), jnp.bfloat16),
         ],
         axis=1,
     )
-    query_rows = gather_directly(query_row, DP_SEQ, 0)
+    query_rows = from_everyone(query_row.reshape(2, -1), DP_SEQ).reshape(lax.axis_size(DP_SEQ), -1)
     query_all = query_rows[:, :query_width]
     pack_routes = query_rows[:, query_width : query_width + routes.shape[2]].astype(jnp.int32)
     positions = step_pos[0]
@@ -154,10 +154,11 @@
     totals_hi, totals_lo = split_pair(totals)
     stats = jnp.stack([totals_hi, totals_lo, shift, jnp.zeros_like(shift)], axis=-1)
     stats = jnp.swapaxes(stats, 0, 1).reshape(QUERY_HEADS, 1, -1)
-    packed = jnp.concatenate([weighted.astype(jnp.bfloat16), stats], axis=1)
-    packed = packed.reshape(1, QUERY_HEADS, -1)
-    arrived = lax.all_to_all(packed, DP_SEQ, split_axis=1, concat_axis=0, tiled=True)
-    arrived = arrived.reshape(arrived.shape[0], number_of_steps + 1, 1, HEAD_WIDTH)
+    filler = jnp.zeros((QUERY_HEADS, 1, HEAD_WIDTH), jnp.bfloat16)
+    packed = jnp.concatenate([weighted.astype(jnp.bfloat16), stats, filler], axis=1)
+    packed = packed.reshape(QUERY_HEADS, 2, -1)
+    arrived = lax.all_to_all(packed, DP_SEQ, split_axis=0, concat_axis=0, tiled=True)
+    arrived = arrived.reshape(arrived.shape[0], number_of_steps + 2, 1, HEAD_WIDTH)
     got_stats = arrived[:, number_of_steps].reshape(arrived.shape[0], number_of_steps, 1, 4)
     attn = merge_heads(
         arrived[:, :number_of_steps].astype(jnp.float32),

time: 266 us -> 260 us (0.977)
  other arithmetic: 19.7 us -> 16 us
    unnamed x46 -> x40, local copies, waits for them, and re-layouts: 6.94 us -> 5.19 us
  transfers between devices with their start and end apart: 6 -> 6, of which waited for: 6 -> 6; matrix products, arithmetic and copies ran while one was open for 1% -> 2% of each run, Pallas kernels for 0% -> 0%
where the time goes in v9:
time: 260 us; the launch traced here: 259 us
  blocking collectives  88.3 us (34%)
  waiting for transfers between devices  84.3 us (32%)
  starting transfers between devices  41.8 us (16%)
  other arithmetic  16 us (6%)
  local copies, waits for them, and re-layouts  11.1 us (4%)
  between operations  10.1 us (4%)
  matrix products  7.04 us (3%)
    all_to_all x3, blocking collectives, across_group(): lax.all_to_all(buffer, EXPERT, split_axis=0, concat_axis=0, tiled=True)  62.7 us
    all_to_all x4, waiting for transfers between devices, from_everyone(): return lax.all_to_all(copies, axis, split_axis=0, concat_axis=0, tiled=True)  54.4 us
    all_to_all x2, waiting for transfers between devices, sent_and_summed(): lax.all_to_all(in_blocks(array, dim, count), axis, 0, 0, tiled=True)  29.9 us
    all_to_all x4, starting transfers between devices, from_everyone(): return lax.all_to_all(copies, axis, split_axis=0, concat_axis=0, tiled=True)  29.4 us
    all_to_all x1, blocking collectives, shards(): lax.all_to_all(packed, DP_SEQ, split_axis=0, concat_axis=0, tiled=True)  25.7 us
    all_to_all x2, starting transfers between devices, sent_and_summed(): lax.all_to_all(in_blocks(array, dim, count), axis, 0, 0, tiled=True)  12.4 us
  transfers between devices with their start and end apart: 6, of which 6 were waited for; matrix products, arithmetic and copies ran while one was open for 2% of the time, Pallas kernels for 0%

profile of v9, /device:TPU:1, one launch (start us, length us, event | category | flops | bytes accessed | tf_op | source)
XLA Modules:
  0.0 258.6 jit_solution(7278934740603635926)
XLA Ops:
  0.7 0.8 convert_bitcast_fusion.2
  1.4 0.8 concatenate.15
  2.3 0.9 broadcast_in_dim.122
  3.2 16.9 %all-to-all-start = ((bf16[32,2,2176]{2,1,0:T(2,128)(2,1)}), bf16[32,2,2176]{2,1,0:T(2,128)(2,1)S(1)}, u32[]{:S(2)}, u32[]{:S(2)}) async-start(bf16[32,2,2176]{2,1,0:T(2,128)(2,1)} %broadcast_in_dim.122), calls=%async_computation | async-start | bytes 557056 | tf_op jit(solution)/shard_map/all_to_all | solution.py:29
  20.2 0.8 reduce-window.8
  21.1 0.9 reshape_squeeze.6
  22.3 17.4 %all-to-all-done = bf16[32,2,2176]{2,1,0:T(2,128)(2,1)S(1)} async-done(((bf16[32,2,2176]{2,1,0:T(2,128)(2,1)}), bf16[32,2,2176]{2,1,0:T(2,128)(2,1)S(1)}, u32[]{:S(2)}, u32[]{:S(2)}) %all-to-all-start) | async-done | bytes 278560 | tf_op jit(solution)/shard_map/all_to_all | solution.py:29
  42.4 25.7 %all_to_all.50 = bf16[32,2,2176]{2,1,0:T(2,128)(2,1)S(1)} all-to-all(bf16[32,2,2176]{2,1,0:T(2,128)(2,1)S(1)} %reshape.560), channel_id=1, replica_groups=mesh['dp'=8,'seq_0'=2,'seq_1'=2,'expert_0'=4,'expert_1'=4] {'dp','seq_0'..., dimensions={0} | all-to-all | bytes 557056 | tf_op jit(solution)/shard_map/all_to_all | solution.py:160
  71.1 0.7 reshape.584
  71.8 6.1 %all-to-all-start.2 = ((bf16[32,2,1024]{2,1,0:T(2,128)(2,1)}), bf16[32,2,1024]{2,1,0:T(2,128)(2,1)S(1)}, u32[]{:S(2)}, u32[]{:S(2)}) async-start(bf16[32,2,1024]{2,1,0:T(2,128)(2,1)} %reshape.584), calls=%async_computation.2 | async-start | bytes 262144 | tf_op jit(solution)/shard_map/all_to_all | solution.py:44
  78.0 15.2 %all-to-all-done.2 = bf16[32,2,1024]{2,1,0:T(2,128)(2,1)S(1)} async-done(((bf16[32,2,1024]{2,1,0:T(2,128)(2,1)}), bf16[32,2,1024]{2,1,0:T(2,128)(2,1)S(1)}, u32[]{:S(2)}, u32[]{:S(2)}) %all-to-all-start.2) | async-done | bytes 131104 | tf_op jit(solution)/shard_map/all_to_all | solution.py:44
  95.1 1.4 reduce.22
  96.5 0.7 reshape.586
  97.2 4.2 %all-to-all-start.3 = ((bf16[32,2,1024]{2,1,0:T(2,128)(2,1)}), bf16[32,2,1024]{2,1,0:T(2,128)(2,1)S(1)}, u32[]{:S(2)}, u32[]{:S(2)}) async-start(bf16[32,2,1024]{2,1,0:T(2,128)(2,1)} %reshape.586), calls=%async_computation.3 | async-start | bytes 262144 | tf_op jit(solution)/shard_map/all_to_all | solution.py:29
  101.6 15.1 %all-to-all-done.3 = bf16[32,2,1024]{2,1,0:T(2,128)(2,1)S(1)} async-done(((bf16[32,2,1024]{2,1,0:T(2,128)(2,1)}), bf16[32,2,1024]{2,1,0:T(2,128)(2,1)S(1)}, u32[]{:S(2)}, u32[]{:S(2)}) %all-to-all-start.3) | async-done | bytes 131104 | tf_op jit(solution)/shard_map/all_to_all | solution.py:29
  118.4 23.3 %all_to_all.51 = bf16[16,16,2048]{2,1,0:T(8,128)(2,1)S(1)} all-to-all(bf16[16,16,2048]{2,1,0:T(8,128)(2,1)S(1)} %bitcast.141), channel_id=1, replica_groups=mesh['dp'=8,'seq_0'=2,'seq_1'=2,'expert_0'=4,'expert_1'=4] {'expert_0','..., dimensions={0} | all-to-all | bytes 2097152 | tf_op jit(solution)/shard_map/all_to_all | solution.py:57
  143.8 18.8 %all_to_all.52 = bf16[16,16,2048]{2,1,0:T(8,128)(2,1)S(1)} all-to-all(bf16[16,16,2048]{2,1,0:T(8,128)(2,1)S(1)} %bitcast.143), channel_id=1, replica_groups=mesh['dp'=8,'seq_0'=2,'seq_1'=2,'expert_0'=4,'expert_1'=4] {'expert_0','..., dimensions={0} | all-to-all | bytes 2097152 | tf_op jit(solution)/shard_map/all_to_all | solution.py:57
  163.9 0.7 reshape.588
  164.6 6.3 %all-to-all-start.6 = ((bf16[32,2,1024]{2,1,0:T(2,128)(2,1)}), bf16[32,2,1024]{2,1,0:T(2,128)(2,1)S(1)}, u32[]{:S(2)}, u32[]{:S(2)}) async-start(bf16[32,2,1024]{2,1,0:T(2,128)(2,1)} %reshape.588), calls=%async_computation.6 | async-start | bytes 262144 | tf_op jit(solution)/shard_map/all_to_all | solution.py:44
  171.6 14.6 %all-to-all-done.6 = bf16[32,2,1024]{2,1,0:T(2,128)(2,1)S(1)} async-done(((bf16[32,2,1024]{2,1,0:T(2,128)(2,1)}), bf16[32,2,1024]{2,1,0:T(2,128)(2,1)S(1)}, u32[]{:S(2)}, u32[]{:S(2)}) %all-to-all-start.6) | async-done | bytes 131104 | tf_op jit(solution)/shard_map/all_to_all | solution.py:44
  190.7 1.4 reduce.24
  192.1 0.7 reshape.590
  192.8 4.2 %all-to-all-start.7 = ((bf16[32,2,1024]{2,1,0:T(2,128)(2,1)}), bf16[32,2,1024]{2,1,0:T(2,128)(2,1)S(1)}, u32[]{:S(2)}, u32[]{:S(2)}) async-start(bf16[32,2,1024]{2,1,0:T(2,128)(2,1)} %reshape.590), calls=%async_computation.7 | async-start | bytes 262144 | tf_op jit(solution)/shard_map/all_to_all | solution.py:29
  197.0 0.7 reduce.20
  202.0 10.3 %all-to-all-done.7 = bf16[32,2,1024]{2,1,0:T(2,128)(2,1)S(1)} async-done(((bf16[32,2,1024]{2,1,0:T(2,128)(2,1)}), bf16[32,2,1024]{2,1,0:T(2,128)(2,1)S(1)}, u32[]{:S(2)}, u32[]{:S(2)}) %all-to-all-start.7) | async-done | bytes 131104 | tf_op jit(solution)/shard_map/all_to_all | solution.py:29
  213.3 0.7 reshape.592
  214.1 4.2 %all-to-all-start.8 = ((f32[32,1,288]{2,1,0:T(1,128)}), f32[32,1,288]{2,1,0:T(1,128)S(1)}, u32[]{:S(2)}, u32[]{:S(2)}) async-start(f32[32,1,288]{2,1,0:T(1,128)} %reshape.592), calls=%async_computation.8 | async-start | bytes 98304 | tf_op jit(solution)/shard_map/all_to_all | solution.py:29
  218.2 1.0 convolution_convert_fusion.1
  219.3 11.7 %all-to-all-done.8 = f32[32,1,288]{2,1,0:T(1,128)S(1)} async-done(((f32[32,1,288]{2,1,0:T(1,128)}), f32[32,1,288]{2,1,0:T(1,128)S(1)}, u32[]{:S(2)}, u32[]{:S(2)}) %all-to-all-start.8) | async-done | bytes 36896 | tf_op jit(solution)/shard_map/all_to_all | solution.py:29
  231.5 0.8 reduce.25
  235.3 20.6 %all_to_all.53 = bf16[16,16,2176]{2,1,0:T(8,128)(2,1)S(1)} all-to-all(bf16[16,16,2176]{2,1,0:T(8,128)(2,1)S(1)} %pad_maximum_fusion), channel_id=1, replica_groups=mesh['dp'=8,'seq_0'=2,'seq_1'=2,'expert_0'=4,'expert_1'=4] {'expert_0','..., dimensions={0} | all-to-all | bytes 2228224 | tf_op jit(solution)/shard_map/all_to_all | solution.py:57
  257.3 1.3 fusion
  (134 shorter events, 19.7 us)
Async XLA Ops:
  0.6 142.7 %copy-start = (bf16[1,192,2048]{2,1,0:T(8,128)(2,1)S(1)}, bf16[1,192,2048]{2,1,0:T(8,128)(2,1)}, u32[]{:S(2)}) copy-start(bf16[1,192,2048]{2,1,0:T(8,128)(2,1)} %param.24) | copy-start | bytes 2359300
  0.6 21.4 %copy-start.9 = (s32[1,8]{1,0:T(1,128)S(1)}, s32[1,8]{1,0:T(1,128)}, u32[]{:S(2)}) copy-start(s32[1,8]{1,0:T(1,128)} %param.29) | copy-start | bytes 100
  0.7 21.4 %copy-start.8 = (s32[1,32]{1,0:T(1,128)S(1)}, s32[1,32]{1,0:T(1,128)}, u32[]{:S(2)}) copy-start(s32[1,32]{1,0:T(1,128)} %param.27) | copy-start | bytes 388
  3.2 36.6 %copy-start.4 = (bf16[1,128,512]{2,1,0:T(8,128)(2,1)S(1)}, bf16[1,128,512]{2,1,0:T(8,128)(2,1)}, u32[]{:S(2)}) copy-start(bf16[1,128,512]{2,1,0:T(8,128)(2,1)} %param.15) | copy-start | bytes 393220
  3.2 36.5 %all-to-all-start = ((bf16[32,2,2176]{2,1,0:T(2,128)(2,1)}), bf16[32,2,2176]{2,1,0:T(2,128)(2,1)S(1)}, u32[]{:S(2)}, u32[]{:S(2)}) async-start(bf16[32,2,2176]{2,1,0:T(2,128)(2,1)} %broadcast_in_dim.122), calls=%async_computation | async-start | bytes 557056 | tf_op jit(solution)/shard_map/all_to_all | solution.py:29
  42.3 27.3 %copy-start.2 = (bf16[128,2048]{1,0:T(8,128)(2,1)S(1)}, bf16[128,2048]{1,0:T(8,128)(2,1)}, u32[]{:S(2)}) copy-start(bf16[128,2048]{1,0:T(8,128)(2,1)} %param.19) | copy-start | bytes 1572868
  68.3 9.7 %copy-start.6 = (bf16[1,1,2048]{2,1,0:T(2,128)(2,1)S(1)}, bf16[1,1,2048]{2,1,0:T(2,128)(2,1)}, u32[]{:S(2)}) copy-start(bf16[1,1,2048]{2,1,0:T(2,128)(2,1)} %param.18) | copy-start | bytes 12292
  69.4 25.5 %copy-start.7 = (bf16[2048]{0:T(1024)(128)(2,1)S(1)}, bf16[2048]{0:T(1024)(128)(2,1)}, u32[]{:S(2)}) copy-start(bf16[2048]{0:T(1024)(128)(2,1)} %param.20) | copy-start | bytes 12292
  71.8 21.4 %all-to-all-start.2 = ((bf16[32,2,1024]{2,1,0:T(2,128)(2,1)}), bf16[32,2,1024]{2,1,0:T(2,128)(2,1)S(1)}, u32[]{:S(2)}, u32[]{:S(2)}) async-start(bf16[32,2,1024]{2,1,0:T(2,128)(2,1)} %reshape.584), calls=%async_computation.2 | async-start | bytes 262144 | tf_op jit(solution)/shard_map/all_to_all | solution.py:44
  93.4 23.4 %copy-start.3 = (bf16[2048,128]{1,0:T(8,128)(2,1)S(1)}, bf16[2048,128]{1,0:T(8,128)(2,1)}, u32[]{:S(2)}) copy-start(bf16[2048,128]{1,0:T(8,128)(2,1)} %param.21) | copy-start | bytes 1572868
  97.2 19.5 %all-to-all-start.3 = ((bf16[32,2,1024]{2,1,0:T(2,128)(2,1)}), bf16[32,2,1024]{2,1,0:T(2,128)(2,1)S(1)}, u32[]{:S(2)}, u32[]{:S(2)}) async-start(bf16[32,2,1024]{2,1,0:T(2,128)(2,1)} %reshape.586), calls=%async_computation.3 | async-start | bytes 262144 | tf_op jit(solution)/shard_map/all_to_all | solution.py:29
  118.4 23.3 %copy-start.1 = (bf16[1,2048,192]{1,2,0:T(8,128)(2,1)S(1)}, bf16[1,2048,192]{1,2,0:T(8,128)(2,1)}, u32[]{:S(2)}) copy-start(bf16[1,2048,192]{1,2,0:T(8,128)(2,1)} %param.22) | copy-start | bytes 2359300
  141.7 1.1 copy-start.10
  162.6 25.3 %copy-start.5 = (bf16[2048]{0:T(1024)(128)(2,1)S(1)}, bf16[2048]{0:T(1024)(128)(2,1)}, u32[]{:S(2)}) copy-start(bf16[2048]{0:T(1024)(128)(2,1)} %param.25) | copy-start | bytes 12292
  164.6 21.6 %all-to-all-start.6 = ((bf16[32,2,1024]{2,1,0:T(2,128)(2,1)}), bf16[32,2,1024]{2,1,0:T(2,128)(2,1)S(1)}, u32[]{:S(2)}, u32[]{:S(2)}) async-start(bf16[32,2,1024]{2,1,0:T(2,128)(2,1)} %reshape.588), calls=%async_computation.6 | async-start | bytes 262144 | tf_op jit(solution)/shard_map/all_to_all | solution.py:44
  192.8 19.5 %all-to-all-start.7 = ((bf16[32,2,1024]{2,1,0:T(2,128)(2,1)}), bf16[32,2,1024]{2,1,0:T(2,128)(2,1)S(1)}, u32[]{:S(2)}, u32[]{:S(2)}) async-start(bf16[32,2,1024]{2,1,0:T(2,128)(2,1)} %reshape.590), calls=%async_computation.7 | async-start | bytes 262144 | tf_op jit(solution)/shard_map/all_to_all | solution.py:29
  214.1 16.9 %all-to-all-start.8 = ((f32[32,1,288]{2,1,0:T(1,128)}), f32[32,1,288]{2,1,0:T(1,128)S(1)}, u32[]{:S(2)}, u32[]{:S(2)}) async-start(f32[32,1,288]{2,1,0:T(1,128)} %reshape.592), calls=%async_computation.8 | async-start | bytes 98304 | tf_op jit(solution)/shard_map/all_to_all | solution.py:29

commit v10 on v9

--- a/solution.py
+++ b/solution.py
@@ -43,6 +43,16 @@
     count = lax.axis_size(axis)
     blocks = lax.all_to_all(in_blocks(array, dim, count), axis, 0, 0, tiled=True)
     return jnp.sum(blocks.astype(jnp.float32), axis=0)
+
+
+def rows_summed(array, axis):
+    count = lax.axis_size(axis)
+    blocks = lax.all_to_all(array.reshape(count, 2, -1), axis, 0, 0, tiled=True)
+    return jnp.sum(blocks.astype(jnp.float32), axis=0).reshape(1, -1)
+
+
+def rows_gathered(row, axis):
+    return from_everyone(row.reshape(2, -1), axis).reshape(lax.axis_size(axis), -1)
 
 
 def rms_scale(stream):
@@ -165,14 +175,14 @@
         join_pair(got_stats[..., 0], got_stats[..., 1]),
         got_stats[..., 2].astype(jnp.float32),
     )
-    mixed = sent_and_summed(
-        jnp.dot(attn, out_proj, preferred_element_type=jnp.float32).astype(jnp.bfloat16), DP_SEQ, 0
+    mixed = rows_summed(
+        jnp.dot(attn, out_proj, preferred_element_type=jnp.float32).astype(jnp.bfloat16), DP_SEQ
     )
     stream = residual[0].astype(jnp.float32) + mixed
     normed = (stream * rms_scale(stream) * norm_gain.astype(jnp.float32)[None, :]).astype(
         jnp.bfloat16
     )
-    pack_normed = gather_directly(normed, DP_SEQ, 0)
+    pack_normed = rows_gathered(normed, DP_SEQ)
     rows = pack_normed.shape[0]
     width = pack_normed.shape[1]
     block_rows = routes.shape[1]
@@ -219,7 +229,7 @@
         (((1,), (0,)), ((), ())),
         precision=lax.Precision.HIGHEST,
     )
-    expert_mix = sent_and_summed(group_mix.astype(jnp.bfloat16), DP_SEQ, 0)
+    expert_mix = rows_summed(group_mix.astype(jnp.bfloat16), DP_SEQ)
     final = stream + expert_mix
     reward, pull = jax.vjp(lambda value: head_logit(value, head_vec), final)
     target = labels[0].astype(jnp.float32)
@@ -227,7 +237,7 @@
     logit_grad = jax.nn.sigmoid(reward) - target
     (final_grad,) = pull(logit_grad)
     d_mix = final_grad.astype(jnp.bfloat16)
-    pack_grads = gather_directly(d_mix, DP_SEQ, 0)
+    pack_grads = rows_gathered(d_mix, DP_SEQ)
     d_out = lax.dot_general(
         weight_map, pack_grads.astype(jnp.float32), contract_rows, precision=lax.Precision.HIGHEST
     ).astype(jnp.bfloat16)

time: 260 us -> 254 us (0.977)
  other arithmetic: 16 us -> 10.9 us
    unnamed x40 -> x34, local copies, waits for them, and re-layouts: 5.19 us -> 1.91 us
    broadcast_in_dim x2 -> x0, other arithmetic: 2.76 us -> none  [from_everyone(): copies = jnp.broadcast_to(array, (lax.axis_size(axis), *array.shape))]
  transfers between devices with their start and end apart: 6 -> 6, of which waited for: 6 -> 6; matrix products, arithmetic and copies ran while one was open for 2% -> 1% of each run, Pallas kernels for 0% -> 0%
where the time goes in v10:
time: 254 us; the launch traced here: 253 us
  blocking collectives  88.3 us (35%)
  waiting for transfers between devices  85 us (33%)
  starting transfers between devices  41.8 us (16%)
  other arithmetic  10.9 us (4%)
  local copies, waits for them, and re-layouts  9.99 us (4%)
  between operations  9.93 us (4%)
  matrix products  7.01 us (3%)
    all_to_all x3, blocking collectives, across_group(): lax.all_to_all(buffer, EXPERT, split_axis=0, concat_axis=0, tiled=True)  62.7 us
    all_to_all x4, waiting for transfers between devices, from_everyone(): return lax.all_to_all(copies, axis, split_axis=0, concat_axis=0, tiled=True)  55.2 us
    all_to_all x2, waiting for transfers between devices, rows_summed(): blocks = lax.all_to_all(array.reshape(count, 2, -1), axis, 0, 0, tiled=True)  29.9 us
    all_to_all x4, starting transfers between devices, from_everyone(): return lax.all_to_all(copies, axis, split_axis=0, concat_axis=0, tiled=True)  29.4 us
    all_to_all x1, blocking collectives, shards(): lax.all_to_all(packed, DP_SEQ, split_axis=0, concat_axis=0, tiled=True)  25.7 us
    all_to_all x2, starting transfers between devices, rows_summed(): blocks = lax.all_to_all(array.reshape(count, 2, -1), axis, 0, 0, tiled=True)  12.5 us
  transfers between devices with their start and end apart: 6, of which 6 were waited for; matrix products, arithmetic and copies ran while one was open for 1% of the time, Pallas kernels for 0%

profile of v10, /device:TPU:1, one launch (start us, length us, event | category | flops | bytes accessed | tf_op | source)
XLA Modules:
  0.0 253.1 jit_solution(15812918838539209269)
XLA Ops:
  0.7 0.8 convert_bitcast_fusion.2
  1.4 0.8 concatenate.15
  2.3 0.9 broadcast_in_dim.122
  3.2 16.9 %all-to-all-start = ((bf16[32,2,2176]{2,1,0:T(2,128)(2,1)}), bf16[32,2,2176]{2,1,0:T(2,128)(2,1)S(1)}, u32[]{:S(2)}, u32[]{:S(2)}) async-start(bf16[32,2,2176]{2,1,0:T(2,128)(2,1)} %broadcast_in_dim.122), calls=%async_computation | async-start | bytes 557056 | tf_op jit(solution)/shard_map/all_to_all | solution.py:29
  20.2 0.8 reduce-window.8
  21.1 0.9 reshape_squeeze.6
  22.3 17.4 %all-to-all-done = bf16[32,2,2176]{2,1,0:T(2,128)(2,1)S(1)} async-done(((bf16[32,2,2176]{2,1,0:T(2,128)(2,1)}), bf16[32,2,2176]{2,1,0:T(2,128)(2,1)S(1)}, u32[]{:S(2)}, u32[]{:S(2)}) %all-to-all-start) | async-done | bytes 278560 | tf_op jit(solution)/shard_map/all_to_all | solution.py:29
  42.4 25.7 %all_to_all.50 = bf16[32,2,2176]{2,1,0:T(2,128)(2,1)S(1)} all-to-all(bf16[32,2,2176]{2,1,0:T(2,128)(2,1)S(1)} %reshape.561), channel_id=1, replica_groups=mesh['dp'=8,'seq_0'=2,'seq_1'=2,'expert_0'=4,'expert_1'=4] {'dp','seq_0'..., dimensions={0} | all-to-all | bytes 557056 | tf_op jit(solution)/shard_map/all_to_all | solution.py:170
  69.9 0.8 reshape.563
  70.7 6.2 %all-to-all-start.2 = ((bf16[32,2,1024]{2,1,0:T(2,128)(2,1)}), bf16[32,2,1024]{2,1,0:T(2,128)(2,1)S(1)}, u32[]{:S(2)}, u32[]{:S(2)}) async-start(bf16[32,2,1024]{2,1,0:T(2,128)(2,1)} %reshape.563), calls=%async_computation.2 | async-start | bytes 262144 | tf_op jit(solution)/shard_map/all_to_all | solution.py:50
  76.9 15.2 %all-to-all-done.2 = bf16[32,2,1024]{2,1,0:T(2,128)(2,1)S(1)} async-done(((bf16[32,2,1024]{2,1,0:T(2,128)(2,1)}), bf16[32,2,1024]{2,1,0:T(2,128)(2,1)S(1)}, u32[]{:S(2)}, u32[]{:S(2)}) %all-to-all-start.2) | async-done | bytes 131104 | tf_op jit(solution)/shard_map/all_to_all | solution.py:50
  92.2 0.6 multiply_reduce_fusion.4
  93.6 0.7 broadcast_in_dim.130
  94.3 4.2 %all-to-all-start.3 = ((bf16[32,2,1024]{2,1,0:T(2,128)(2,1)}), bf16[32,2,1024]{2,1,0:T(2,128)(2,1)S(1)}, u32[]{:S(2)}, u32[]{:S(2)}) async-start(bf16[32,2,1024]{2,1,0:T(2,128)(2,1)} %broadcast_in_dim.130), calls=%async_computation.3 | async-start | bytes 262144 | tf_op jit(solution)/shard_map/all_to_all | solution.py:29
  98.7 15.1 %all-to-all-done.3 = bf16[32,2,1024]{2,1,0:T(2,128)(2,1)S(1)} async-done(((bf16[32,2,1024]{2,1,0:T(2,128)(2,1)}), bf16[32,2,1024]{2,1,0:T(2,128)(2,1)S(1)}, u32[]{:S(2)}, u32[]{:S(2)}) %all-to-all-start.3) | async-done | bytes 131104 | tf_op jit(solution)/shard_map/all_to_all | solution.py:29
  115.4 23.3 %all_to_all.51 = bf16[16,16,2048]{2,1,0:T(8,128)(2,1)S(1)} all-to-all(bf16[16,16,2048]{2,1,0:T(8,128)(2,1)S(1)} %bitcast.147), channel_id=1, replica_groups=mesh['dp'=8,'seq_0'=2,'seq_1'=2,'expert_0'=4,'expert_1'=4] {'expert_0','..., dimensions={0} | all-to-all | bytes 2097152 | tf_op jit(solution)/shard_map/all_to_all | solution.py:67
  140.8 18.8 %all_to_all.52 = bf16[16,16,2048]{2,1,0:T(8,128)(2,1)S(1)} all-to-all(bf16[16,16,2048]{2,1,0:T(8,128)(2,1)S(1)} %bitcast.149), channel_id=1, replica_groups=mesh['dp'=8,'seq_0'=2,'seq_1'=2,'expert_0'=4,'expert_1'=4] {'expert_0','..., dimensions={0} | all-to-all | bytes 2097152 | tf_op jit(solution)/shard_map/all_to_all | solution.py:67
  160.2 0.7 reshape.571
  161.0 6.3 %all-to-all-start.6 = ((bf16[32,2,1024]{2,1,0:T(2,128)(2,1)}), bf16[32,2,1024]{2,1,0:T(2,128)(2,1)S(1)}, u32[]{:S(2)}, u32[]{:S(2)}) async-start(bf16[32,2,1024]{2,1,0:T(2,128)(2,1)} %reshape.571), calls=%async_computation.6 | async-start | bytes 262144 | tf_op jit(solution)/shard_map/all_to_all | solution.py:50
  167.9 14.6 %all-to-all-done.6 = bf16[32,2,1024]{2,1,0:T(2,128)(2,1)S(1)} async-done(((bf16[32,2,1024]{2,1,0:T(2,128)(2,1)}), bf16[32,2,1024]{2,1,0:T(2,128)(2,1)S(1)}, u32[]{:S(2)}, u32[]{:S(2)}) %all-to-all-start.6) | async-done | bytes 131104 | tf_op jit(solution)/shard_map/all_to_all | solution.py:50
  182.7 0.6 multiply_reduce_fusion.3
  186.6 0.7 broadcast_in_dim.134
  187.3 4.2 %all-to-all-start.7 = ((bf16[32,2,1024]{2,1,0:T(2,128)(2,1)}), bf16[32,2,1024]{2,1,0:T(2,128)(2,1)S(1)}, u32[]{:S(2)}, u32[]{:S(2)}) async-start(bf16[32,2,1024]{2,1,0:T(2,128)(2,1)} %broadcast_in_dim.134), calls=%async_computation.7 | async-start | bytes 262144 | tf_op jit(solution)/shard_map/all_to_all | solution.py:29
  195.8 11.0 %all-to-all-done.7 = bf16[32,2,1024]{2,1,0:T(2,128)(2,1)S(1)} async-done(((bf16[32,2,1024]{2,1,0:T(2,128)(2,1)}), bf16[32,2,1024]{2,1,0:T(2,128)(2,1)S(1)}, u32[]{:S(2)}, u32[]{:S(2)}) %all-to-all-start.7) | async-done | bytes 131104 | tf_op jit(solution)/shard_map/all_to_all | solution.py:29
  207.8 0.7 reshape.588
  208.5 4.2 %all-to-all-start.8 = ((f32[32,1,288]{2,1,0:T(1,128)}), f32[32,1,288]{2,1,0:T(1,128)S(1)}, u32[]{:S(2)}, u32[]{:S(2)}) async-start(f32[32,1,288]{2,1,0:T(1,128)} %reshape.588), calls=%async_computation.8 | async-start | bytes 98304 | tf_op jit(solution)/shard_map/all_to_all | solution.py:29
  212.7 1.0 convolution_convert_fusion.1
  213.7 11.7 %all-to-all-done.8 = f32[32,1,288]{2,1,0:T(1,128)S(1)} async-done(((f32[32,1,288]{2,1,0:T(1,128)}), f32[32,1,288]{2,1,0:T(1,128)S(1)}, u32[]{:S(2)}, u32[]{:S(2)}) %all-to-all-start.8) | async-done | bytes 36896 | tf_op jit(solution)/shard_map/all_to_all | solution.py:29
  226.0 0.8 reduce.18
  229.8 20.6 %all_to_all.53 = bf16[16,16,2176]{2,1,0:T(8,128)(2,1)S(1)} all-to-all(bf16[16,16,2176]{2,1,0:T(8,128)(2,1)S(1)} %pad_maximum_fusion), channel_id=1, replica_groups=mesh['dp'=8,'seq_0'=2,'seq_1'=2,'expert_0'=4,'expert_1'=4] {'expert_0','..., dimensions={0} | all-to-all | bytes 2228224 | tf_op jit(solution)/shard_map/all_to_all | solution.py:67
  250.4 0.7 add_reduce_fusion.1
  251.8 1.3 fusion
  (128 shorter events, 15.1 us)
Async XLA Ops:
  0.6 139.7 %copy-start = (bf16[1,192,2048]{2,1,0:T(8,128)(2,1)S(1)}, bf16[1,192,2048]{2,1,0:T(8,128)(2,1)}, u32[]{:S(2)}) copy-start(bf16[1,192,2048]{2,1,0:T(8,128)(2,1)} %param.24) | copy-start | bytes 2359300
  0.6 21.4 %copy-start.9 = (s32[1,8]{1,0:T(1,128)S(1)}, s32[1,8]{1,0:T(1,128)}, u32[]{:S(2)}) copy-start(s32[1,8]{1,0:T(1,128)} %param.29) | copy-start | bytes 100
  0.7 21.4 %copy-start.8 = (s32[1,32]{1,0:T(1,128)S(1)}, s32[1,32]{1,0:T(1,128)}, u32[]{:S(2)}) copy-start(s32[1,32]{1,0:T(1,128)} %param.27) | copy-start | bytes 388
  3.2 36.6 %copy-start.4 = (bf16[1,128,512]{2,1,0:T(8,128)(2,1)S(1)}, bf16[1,128,512]{2,1,0:T(8,128)(2,1)}, u32[]{:S(2)}) copy-start(bf16[1,128,512]{2,1,0:T(8,128)(2,1)} %param.15) | copy-start | bytes 393220
  3.2 36.5 %all-to-all-start = ((bf16[32,2,2176]{2,1,0:T(2,128)(2,1)}), bf16[32,2,2176]{2,1,0:T(2,128)(2,1)S(1)}, u32[]{:S(2)}, u32[]{:S(2)}) async-start(bf16[32,2,2176]{2,1,0:T(2,128)(2,1)} %broadcast_in_dim.122), calls=%async_computation | async-start | bytes 557056 | tf_op jit(solution)/shard_map/all_to_all | solution.py:29
  42.3 27.3 %copy-start.2 = (bf16[128,2048]{1,0:T(8,128)(2,1)S(1)}, bf16[128,2048]{1,0:T(8,128)(2,1)}, u32[]{:S(2)}) copy-start(bf16[128,2048]{1,0:T(8,128)(2,1)} %param.19) | copy-start | bytes 1572868
  68.1 8.7 %copy-start.5 = (bf16[1,1,2048]{2,1,0:T(2,128)(2,1)S(1)}, bf16[1,1,2048]{2,1,0:T(2,128)(2,1)}, u32[]{:S(2)}) copy-start(bf16[1,1,2048]{2,1,0:T(2,128)(2,1)} %param.18) | copy-start | bytes 12292
  68.3 25.3 %copy-start.7 = (bf16[2048]{0:T(1024)(128)(2,1)S(1)}, bf16[2048]{0:T(1024)(128)(2,1)}, u32[]{:S(2)}) copy-start(bf16[2048]{0:T(1024)(128)(2,1)} %param.20) | copy-start | bytes 12292
  69.6 44.2 %copy-start.3 = (bf16[2048,128]{1,0:T(8,128)(2,1)S(1)}, bf16[2048,128]{1,0:T(8,128)(2,1)}, u32[]{:S(2)}) copy-start(bf16[2048,128]{1,0:T(8,128)(2,1)} %param.21) | copy-start | bytes 1572868
  70.7 21.4 %all-to-all-start.2 = ((bf16[32,2,1024]{2,1,0:T(2,128)(2,1)}), bf16[32,2,1024]{2,1,0:T(2,128)(2,1)S(1)}, u32[]{:S(2)}, u32[]{:S(2)}) async-start(bf16[32,2,1024]{2,1,0:T(2,128)(2,1)} %reshape.563), calls=%async_computation.2 | async-start | bytes 262144 | tf_op jit(solution)/shard_map/all_to_all | solution.py:50
  94.3 19.4 %all-to-all-start.3 = ((bf16[32,2,1024]{2,1,0:T(2,128)(2,1)}), bf16[32,2,1024]{2,1,0:T(2,128)(2,1)S(1)}, u32[]{:S(2)}, u32[]{:S(2)}) async-start(bf16[32,2,1024]{2,1,0:T(2,128)(2,1)} %broadcast_in_dim.130), calls=%async_computation.3 | async-start | bytes 262144 | tf_op jit(solution)/shard_map/all_to_all | solution.py:29
  115.4 23.3 %copy-start.1 = (bf16[1,2048,192]{1,2,0:T(8,128)(2,1)S(1)}, bf16[1,2048,192]{1,2,0:T(8,128)(2,1)}, u32[]{:S(2)}) copy-start(bf16[1,2048,192]{1,2,0:T(8,128)(2,1)} %param.22) | copy-start | bytes 2359300
  138.7 1.1 copy-start.10
  159.6 24.4 %copy-start.6 = (bf16[2048]{0:T(1024)(128)(2,1)S(1)}, bf16[2048]{0:T(1024)(128)(2,1)}, u32[]{:S(2)}) copy-start(bf16[2048]{0:T(1024)(128)(2,1)} %param.25) | copy-start | bytes 12292
  161.0 21.6 %all-to-all-start.6 = ((bf16[32,2,1024]{2,1,0:T(2,128)(2,1)}), bf16[32,2,1024]{2,1,0:T(2,128)(2,1)S(1)}, u32[]{:S(2)}, u32[]{:S(2)}) async-start(bf16[32,2,1024]{2,1,0:T(2,128)(2,1)} %reshape.571), calls=%async_computation.6 | async-start | bytes 262144 | tf_op jit(solution)/shard_map/all_to_all | solution.py:50
  187.3 19.5 %all-to-all-start.7 = ((bf16[32,2,1024]{2,1,0:T(2,128)(2,1)}), bf16[32,2,1024]{2,1,0:T(2,128)(2,1)S(1)}, u32[]{:S(2)}, u32[]{:S(2)}) async-start(bf16[32,2,1024]{2,1,0:T(2,128)(2,1)} %broadcast_in_dim.134), calls=%async_computation.7 | async-start | bytes 262144 | tf_op jit(solution)/shard_map/all_to_all | solution.py:29
  208.5 16.9 %all-to-all-start.8 = ((f32[32,1,288]{2,1,0:T(1,128)}), f32[32,1,288]{2,1,0:T(1,128)S(1)}, u32[]{:S(2)}, u32[]{:S(2)}) async-start(f32[32,1,288]{2,1,0:T(1,128)} %reshape.588), calls=%async_computation.8 | async-start | bytes 98304 | tf_op jit(solution)/shard_map/all_to_all | solution.py:29

commit v11 on v10

--- a/solution.py
+++ b/solution.py
@@ -247,8 +247,17 @@
     slot_dots = jnp.sum(slot_grads * returned.astype(jnp.float32), axis=1)
     dots_part = jnp.sum(slot_map * slot_dots[None, None, :], axis=2)
     own_row = jnp.arange(rows, dtype=jnp.int32) == lax.axis_index(DP_SEQ)
-    payload = jnp.concatenate([dots_part, jnp.where(own_row, loss_term, 0.0)[:, None]], axis=1)
-    summed = taken_together(payload, DP_SEQ)
+    payload = jnp.concatenate(
+        [
+            dots_part,
+            jnp.where(own_row, loss_term, 0.0)[:, None],
+            jnp.zeros((rows, HEAD_WIDTH // 8 - topk - 1), jnp.float32),
+        ],
+        axis=1,
+    )
+    summed = jnp.sum(
+        from_everyone(payload.reshape(2, -1), DP_SEQ).reshape(lax.axis_size(DP_SEQ), rows, -1), axis=0
+    )
     route_dot = summed[:, :topk]
     pack_loss = jnp.sum(summed[:, topk])
     pick_grad = gate_weight * (route_dot - jnp.sum(gate_weight * route_dot, axis=1, keepdims=True))

time: 254 us -> 253 us (level)
  no operation moved by 1% of the time
where the time goes in v11:
time: 253 us; the launch traced here: 252 us
  blocking collectives  88.5 us (35%)
  waiting for transfers between devices  85.4 us (34%)
  starting transfers between devices  41.8 us (17%)
  other arithmetic  10.2 us (4%)
  between operations  9.92 us (4%)
  local copies, waits for them, and re-layouts  9.35 us (4%)
  matrix products  7 us (3%)
    all_to_all x3, blocking collectives, across_group(): lax.all_to_all(buffer, EXPERT, split_axis=0, concat_axis=0, tiled=True)  62.9 us
    all_to_all x4, waiting for transfers between devices, from_everyone(): return lax.all_to_all(copies, axis, split_axis=0, concat_axis=0, tiled=True)  55.5 us
    all_to_all x2, waiting for transfers between devices, rows_summed(): blocks = lax.all_to_all(array.reshape(count, 2, -1), axis, 0, 0, tiled=True)  29.9 us
    all_to_all x4, starting transfers between devices, from_everyone(): return lax.all_to_all(copies, axis, split_axis=0, concat_axis=0, tiled=True)  29.4 us
    all_to_all x1, blocking collectives, shards(): lax.all_to_all(packed, DP_SEQ, split_axis=0, concat_axis=0, tiled=True)  25.7 us
    all_to_all x2, starting transfers between devices, rows_summed(): blocks = lax.all_to_all(array.reshape(count, 2, -1), axis, 0, 0, tiled=True)  12.5 us
  transfers between devices with their start and end apart: 6, of which 6 were waited for; matrix products, arithmetic and copies ran while one was open for 1% of the time, Pallas kernels for 0%

profile of v11, /device:TPU:1, one launch (start us, length us, event | category | flops | bytes accessed | tf_op | source)
XLA Modules:
  0.0 252.2 jit_solution(6240147236532623726)
XLA Ops:
  0.7 0.8 convert_bitcast_fusion.2
  1.4 0.8 concatenate.15
  2.3 0.9 broadcast_in_dim.125
  3.2 16.9 %all-to-all-start = ((bf16[32,2,2176]{2,1,0:T(2,128)(2,1)}), bf16[32,2,2176]{2,1,0:T(2,128)(2,1)S(1)}, u32[]{:S(2)}, u32[]{:S(2)}) async-start(bf16[32,2,2176]{2,1,0:T(2,128)(2,1)} %broadcast_in_dim.125), calls=%async_computation | async-start | bytes 557056 | tf_op jit(solution)/shard_map/all_to_all | solution.py:29
  20.2 0.8 reduce-window.8
  21.1 0.9 reshape_squeeze.6
  22.3 17.4 %all-to-all-done = bf16[32,2,2176]{2,1,0:T(2,128)(2,1)S(1)} async-done(((bf16[32,2,2176]{2,1,0:T(2,128)(2,1)}), bf16[32,2,2176]{2,1,0:T(2,128)(2,1)S(1)}, u32[]{:S(2)}, u32[]{:S(2)}) %all-to-all-start) | async-done | bytes 278560 | tf_op jit(solution)/shard_map/all_to_all | solution.py:29
  42.4 25.7 %all_to_all.50 = bf16[32,2,2176]{2,1,0:T(2,128)(2,1)S(1)} all-to-all(bf16[32,2,2176]{2,1,0:T(2,128)(2,1)S(1)} %reshape.566), channel_id=1, replica_groups=mesh['dp'=8,'seq_0'=2,'seq_1'=2,'expert_0'=4,'expert_1'=4] {'dp','seq_0'..., dimensions={0} | all-to-all | bytes 557056 | tf_op jit(solution)/shard_map/all_to_all | solution.py:170
  69.9 0.8 reshape.568
  70.7 6.2 %all-to-all-start.2 = ((bf16[32,2,1024]{2,1,0:T(2,128)(2,1)}), bf16[32,2,1024]{2,1,0:T(2,128)(2,1)S(1)}, u32[]{:S(2)}, u32[]{:S(2)}) async-start(bf16[32,2,1024]{2,1,0:T(2,128)(2,1)} %reshape.568), calls=%async_computation.2 | async-start | bytes 262144 | tf_op jit(solution)/shard_map/all_to_all | solution.py:50
  76.9 15.2 %all-to-all-done.2 = bf16[32,2,1024]{2,1,0:T(2,128)(2,1)S(1)} async-done(((bf16[32,2,1024]{2,1,0:T(2,128)(2,1)}), bf16[32,2,1024]{2,1,0:T(2,128)(2,1)S(1)}, u32[]{:S(2)}, u32[]{:S(2)}) %all-to-all-start.2) | async-done | bytes 131104 | tf_op jit(solution)/shard_map/all_to_all | solution.py:50
  92.2 0.6 multiply_reduce_fusion.4
  93.6 0.7 broadcast_in_dim.133
  94.3 4.2 %all-to-all-start.3 = ((bf16[32,2,1024]{2,1,0:T(2,128)(2,1)}), bf16[32,2,1024]{2,1,0:T(2,128)(2,1)S(1)}, u32[]{:S(2)}, u32[]{:S(2)}) async-start(bf16[32,2,1024]{2,1,0:T(2,128)(2,1)} %broadcast_in_dim.133), calls=%async_computation.3 | async-start | bytes 262144 | tf_op jit(solution)/shard_map/all_to_all | solution.py:29
  98.7 15.1 %all-to-all-done.3 = bf16[32,2,1024]{2,1,0:T(2,128)(2,1)S(1)} async-done(((bf16[32,2,1024]{2,1,0:T(2,128)(2,1)}), bf16[32,2,1024]{2,1,0:T(2,128)(2,1)S(1)}, u32[]{:S(2)}, u32[]{:S(2)}) %all-to-all-start.3) | async-done | bytes 131104 | tf_op jit(solution)/shard_map/all_to_all | solution.py:29
  115.4 23.3 %all_to_all.51 = bf16[16,16,2048]{2,1,0:T(8,128)(2,1)S(1)} all-to-all(bf16[16,16,2048]{2,1,0:T(8,128)(2,1)S(1)} %bitcast.143), channel_id=1, replica_groups=mesh['dp'=8,'seq_0'=2,'seq_1'=2,'expert_0'=4,'expert_1'=4] {'expert_0','..., dimensions={0} | all-to-all | bytes 2097152 | tf_op jit(solution)/shard_map/all_to_all | solution.py:67
  140.8 18.8 %all_to_all.52 = bf16[16,16,2048]{2,1,0:T(8,128)(2,1)S(1)} all-to-all(bf16[16,16,2048]{2,1,0:T(8,128)(2,1)S(1)} %bitcast.145), channel_id=1, replica_groups=mesh['dp'=8,'seq_0'=2,'seq_1'=2,'expert_0'=4,'expert_1'=4] {'expert_0','..., dimensions={0} | all-to-all | bytes 2097152 | tf_op jit(solution)/shard_map/all_to_all | solution.py:67
  160.2 0.7 reshape.576
  161.0 6.3 %all-to-all-start.6 = ((bf16[32,2,1024]{2,1,0:T(2,128)(2,1)}), bf16[32,2,1024]{2,1,0:T(2,128)(2,1)S(1)}, u32[]{:S(2)}, u32[]{:S(2)}) async-start(bf16[32,2,1024]{2,1,0:T(2,128)(2,1)} %reshape.576), calls=%async_computation.6 | async-start | bytes 262144 | tf_op jit(solution)/shard_map/all_to_all | solution.py:50
  167.9 14.6 %all-to-all-done.6 = bf16[32,2,1024]{2,1,0:T(2,128)(2,1)S(1)} async-done(((bf16[32,2,1024]{2,1,0:T(2,128)(2,1)}), bf16[32,2,1024]{2,1,0:T(2,128)(2,1)S(1)}, u32[]{:S(2)}, u32[]{:S(2)}) %all-to-all-start.6) | async-done | bytes 131104 | tf_op jit(solution)/shard_map/all_to_all | solution.py:50
  182.7 0.6 multiply_reduce_fusion.3
  186.6 0.7 broadcast_in_dim.137
  187.3 4.2 %all-to-all-start.7 = ((bf16[32,2,1024]{2,1,0:T(2,128)(2,1)}), bf16[32,2,1024]{2,1,0:T(2,128)(2,1)S(1)}, u32[]{:S(2)}, u32[]{:S(2)}) async-start(bf16[32,2,1024]{2,1,0:T(2,128)(2,1)} %broadcast_in_dim.137), calls=%async_computation.7 | async-start | bytes 262144 | tf_op jit(solution)/shard_map/all_to_all | solution.py:29
  195.8 10.9 %all-to-all-done.7 = bf16[32,2,1024]{2,1,0:T(2,128)(2,1)S(1)} async-done(((bf16[32,2,1024]{2,1,0:T(2,128)(2,1)}), bf16[32,2,1024]{2,1,0:T(2,128)(2,1)S(1)}, u32[]{:S(2)}, u32[]{:S(2)}) %all-to-all-start.7) | async-done | bytes 131104 | tf_op jit(solution)/shard_map/all_to_all | solution.py:29
  207.7 0.7 broadcast_in_dim.141
  208.4 4.2 %all-to-all-start.8 = ((f32[32,2,256]{2,1,0:T(2,128)}), f32[32,2,256]{2,1,0:T(2,128)S(1)}, u32[]{:S(2)}, u32[]{:S(2)}) async-start(f32[32,2,256]{2,1,0:T(2,128)} %broadcast_in_dim.141), calls=%async_computation.8 | async-start | bytes 131072 | tf_op jit(solution)/shard_map/all_to_all | solution.py:29
  212.6 1.0 convolution_convert_fusion.1
  213.6 12.1 %all-to-all-done.8 = f32[32,2,256]{2,1,0:T(2,128)S(1)} async-done(((f32[32,2,256]{2,1,0:T(2,128)}), f32[32,2,256]{2,1,0:T(2,128)S(1)}, u32[]{:S(2)}, u32[]{:S(2)}) %all-to-all-start.8) | async-done | bytes 65568 | tf_op jit(solution)/shard_map/all_to_all | solution.py:29
  225.9 0.7 slice_reduce_fusion
  228.8 20.8 %all_to_all.53 = bf16[16,16,2176]{2,1,0:T(8,128)(2,1)S(1)} all-to-all(bf16[16,16,2176]{2,1,0:T(8,128)(2,1)S(1)} %pad_maximum_fusion), channel_id=1, replica_groups=mesh['dp'=8,'seq_0'=2,'seq_1'=2,'expert_0'=4,'expert_1'=4] {'expert_0','..., dimensions={0} | all-to-all | bytes 2228224 | tf_op jit(solution)/shard_map/all_to_all | solution.py:67
  249.6 0.7 add_reduce_fusion.1
  251.0 1.3 fusion
  (125 shorter events, 13.9 us)
Async XLA Ops:
  0.6 139.7 %copy-start = (bf16[1,192,2048]{2,1,0:T(8,128)(2,1)S(1)}, bf16[1,192,2048]{2,1,0:T(8,128)(2,1)}, u32[]{:S(2)}) copy-start(bf16[1,192,2048]{2,1,0:T(8,128)(2,1)} %param.24) | copy-start | bytes 2359300
  0.6 21.4 %copy-start.9 = (s32[1,8]{1,0:T(1,128)S(1)}, s32[1,8]{1,0:T(1,128)}, u32[]{:S(2)}) copy-start(s32[1,8]{1,0:T(1,128)} %param.29) | copy-start | bytes 100
  0.7 21.4 %copy-start.8 = (s32[1,32]{1,0:T(1,128)S(1)}, s32[1,32]{1,0:T(1,128)}, u32[]{:S(2)}) copy-start(s32[1,32]{1,0:T(1,128)} %param.27) | copy-start | bytes 388
  3.2 36.6 %copy-start.4 = (bf16[1,128,512]{2,1,0:T(8,128)(2,1)S(1)}, bf16[1,128,512]{2,1,0:T(8,128)(2,1)}, u32[]{:S(2)}) copy-start(bf16[1,128,512]{2,1,0:T(8,128)(2,1)} %param.15) | copy-start | bytes 393220
  3.2 36.5 %all-to-all-start = ((bf16[32,2,2176]{2,1,0:T(2,128)(2,1)}), bf16[32,2,2176]{2,1,0:T(2,128)(2,1)S(1)}, u32[]{:S(2)}, u32[]{:S(2)}) async-start(bf16[32,2,2176]{2,1,0:T(2,128)(2,1)} %broadcast_in_dim.125), calls=%async_computation | async-start | bytes 557056 | tf_op jit(solution)/shard_map/all_to_all | solution.py:29
  42.3 27.3 %copy-start.2 = (bf16[128,2048]{1,0:T(8,128)(2,1)S(1)}, bf16[128,2048]{1,0:T(8,128)(2,1)}, u32[]{:S(2)}) copy-start(bf16[128,2048]{1,0:T(8,128)(2,1)} %param.19) | copy-start | bytes 1572868
  68.1 8.7 %copy-start.5 = (bf16[1,1,2048]{2,1,0:T(2,128)(2,1)S(1)}, bf16[1,1,2048]{2,1,0:T(2,128)(2,1)}, u32[]{:S(2)}) copy-start(bf16[1,1,2048]{2,1,0:T(2,128)(2,1)} %param.18) | copy-start | bytes 12292
  68.3 25.3 %copy-start.7 = (bf16[2048]{0:T(1024)(128)(2,1)S(1)}, bf16[2048]{0:T(1024)(128)(2,1)}, u32[]{:S(2)}) copy-start(bf16[2048]{0:T(1024)(128)(2,1)} %param.20) | copy-start | bytes 12292
  69.6 44.2 %copy-start.3 = (bf16[2048,128]{1,0:T(8,128)(2,1)S(1)}, bf16[2048,128]{1,0:T(8,128)(2,1)}, u32[]{:S(2)}) copy-start(bf16[2048,128]{1,0:T(8,128)(2,1)} %param.21) | copy-start | bytes 1572868
  70.7 21.4 %all-to-all-start.2 = ((bf16[32,2,1024]{2,1,0:T(2,128)(2,1)}), bf16[32,2,1024]{2,1,0:T(2,128)(2,1)S(1)}, u32[]{:S(2)}, u32[]{:S(2)}) async-start(bf16[32,2,1024]{2,1,0:T(2,128)(2,1)} %reshape.568), calls=%async_computation.2 | async-start | bytes 262144 | tf_op jit(solution)/shard_map/all_to_all | solution.py:50
  94.3 19.4 %all-to-all-start.3 = ((bf16[32,2,1024]{2,1,0:T(2,128)(2,1)}), bf16[32,2,1024]{2,1,0:T(2,128)(2,1)S(1)}, u32[]{:S(2)}, u32[]{:S(2)}) async-start(bf16[32,2,1024]{2,1,0:T(2,128)(2,1)} %broadcast_in_dim.133), calls=%async_computation.3 | async-start | bytes 262144 | tf_op jit(solution)/shard_map/all_to_all | solution.py:29
  115.4 23.3 %copy-start.1 = (bf16[1,2048,192]{1,2,0:T(8,128)(2,1)S(1)}, bf16[1,2048,192]{1,2,0:T(8,128)(2,1)}, u32[]{:S(2)}) copy-start(bf16[1,2048,192]{1,2,0:T(8,128)(2,1)} %param.22) | copy-start | bytes 2359300
  138.7 1.1 copy-start.10
  159.6 24.4 %copy-start.6 = (bf16[2048]{0:T(1024)(128)(2,1)S(1)}, bf16[2048]{0:T(1024)(128)(2,1)}, u32[]{:S(2)}) copy-start(bf16[2048]{0:T(1024)(128)(2,1)} %param.25) | copy-start | bytes 12292
  161.0 21.6 %all-to-all-start.6 = ((bf16[32,2,1024]{2,1,0:T(2,128)(2,1)}), bf16[32,2,1024]{2,1,0:T(2,128)(2,1)S(1)}, u32[]{:S(2)}, u32[]{:S(2)}) async-start(bf16[32,2,1024]{2,1,0:T(2,128)(2,1)} %reshape.576), calls=%async_computation.6 | async-start | bytes 262144 | tf_op jit(solution)/shard_map/all_to_all | solution.py:50
  187.3 19.5 %all-to-all-start.7 = ((bf16[32,2,1024]{2,1,0:T(2,128)(2,1)}), bf16[32,2,1024]{2,1,0:T(2,128)(2,1)S(1)}, u32[]{:S(2)}, u32[]{:S(2)}) async-start(bf16[32,2,1024]{2,1,0:T(2,128)(2,1)} %broadcast_in_dim.137), calls=%async_computation.7 | async-start | bytes 262144 | tf_op jit(solution)/shard_map/all_to_all | solution.py:29
  208.4 17.4 %all-to-all-start.8 = ((f32[32,2,256]{2,1,0:T(2,128)}), f32[32,2,256]{2,1,0:T(2,128)S(1)}, u32[]{:S(2)}, u32[]{:S(2)}) async-start(f32[32,2,256]{2,1,0:T(2,128)} %broadcast_in_dim.141), calls=%async_computation.8 | async-start | bytes 131072 | tf_op jit(solution)/shard_map/all_to_all | solution.py:29

commit v12 on v11

--- a/solution.py
+++ b/solution.py
@@ -231,11 +231,14 @@
     )
     expert_mix = rows_summed(group_mix.astype(jnp.bfloat16), DP_SEQ)
     final = stream + expert_mix
-    reward, pull = jax.vjp(lambda value: head_logit(value, head_vec), final)
+    head = head_vec.astype(jnp.float32)[None, :]
+    rho = rms_scale(final)
+    final_head = jnp.sum(final * head, axis=-1, keepdims=True)
+    reward = (rho * final_head)[:, 0]
     target = labels[0].astype(jnp.float32)
     loss_term = jnp.sum(jax.nn.softplus(reward) - target * reward)
-    logit_grad = jax.nn.sigmoid(reward) - target
-    (final_grad,) = pull(logit_grad)
+    logit_grad = (jax.nn.sigmoid(reward) - target)[:, None]
+    final_grad = logit_grad * (rho * head - rho * rho * rho * final_head / final.shape[1] * final)
     d_mix = final_grad.astype(jnp.bfloat16)
     pack_grads = rows_gathered(d_mix, DP_SEQ)
     d_out = lax.dot_general(

time: 253 us -> 253 us (level)
  between operations: 9.92 us -> 6.1 us
  waiting for transfers between devices: 85.4 us -> 89.2 us
    all_to_all x4, waiting for transfers between devices: 55.5 us -> 59.4 us  [from_everyone(): return lax.all_to_all(copies, axis, split_axis=0, concat_axis=0, tiled=True)]
where the time goes in v12:
time: 253 us; the launch traced here: 252 us
  waiting for transfers between devices  89.2 us (35%)
  blocking collectives  88.6 us (35%)
  starting transfers between devices  41.8 us (17%)
  other arithmetic  9.63 us (4%)
  local copies, waits for them, and re-layouts  9.35 us (4%)
  matrix products  7 us (3%)
  between operations  6.1 us (2%)
    all_to_all x3, blocking collectives, across_group(): lax.all_to_all(buffer, EXPERT, split_axis=0, concat_axis=0, tiled=True)  62.9 us
    all_to_all x4, waiting for transfers between devices, from_everyone(): return lax.all_to_all(copies, axis, split_axis=0, concat_axis=0, tiled=True)  59.4 us
    all_to_all x2, waiting for transfers between devices, rows_summed(): blocks = lax.all_to_all(array.reshape(count, 2, -1), axis, 0, 0, tiled=True)  29.9 us
    all_to_all x4, starting transfers between devices, from_everyone(): return lax.all_to_all(copies, axis, split_axis=0, concat_axis=0, tiled=True)  29.4 us
    all_to_all x1, blocking collectives, shards(): lax.all_to_all(packed, DP_SEQ, split_axis=0, concat_axis=0, tiled=True)  25.7 us
    all_to_all x2, starting transfers between devices, rows_summed(): blocks = lax.all_to_all(array.reshape(count, 2, -1), axis, 0, 0, tiled=True)  12.4 us
  transfers between devices with their start and end apart: 6, of which 6 were waited for; matrix products, arithmetic and copies ran while one was open for 1% of the time, Pallas kernels for 0%

profile of v12, /device:TPU:1, one launch (start us, length us, event | category | flops | bytes accessed | tf_op | source)
XLA Modules:
  0.0 251.7 jit_solution(10878605474818746649)
XLA Ops:
  0.7 0.8 convert_bitcast_fusion.2
  1.4 0.8 concatenate.15
  2.3 0.9 broadcast_in_dim.120
  3.2 16.9 %all-to-all-start = ((bf16[32,2,2176]{2,1,0:T(2,128)(2,1)}), bf16[32,2,2176]{2,1,0:T(2,128)(2,1)S(1)}, u32[]{:S(2)}, u32[]{:S(2)}) async-start(bf16[32,2,2176]{2,1,0:T(2,128)(2,1)} %broadcast_in_dim.120), calls=%async_computation | async-start | bytes 557056 | tf_op jit(solution)/shard_map/all_to_all | solution.py:29
  20.2 0.8 reduce-window.8
  21.1 0.9 reshape_squeeze.6
  22.3 17.4 %all-to-all-done = bf16[32,2,2176]{2,1,0:T(2,128)(2,1)S(1)} async-done(((bf16[32,2,2176]{2,1,0:T(2,128)(2,1)}), bf16[32,2,2176]{2,1,0:T(2,128)(2,1)S(1)}, u32[]{:S(2)}, u32[]{:S(2)}) %all-to-all-start) | async-done | bytes 278560 | tf_op jit(solution)/shard_map/all_to_all | solution.py:29
  42.4 25.7 %all_to_all.50 = bf16[32,2,2176]{2,1,0:T(2,128)(2,1)S(1)} all-to-all(bf16[32,2,2176]{2,1,0:T(2,128)(2,1)S(1)} %reshape.561), channel_id=1, replica_groups=mesh['dp'=8,'seq_0'=2,'seq_1'=2,'expert_0'=4,'expert_1'=4] {'dp','seq_0'..., dimensions={0} | all-to-all | bytes 557056 | tf_op jit(solution)/shard_map/all_to_all | solution.py:170
  69.9 0.7 reshape.563
  70.7 6.2 %all-to-all-start.2 = ((bf16[32,2,1024]{2,1,0:T(2,128)(2,1)}), bf16[32,2,1024]{2,1,0:T(2,128)(2,1)S(1)}, u32[]{:S(2)}, u32[]{:S(2)}) async-start(bf16[32,2,1024]{2,1,0:T(2,128)(2,1)} %reshape.563), calls=%async_computation.2 | async-start | bytes 262144 | tf_op jit(solution)/shard_map/all_to_all | solution.py:50
  76.9 15.2 %all-to-all-done.2 = bf16[32,2,1024]{2,1,0:T(2,128)(2,1)S(1)} async-done(((bf16[32,2,1024]{2,1,0:T(2,128)(2,1)}), bf16[32,2,1024]{2,1,0:T(2,128)(2,1)S(1)}, u32[]{:S(2)}, u32[]{:S(2)}) %all-to-all-start.2) | async-done | bytes 131104 | tf_op jit(solution)/shard_map/all_to_all | solution.py:50
  93.6 0.7 broadcast_in_dim.128
  94.3 4.2 %all-to-all-start.3 = ((bf16[32,2,1024]{2,1,0:T(2,128)(2,1)}), bf16[32,2,1024]{2,1,0:T(2,128)(2,1)S(1)}, u32[]{:S(2)}, u32[]{:S(2)}) async-start(bf16[32,2,1024]{2,1,0:T(2,128)(2,1)} %broadcast_in_dim.128), calls=%async_computation.3 | async-start | bytes 262144 | tf_op jit(solution)/shard_map/all_to_all | solution.py:29
  98.7 15.1 %all-to-all-done.3 = bf16[32,2,1024]{2,1,0:T(2,128)(2,1)S(1)} async-done(((bf16[32,2,1024]{2,1,0:T(2,128)(2,1)}), bf16[32,2,1024]{2,1,0:T(2,128)(2,1)S(1)}, u32[]{:S(2)}, u32[]{:S(2)}) %all-to-all-start.3) | async-done | bytes 131104 | tf_op jit(solution)/shard_map/all_to_all | solution.py:29
  115.4 23.3 %all_to_all.51 = bf16[16,16,2048]{2,1,0:T(8,128)(2,1)S(1)} all-to-all(bf16[16,16,2048]{2,1,0:T(8,128)(2,1)S(1)} %bitcast.148), channel_id=1, replica_groups=mesh['dp'=8,'seq_0'=2,'seq_1'=2,'expert_0'=4,'expert_1'=4] {'expert_0','..., dimensions={0} | all-to-all | bytes 2097152 | tf_op jit(solution)/shard_map/all_to_all | solution.py:67
  139.2 0.6 copy-done.10
  140.8 18.8 %all_to_all.52 = bf16[16,16,2048]{2,1,0:T(8,128)(2,1)S(1)} all-to-all(bf16[16,16,2048]{2,1,0:T(8,128)(2,1)S(1)} %bitcast.150), channel_id=1, replica_groups=mesh['dp'=8,'seq_0'=2,'seq_1'=2,'expert_0'=4,'expert_1'=4] {'expert_0','..., dimensions={0} | all-to-all | bytes 2097152 | tf_op jit(solution)/shard_map/all_to_all | solution.py:67
  160.3 0.7 reshape.571
  161.0 6.3 %all-to-all-start.6 = ((bf16[32,2,1024]{2,1,0:T(2,128)(2,1)}), bf16[32,2,1024]{2,1,0:T(2,128)(2,1)S(1)}, u32[]{:S(2)}, u32[]{:S(2)}) async-start(bf16[32,2,1024]{2,1,0:T(2,128)(2,1)} %reshape.571), calls=%async_computation.6 | async-start | bytes 262144 | tf_op jit(solution)/shard_map/all_to_all | solution.py:50
  167.9 14.6 %all-to-all-done.6 = bf16[32,2,1024]{2,1,0:T(2,128)(2,1)S(1)} async-done(((bf16[32,2,1024]{2,1,0:T(2,128)(2,1)}), bf16[32,2,1024]{2,1,0:T(2,128)(2,1)S(1)}, u32[]{:S(2)}, u32[]{:S(2)}) %all-to-all-start.6) | async-done | bytes 131104 | tf_op jit(solution)/shard_map/all_to_all | solution.py:50
  182.7 0.6 multiply_reduce_fusion.3
  186.1 0.7 broadcast_in_dim.130
  186.8 4.2 %all-to-all-start.7 = ((bf16[32,2,1024]{2,1,0:T(2,128)(2,1)}), bf16[32,2,1024]{2,1,0:T(2,128)(2,1)S(1)}, u32[]{:S(2)}, u32[]{:S(2)}) async-start(bf16[32,2,1024]{2,1,0:T(2,128)(2,1)} %broadcast_in_dim.130), calls=%async_computation.7 | async-start | bytes 262144 | tf_op jit(solution)/shard_map/all_to_all | solution.py:29
  191.4 14.8 %all-to-all-done.7 = bf16[32,2,1024]{2,1,0:T(2,128)(2,1)S(1)} async-done(((bf16[32,2,1024]{2,1,0:T(2,128)(2,1)}), bf16[32,2,1024]{2,1,0:T(2,128)(2,1)S(1)}, u32[]{:S(2)}, u32[]{:S(2)}) %all-to-all-start.7) | async-done | bytes 131104 | tf_op jit(solution)/shard_map/all_to_all | solution.py:29
  207.2 0.7 broadcast_in_dim.134
  207.8 4.2 %all-to-all-start.8 = ((f32[32,2,256]{2,1,0:T(2,128)}), f32[32,2,256]{2,1,0:T(2,128)S(1)}, u32[]{:S(2)}, u32[]{:S(2)}) async-start(f32[32,2,256]{2,1,0:T(2,128)} %broadcast_in_dim.134), calls=%async_computation.8 | async-start | bytes 131072 | tf_op jit(solution)/shard_map/all_to_all | solution.py:29
  212.0 1.0 convolution_convert_fusion.1
  213.0 12.1 %all-to-all-done.8 = f32[32,2,256]{2,1,0:T(2,128)S(1)} async-done(((f32[32,2,256]{2,1,0:T(2,128)}), f32[32,2,256]{2,1,0:T(2,128)S(1)}, u32[]{:S(2)}, u32[]{:S(2)}) %all-to-all-start.8) | async-done | bytes 65568 | tf_op jit(solution)/shard_map/all_to_all | solution.py:29
  225.3 0.7 slice_reduce_fusion
  228.2 20.8 %all_to_all.53 = bf16[16,16,2176]{2,1,0:T(8,128)(2,1)S(1)} all-to-all(bf16[16,16,2176]{2,1,0:T(8,128)(2,1)S(1)} %pad_maximum_fusion), channel_id=1, replica_groups=mesh['dp'=8,'seq_0'=2,'seq_1'=2,'expert_0'=4,'expert_1'=4] {'expert_0','..., dimensions={0} | all-to-all | bytes 2228224 | tf_op jit(solution)/shard_map/all_to_all | solution.py:67
  249.1 0.7 add_reduce_fusion.1
  250.4 1.3 fusion
  (124 shorter events, 13.3 us)
Async XLA Ops:
  0.6 139.7 %copy-start = (bf16[1,192,2048]{2,1,0:T(8,128)(2,1)S(1)}, bf16[1,192,2048]{2,1,0:T(8,128)(2,1)}, u32[]{:S(2)}) copy-start(bf16[1,192,2048]{2,1,0:T(8,128)(2,1)} %param.24) | copy-start | bytes 2359300
  0.6 21.4 %copy-start.9 = (s32[1,8]{1,0:T(1,128)S(1)}, s32[1,8]{1,0:T(1,128)}, u32[]{:S(2)}) copy-start(s32[1,8]{1,0:T(1,128)} %param.29) | copy-start | bytes 100
  0.7 21.4 %copy-start.8 = (s32[1,32]{1,0:T(1,128)S(1)}, s32[1,32]{1,0:T(1,128)}, u32[]{:S(2)}) copy-start(s32[1,32]{1,0:T(1,128)} %param.27) | copy-start | bytes 388
  3.2 36.6 %copy-start.4 = (bf16[1,128,512]{2,1,0:T(8,128)(2,1)S(1)}, bf16[1,128,512]{2,1,0:T(8,128)(2,1)}, u32[]{:S(2)}) copy-start(bf16[1,128,512]{2,1,0:T(8,128)(2,1)} %param.15) | copy-start | bytes 393220
  3.2 36.5 %all-to-all-start = ((bf16[32,2,2176]{2,1,0:T(2,128)(2,1)}), bf16[32,2,2176]{2,1,0:T(2,128)(2,1)S(1)}, u32[]{:S(2)}, u32[]{:S(2)}) async-start(bf16[32,2,2176]{2,1,0:T(2,128)(2,1)} %broadcast_in_dim.120), calls=%async_computation | async-start | bytes 557056 | tf_op jit(solution)/shard_map/all_to_all | solution.py:29
  42.3 27.3 %copy-start.2 = (bf16[128,2048]{1,0:T(8,128)(2,1)S(1)}, bf16[128,2048]{1,0:T(8,128)(2,1)}, u32[]{:S(2)}) copy-start(bf16[128,2048]{1,0:T(8,128)(2,1)} %param.19) | copy-start | bytes 1572868
  68.1 8.7 %copy-start.5 = (bf16[1,1,2048]{2,1,0:T(2,128)(2,1)S(1)}, bf16[1,1,2048]{2,1,0:T(2,128)(2,1)}, u32[]{:S(2)}) copy-start(bf16[1,1,2048]{2,1,0:T(2,128)(2,1)} %param.18) | copy-start | bytes 12292
  68.3 25.3 %copy-start.7 = (bf16[2048]{0:T(1024)(128)(2,1)S(1)}, bf16[2048]{0:T(1024)(128)(2,1)}, u32[]{:S(2)}) copy-start(bf16[2048]{0:T(1024)(128)(2,1)} %param.20) | copy-start | bytes 12292
  69.6 44.2 %copy-start.3 = (bf16[2048,128]{1,0:T(8,128)(2,1)S(1)}, bf16[2048,128]{1,0:T(8,128)(2,1)}, u32[]{:S(2)}) copy-start(bf16[2048,128]{1,0:T(8,128)(2,1)} %param.21) | copy-start | bytes 1572868
  70.7 21.4 %all-to-all-start.2 = ((bf16[32,2,1024]{2,1,0:T(2,128)(2,1)}), bf16[32,2,1024]{2,1,0:T(2,128)(2,1)S(1)}, u32[]{:S(2)}, u32[]{:S(2)}) async-start(bf16[32,2,1024]{2,1,0:T(2,128)(2,1)} %reshape.563), calls=%async_computation.2 | async-start | bytes 262144 | tf_op jit(solution)/shard_map/all_to_all | solution.py:50
  94.3 19.5 %all-to-all-start.3 = ((bf16[32,2,1024]{2,1,0:T(2,128)(2,1)}), bf16[32,2,1024]{2,1,0:T(2,128)(2,1)S(1)}, u32[]{:S(2)}, u32[]{:S(2)}) async-start(bf16[32,2,1024]{2,1,0:T(2,128)(2,1)} %broadcast_in_dim.128), calls=%async_computation.3 | async-start | bytes 262144 | tf_op jit(solution)/shard_map/all_to_all | solution.py:29
  115.4 23.3 %copy-start.1 = (bf16[1,2048,192]{1,2,0:T(8,128)(2,1)S(1)}, bf16[1,2048,192]{1,2,0:T(8,128)(2,1)}, u32[]{:S(2)}) copy-start(bf16[1,2048,192]{1,2,0:T(8,128)(2,1)} %param.22) | copy-start | bytes 2359300
  138.7 1.1 copy-start.10
  159.6 24.4 %copy-start.6 = (bf16[2048]{0:T(1024)(128)(2,1)S(1)}, bf16[2048]{0:T(1024)(128)(2,1)}, u32[]{:S(2)}) copy-start(bf16[2048]{0:T(1024)(128)(2,1)} %param.25) | copy-start | bytes 12292
  161.0 21.6 %all-to-all-start.6 = ((bf16[32,2,1024]{2,1,0:T(2,128)(2,1)}), bf16[32,2,1024]{2,1,0:T(2,128)(2,1)S(1)}, u32[]{:S(2)}, u32[]{:S(2)}) async-start(bf16[32,2,1024]{2,1,0:T(2,128)(2,1)} %reshape.571), calls=%async_computation.6 | async-start | bytes 262144 | tf_op jit(solution)/shard_map/all_to_all | solution.py:50
  186.8 19.5 %all-to-all-start.7 = ((bf16[32,2,1024]{2,1,0:T(2,128)(2,1)}), bf16[32,2,1024]{2,1,0:T(2,128)(2,1)S(1)}, u32[]{:S(2)}, u32[]{:S(2)}) async-start(bf16[32,2,1024]{2,1,0:T(2,128)(2,1)} %broadcast_in_dim.130), calls=%async_computation.7 | async-start | bytes 262144 | tf_op jit(solution)/shard_map/all_to_all | solution.py:29
  207.8 17.4 %all-to-all-start.8 = ((f32[32,2,256]{2,1,0:T(2,128)}), f32[32,2,256]{2,1,0:T(2,128)S(1)}, u32[]{:S(2)}, u32[]{:S(2)}) async-start(f32[32,2,256]{2,1,0:T(2,128)} %broadcast_in_dim.134), calls=%async_computation.8 | async-start | bytes 131072 | tf_op jit(solution)/shard_map/all_to_all | solution.py:29

commit v13 on v12

--- a/solution.py
+++ b/solution.py
@@ -75,6 +75,13 @@
     high = value.astype(jnp.bfloat16)
     low = (value - high.astype(jnp.float32)).astype(jnp.bfloat16)
     return high, low
+
+
+def paired_dot(wide, narrow, dims):
+    high, low = split_pair(wide)
+    return lax.dot_general(high, narrow, dims, preferred_element_type=jnp.float32) + lax.dot_general(
+        low, narrow, dims, preferred_element_type=jnp.float32
+    )
 
 
 def join_pair(high, low):
@@ -223,12 +230,7 @@
     returned = across_group(
         partial_value.astype(jnp.bfloat16).reshape(group_size, per_source, width)
     ).reshape(slots, width)
-    group_mix = lax.dot_general(
-        weight_map,
-        returned.astype(jnp.float32),
-        (((1,), (0,)), ((), ())),
-        precision=lax.Precision.HIGHEST,
-    )
+    group_mix = paired_dot(weight_map, returned, (((1,), (0,)), ((), ())))
     expert_mix = rows_summed(group_mix.astype(jnp.bfloat16), DP_SEQ)
     final = stream + expert_mix
     head = head_vec.astype(jnp.float32)[None, :]
@@ -241,9 +243,7 @@
     final_grad = logit_grad * (rho * head - rho * rho * rho * final_head / final.shape[1] * final)
     d_mix = final_grad.astype(jnp.bfloat16)
     pack_grads = rows_gathered(d_mix, DP_SEQ)
-    d_out = lax.dot_general(
-        weight_map, pack_grads.astype(jnp.float32), contract_rows, precision=lax.Precision.HIGHEST
-    ).astype(jnp.bfloat16)
+    d_out = paired_dot(weight_map, pack_grads, contract_rows).astype(jnp.bfloat16)
     slot_grads = lax.dot_general(
         row_map.astype(jnp.bfloat16), pack_grads, contract_rows, preferred_element_type=jnp.float32
     )
@@ -267,9 +267,7 @@
     d_logits = jnp.sum(chosen * pick_grad[:, :, None], axis=1)
     columns = pack_normed.reshape(rows, lax.axis_size(DP_SEQ), -1)
     my_columns = lax.dynamic_index_in_dim(columns, lax.axis_index(DP_SEQ), 1, keepdims=False)
-    router_part = lax.dot_general(
-        my_columns.astype(jnp.float32), d_logits, contract_rows, precision=lax.Precision.HIGHEST
-    )
+    router_part = paired_dot(d_logits, my_columns, contract_rows).T
     router_part = router_part.reshape(group_size, -1)
     chunk = router_part.shape[1]
     router_hi, router_lo = split_pair(router_part)

time: 253 us -> 254 us (level)
  other arithmetic: 9.63 us -> 12.2 us
  transfers between devices with their start and end apart: 6 -> 6, of which waited for: 6 -> 6; matrix products, arithmetic and copies ran while one was open for 1% -> 2% of each run, Pallas kernels for 0% -> 0%
where the time goes in v13:
time: 254 us; the launch traced here: 253 us
  blocking collectives  88.5 us (35%)
  waiting for transfers between devices  87.5 us (34%)
  starting transfers between devices  41.7 us (16%)
  other arithmetic  12.2 us (5%)
  local copies, waits for them, and re-layouts  8.73 us (3%)
  matrix products  8.02 us (3%)
  between operations  6.06 us (2%)
    all_to_all x3, blocking collectives, across_group(): lax.all_to_all(buffer, EXPERT, split_axis=0, concat_axis=0, tiled=True)  62.9 us
    all_to_all x4, waiting for transfers between devices, from_everyone(): return lax.all_to_all(copies, axis, split_axis=0, concat_axis=0, tiled=True)  57.7 us
    all_to_all x2, waiting for transfers between devices, rows_summed(): blocks = lax.all_to_all(array.reshape(count, 2, -1), axis, 0, 0, tiled=True)  29.9 us
    all_to_all x4, starting transfers between devices, from_everyone(): return lax.all_to_all(copies, axis, split_axis=0, concat_axis=0, tiled=True)  29.3 us
    all_to_all x1, blocking collectives, shards(): lax.all_to_all(packed, DP_SEQ, split_axis=0, concat_axis=0, tiled=True)  25.7 us
    all_to_all x2, starting transfers between devices, rows_summed(): blocks = lax.all_to_all(array.reshape(count, 2, -1), axis, 0, 0, tiled=True)  12.4 us
  transfers between devices with their start and end apart: 6, of which 6 were waited for; matrix products, arithmetic and copies ran while one was open for 2% of the time, Pallas kernels for 0%

profile of v13, /device:TPU:1, one launch (start us, length us, event | category | flops | bytes accessed | tf_op | source)
XLA Modules:
  0.0 252.8 jit_solution(5675998160379760117)
XLA Ops:
  0.7 0.8 convert_bitcast_fusion.2
  1.5 0.8 concatenate.15
  2.4 0.9 broadcast_in_dim.120
  3.2 16.7 %all-to-all-start = ((bf16[32,2,2176]{2,1,0:T(2,128)(2,1)}), bf16[32,2,2176]{2,1,0:T(2,128)(2,1)S(1)}, u32[]{:S(2)}, u32[]{:S(2)}) async-start(bf16[32,2,2176]{2,1,0:T(2,128)(2,1)} %broadcast_in_dim.120), calls=%async_computation | async-start | bytes 557056 | tf_op jit(solution)/shard_map/all_to_all | solution.py:29
  20.1 0.8 reduce-window.8
  21.0 0.9 reshape_squeeze.6
  21.9 0.9 select_reduce_fusion.5
  22.8 0.7 compare_and_fusion
  23.5 16.1 %all-to-all-done = bf16[32,2,2176]{2,1,0:T(2,128)(2,1)S(1)} async-done(((bf16[32,2,2176]{2,1,0:T(2,128)(2,1)}), bf16[32,2,2176]{2,1,0:T(2,128)(2,1)S(1)}, u32[]{:S(2)}, u32[]{:S(2)}) %all-to-all-start) | async-done | bytes 278560 | tf_op jit(solution)/shard_map/all_to_all | solution.py:29
  42.4 25.7 %all_to_all.50 = bf16[32,2,2176]{2,1,0:T(2,128)(2,1)S(1)} all-to-all(bf16[32,2,2176]{2,1,0:T(2,128)(2,1)S(1)} %reshape.561), channel_id=1, replica_groups=mesh['dp'=8,'seq_0'=2,'seq_1'=2,'expert_0'=4,'expert_1'=4] {'dp','seq_0'..., dimensions={0} | all-to-all | bytes 557056 | tf_op jit(solution)/shard_map/all_to_all | solution.py:177
  69.8 0.7 reshape.563
  70.6 6.1 %all-to-all-start.2 = ((bf16[32,2,1024]{2,1,0:T(2,128)(2,1)}), bf16[32,2,1024]{2,1,0:T(2,128)(2,1)S(1)}, u32[]{:S(2)}, u32[]{:S(2)}) async-start(bf16[32,2,1024]{2,1,0:T(2,128)(2,1)} %reshape.563), calls=%async_computation.2 | async-start | bytes 262144 | tf_op jit(solution)/shard_map/all_to_all | solution.py:50
  76.8 15.2 %all-to-all-done.2 = bf16[32,2,1024]{2,1,0:T(2,128)(2,1)S(1)} async-done(((bf16[32,2,1024]{2,1,0:T(2,128)(2,1)}), bf16[32,2,1024]{2,1,0:T(2,128)(2,1)S(1)}, u32[]{:S(2)}, u32[]{:S(2)}) %all-to-all-start.2) | async-done | bytes 131104 | tf_op jit(solution)/shard_map/all_to_all | solution.py:50
  93.5 0.7 broadcast_in_dim.128
  94.2 4.2 %all-to-all-start.3 = ((bf16[32,2,1024]{2,1,0:T(2,128)(2,1)}), bf16[32,2,1024]{2,1,0:T(2,128)(2,1)S(1)}, u32[]{:S(2)}, u32[]{:S(2)}) async-start(bf16[32,2,1024]{2,1,0:T(2,128)(2,1)} %broadcast_in_dim.128), calls=%async_computation.3 | async-start | bytes 262144 | tf_op jit(solution)/shard_map/all_to_all | solution.py:29
  98.6 15.1 %all-to-all-done.3 = bf16[32,2,1024]{2,1,0:T(2,128)(2,1)S(1)} async-done(((bf16[32,2,1024]{2,1,0:T(2,128)(2,1)}), bf16[32,2,1024]{2,1,0:T(2,128)(2,1)S(1)}, u32[]{:S(2)}, u32[]{:S(2)}) %all-to-all-start.3) | async-done | bytes 131104 | tf_op jit(solution)/shard_map/all_to_all | solution.py:29
  115.3 23.3 %all_to_all.51 = bf16[16,16,2048]{2,1,0:T(8,128)(2,1)S(1)} all-to-all(bf16[16,16,2048]{2,1,0:T(8,128)(2,1)S(1)} %bitcast.150), channel_id=1, replica_groups=mesh['dp'=8,'seq_0'=2,'seq_1'=2,'expert_0'=4,'expert_1'=4] {'expert_0','..., dimensions={0} | all-to-all | bytes 2097152 | tf_op jit(solution)/shard_map/all_to_all | solution.py:67
  140.1 18.8 %all_to_all.52 = bf16[16,16,2048]{2,1,0:T(8,128)(2,1)S(1)} all-to-all(bf16[16,16,2048]{2,1,0:T(8,128)(2,1)S(1)} %bitcast.152), channel_id=1, replica_groups=mesh['dp'=8,'seq_0'=2,'seq_1'=2,'expert_0'=4,'expert_1'=4] {'expert_0','..., dimensions={0} | all-to-all | bytes 2097152 | tf_op jit(solution)/shard_map/all_to_all | solution.py:67
  159.5 0.7 reshape.571
  160.3 6.3 %all-to-all-start.6 = ((bf16[32,2,1024]{2,1,0:T(2,128)(2,1)}), bf16[32,2,1024]{2,1,0:T(2,128)(2,1)S(1)}, u32[]{:S(2)}, u32[]{:S(2)}) async-start(bf16[32,2,1024]{2,1,0:T(2,128)(2,1)} %reshape.571), calls=%async_computation.6 | async-start | bytes 262144 | tf_op jit(solution)/shard_map/all_to_all | solution.py:50
  167.2 14.6 %all-to-all-done.6 = bf16[32,2,1024]{2,1,0:T(2,128)(2,1)S(1)} async-done(((bf16[32,2,1024]{2,1,0:T(2,128)(2,1)}), bf16[32,2,1024]{2,1,0:T(2,128)(2,1)S(1)}, u32[]{:S(2)}, u32[]{:S(2)}) %all-to-all-start.6) | async-done | bytes 131104 | tf_op jit(solution)/shard_map/all_to_all | solution.py:50
  185.3 0.7 broadcast_in_dim.130
  186.1 4.2 %all-to-all-start.7 = ((bf16[32,2,1024]{2,1,0:T(2,128)(2,1)}), bf16[32,2,1024]{2,1,0:T(2,128)(2,1)S(1)}, u32[]{:S(2)}, u32[]{:S(2)}) async-start(bf16[32,2,1024]{2,1,0:T(2,128)(2,1)} %broadcast_in_dim.130), calls=%async_computation.7 | async-start | bytes 262144 | tf_op jit(solution)/shard_map/all_to_all | solution.py:29
  190.7 14.8 %all-to-all-done.7 = bf16[32,2,1024]{2,1,0:T(2,128)(2,1)S(1)} async-done(((bf16[32,2,1024]{2,1,0:T(2,128)(2,1)}), bf16[32,2,1024]{2,1,0:T(2,128)(2,1)S(1)}, u32[]{:S(2)}, u32[]{:S(2)}) %all-to-all-start.7) | async-done | bytes 131104 | tf_op jit(solution)/shard_map/all_to_all | solution.py:29
  207.6 4.2 %all-to-all-start.8 = ((f32[32,2,256]{2,1,0:T(2,128)}), f32[32,2,256]{2,1,0:T(2,128)S(1)}, u32[]{:S(2)}, u32[]{:S(2)}) async-start(f32[32,2,256]{2,1,0:T(2,128)} %broadcast_in_dim.134), calls=%async_computation.8 | async-start | bytes 131072 | tf_op jit(solution)/shard_map/all_to_all | solution.py:29
  211.8 1.4 fusion
  213.2 11.7 %all-to-all-done.8 = f32[32,2,256]{2,1,0:T(2,128)S(1)} async-done(((f32[32,2,256]{2,1,0:T(2,128)}), f32[32,2,256]{2,1,0:T(2,128)S(1)}, u32[]{:S(2)}, u32[]{:S(2)}) %all-to-all-start.8) | async-done | bytes 65568 | tf_op jit(solution)/shard_map/all_to_all | solution.py:29
  225.1 0.7 slice_reduce_fusion
  228.0 1.3 pad_maximum_fusion
  229.3 20.8 %all_to_all.53 = bf16[16,16,2176]{2,1,0:T(8,128)(2,1)S(1)} all-to-all(bf16[16,16,2176]{2,1,0:T(8,128)(2,1)S(1)} %pad_maximum_fusion), channel_id=1, replica_groups=mesh['dp'=8,'seq_0'=2,'seq_1'=2,'expert_0'=4,'expert_1'=4] {'expert_0','..., dimensions={0} | all-to-all | bytes 2228224 | tf_op jit(solution)/shard_map/all_to_all | solution.py:67
  250.2 0.7 add_reduce_fusion.1
  251.5 1.3 fusion.1
  (123 shorter events, 14.8 us)
Async XLA Ops:
  0.6 139.0 %copy-start = (bf16[1,192,2048]{2,1,0:T(8,128)(2,1)S(1)}, bf16[1,192,2048]{2,1,0:T(8,128)(2,1)}, u32[]{:S(2)}) copy-start(bf16[1,192,2048]{2,1,0:T(8,128)(2,1)} %param.24) | copy-start | bytes 2359300
  0.6 39.1 %copy-start.4 = (bf16[1,128,512]{2,1,0:T(8,128)(2,1)S(1)}, bf16[1,128,512]{2,1,0:T(8,128)(2,1)}, u32[]{:S(2)}) copy-start(bf16[1,128,512]{2,1,0:T(8,128)(2,1)} %param.15) | copy-start | bytes 393220
  3.2 36.3 %all-to-all-start = ((bf16[32,2,2176]{2,1,0:T(2,128)(2,1)}), bf16[32,2,2176]{2,1,0:T(2,128)(2,1)S(1)}, u32[]{:S(2)}, u32[]{:S(2)}) async-start(bf16[32,2,2176]{2,1,0:T(2,128)(2,1)} %broadcast_in_dim.120), calls=%async_computation | async-start | bytes 557056 | tf_op jit(solution)/shard_map/all_to_all | solution.py:29
  41.7 27.9 %copy-start.2 = (bf16[128,2048]{1,0:T(8,128)(2,1)S(1)}, bf16[128,2048]{1,0:T(8,128)(2,1)}, u32[]{:S(2)}) copy-start(bf16[128,2048]{1,0:T(8,128)(2,1)} %param.19) | copy-start | bytes 1572868
  42.1 34.6 %copy-start.5 = (bf16[1,1,2048]{2,1,0:T(2,128)(2,1)S(1)}, bf16[1,1,2048]{2,1,0:T(2,128)(2,1)}, u32[]{:S(2)}) copy-start(bf16[1,1,2048]{2,1,0:T(2,128)(2,1)} %param.18) | copy-start | bytes 12292
  42.1 51.4 %copy-start.7 = (bf16[2048]{0:T(1024)(128)(2,1)S(1)}, bf16[2048]{0:T(1024)(128)(2,1)}, u32[]{:S(2)}) copy-start(bf16[2048]{0:T(1024)(128)(2,1)} %param.20) | copy-start | bytes 12292
  42.4 71.3 %copy-start.3 = (bf16[2048,128]{1,0:T(8,128)(2,1)S(1)}, bf16[2048,128]{1,0:T(8,128)(2,1)}, u32[]{:S(2)}) copy-start(bf16[2048,128]{1,0:T(8,128)(2,1)} %param.21) | copy-start | bytes 1572868
  70.6 21.4 %all-to-all-start.2 = ((bf16[32,2,1024]{2,1,0:T(2,128)(2,1)}), bf16[32,2,1024]{2,1,0:T(2,128)(2,1)S(1)}, u32[]{:S(2)}, u32[]{:S(2)}) async-start(bf16[32,2,1024]{2,1,0:T(2,128)(2,1)} %reshape.563), calls=%async_computation.2 | async-start | bytes 262144 | tf_op jit(solution)/shard_map/all_to_all | solution.py:50
  94.2 19.5 %all-to-all-start.3 = ((bf16[32,2,1024]{2,1,0:T(2,128)(2,1)}), bf16[32,2,1024]{2,1,0:T(2,128)(2,1)S(1)}, u32[]{:S(2)}, u32[]{:S(2)}) async-start(bf16[32,2,1024]{2,1,0:T(2,128)(2,1)} %broadcast_in_dim.128), calls=%async_computation.3 | async-start | bytes 262144 | tf_op jit(solution)/shard_map/all_to_all | solution.py:29
  113.7 24.9 %copy-start.1 = (bf16[1,2048,192]{1,2,0:T(8,128)(2,1)S(1)}, bf16[1,2048,192]{1,2,0:T(8,128)(2,1)}, u32[]{:S(2)}) copy-start(bf16[1,2048,192]{1,2,0:T(8,128)(2,1)} %param.22) | copy-start | bytes 2359300
  115.3 23.8 %copy-start.8 = (bf16[1,2048,192]{1,2,0:T(8,128)(2,1)S(1)}, bf16[1,2048,192]{1,2,0:T(8,128)(2,1)}, u32[]{:S(2)}) copy-start(bf16[1,2048,192]{1,2,0:T(8,128)(2,1)} %param.23) | copy-start | bytes 2359300
  158.9 24.4 %copy-start.6 = (bf16[2048]{0:T(1024)(128)(2,1)S(1)}, bf16[2048]{0:T(1024)(128)(2,1)}, u32[]{:S(2)}) copy-start(bf16[2048]{0:T(1024)(128)(2,1)} %param.25) | copy-start | bytes 12292
  160.3 21.6 %all-to-all-start.6 = ((bf16[32,2,1024]{2,1,0:T(2,128)(2,1)}), bf16[32,2,1024]{2,1,0:T(2,128)(2,1)S(1)}, u32[]{:S(2)}, u32[]{:S(2)}) async-start(bf16[32,2,1024]{2,1,0:T(2,128)(2,1)} %reshape.571), calls=%async_computation.6 | async-start | bytes 262144 | tf_op jit(solution)/shard_map/all_to_all | solution.py:50
  186.1 19.5 %all-to-all-start.7 = ((bf16[32,2,1024]{2,1,0:T(2,128)(2,1)}), bf16[32,2,1024]{2,1,0:T(2,128)(2,1)S(1)}, u32[]{:S(2)}, u32[]{:S(2)}) async-start(bf16[32,2,1024]{2,1,0:T(2,128)(2,1)} %broadcast_in_dim.130), calls=%async_computation.7 | async-start | bytes 262144 | tf_op jit(solution)/shard_map/all_to_all | solution.py:29
  207.6 17.4 %all-to-all-start.8 = ((f32[32,2,256]{2,1,0:T(2,128)}), f32[32,2,256]{2,1,0:T(2,128)S(1)}, u32[]{:S(2)}, u32[]{:S(2)}) async-start(f32[32,2,256]{2,1,0:T(2,128)} %broadcast_in_dim.134), calls=%async_computation.8 | async-start | bytes 131072 | tf_op jit(solution)/shard_map/all_to_all | solution.py:29
